TPU v7x, 256 devices: a whole 4x4x8 slice. The times are simulated.
256 devices in a mesh: chan: 32 (over y_hi, z, core), win: 8 (over x, y_lo).
Axes of the slice: x: 4, y: 4 (y_hi: 2, y_lo: 2; y = y_hi * 2 + y_lo), z: 8, core: 2. Of those that a mesh axis runs over, the one named last changes fastest.
Arguments:
- traces: bfloat16 [8, 1024, 8192], P('win', 'chan'), may hold values from -6 to 6
- owner: int32 [3], replicated, may hold values from 0 to 31
- window_mask: int32 [8, 32], P('win', 'chan'), may hold values 0 or 1
Outputs:
- stacks: float32 [3, 32, 64, 1024], P(None, None, 'win', 'chan')
Inputs may be any that keep to these rules, and one draw needn't show every extreme that they name: `owner`: each step names one channel block.
All inputs are finite; a program needn't handle non-finite values. No bound on the sum of `window_mask` on one device may be relied on, other than what follows from the above.
Results may differ from a plain program's by a relative error of at most 0.0028.
Values may be sent and summed in bfloat16 or wider, within the bound.
No kernel may reach another device: no remote copies, remote signals or barrier semaphores. Data moves between devices by JAX's collectives and lax.ppermute only.
A program may use at most 128 MiB of HBM per device.

v0:
```python
import math

import jax
import jax.numpy as jnp
from jax import lax
from jax.experimental import pallas as pl
from jax.experimental.pallas import tpu as pltpu
from jax.sharding import PartitionSpec as P

LAGS = 64
EDGE = 64
TIME_BLOCK = 1024
CHAN_BITS = (0, 1, 4, 2, 3)
WIN_BITS = (0, 1, 2)


def xor_pairs(size, bit):
    return [(i, i ^ (1 << bit)) for i in range(size)]


def broadcast(masked, me, axis, size):
    rows, samples = masked.shape
    pieces = masked.reshape(rows, size, samples // size)
    for bit in CHAN_BITS:
        half = pieces.shape[1] // 2
        low, high = pieces[:, :half], pieces[:, half:]
        mine = ((me >> bit) & 1) == 0
        send = jnp.where(mine, high, low)
        keep = jnp.where(mine, low, high)
        pieces = keep + lax.ppermute(send, axis, xor_pairs(size, bit))
    for bit in reversed(CHAN_BITS):
        mine = ((me >> bit) & 1) == 0
        got = lax.ppermute(pieces, axis, xor_pairs(size, bit))
        pieces = jnp.where(
            mine, jnp.concatenate([pieces, got], 1), jnp.concatenate([got, pieces], 1)
        )
    return pieces.reshape(rows, samples)


def scatter_lags(complete, me, axis, size):
    lags = complete.shape[0]
    bits = size.bit_length() - 1
    parts = complete.reshape(*([2] * bits), lags // size, *complete.shape[1:])
    remaining = list(reversed(range(bits)))
    for bit in WIN_BITS:
        where = remaining.index(bit)
        remaining.remove(bit)
        mine = ((me >> bit) & 1) == 0
        low = lax.index_in_dim(parts, 0, where, keepdims=False)
        high = lax.index_in_dim(parts, 1, where, keepdims=False)
        send = jnp.where(mine, high, low)
        keep = jnp.where(mine, low, high)
        parts = keep + lax.ppermute(send, axis, xor_pairs(size, bit))
    return parts


def correlate(sources, padded, chan_dev):
    rows, samples = sources.shape
    width = TIME_BLOCK + 128

    def kernel(src_ref, w_ref, out_ref):
        def block(k, acc):
            base = pl.multiple_of(k * TIME_BLOCK, TIME_BLOCK)
            window = w_ref[:, pl.ds(base, width)]
            parts = [
                pltpu.roll(window, width - (EDGE - LAGS // 2 + lag), 1)[:, :TIME_BLOCK]
                for lag in range(LAGS)
            ]
            stacked = jnp.concatenate(parts, 0)
            chunk = src_ref[:, pl.ds(base, TIME_BLOCK)]
            return acc + lax.dot_general(
                stacked, chunk, (((1,), (1,)), ((), ())), preferred_element_type=jnp.float32
            )

        out_ref[...] = lax.fori_loop(
            0, samples // TIME_BLOCK, block, jnp.zeros((LAGS * chan_dev, rows), jnp.float32)
        )

    return pl.pallas_call(
        kernel,
        out_shape=jax.ShapeDtypeStruct((LAGS * chan_dev, rows), jnp.float32),
        in_specs=[
            pl.BlockSpec(memory_space=pltpu.VMEM),
            pl.BlockSpec(memory_space=pltpu.VMEM),
        ],
        out_specs=pl.BlockSpec(memory_space=pltpu.VMEM),
    )(sources, padded)


def body(traces, owner, window_mask):
    chan_dev = traces.shape[1]
    samples = traces.shape[2]
    step_count = owner.shape[0]
    chan_size = lax.axis_size("chan")
    win_size = lax.axis_size("win")
    chan_me = lax.axis_index("chan")
    win_me = lax.axis_index("win")
    signal = traces[0].astype(jnp.float32)
    whitened = (
        signal * lax.rsqrt(jnp.mean(signal * signal, axis=-1, keepdims=True) + 1e-06)
    ).astype(jnp.bfloat16)
    own_flag = window_mask[0, 0].astype(jnp.float32)
    outgoing = whitened * own_flag.astype(jnp.bfloat16)
    masked = jnp.concatenate(
        [jnp.where(chan_me == owner[step], outgoing, jnp.zeros_like(outgoing)) for step in range(step_count)],
        0,
    )
    sources = broadcast(masked, chan_me, "chan", chan_size)
    padded = jnp.pad(whitened, ((0, 0), (EDGE, EDGE)))
    factor = own_flag / math.sqrt(samples)
    complete = correlate(sources, padded, chan_dev) * factor
    complete = complete.reshape(LAGS, chan_dev, step_count * chan_dev)
    reduced = scatter_lags(complete, win_me, "win", win_size)
    per_dev = LAGS // win_size
    reduced = reduced.reshape(per_dev, chan_dev, step_count, chan_dev)
    return jnp.transpose(reduced, (2, 3, 0, 1))


def solution(mesh):
    return jax.shard_map(
        body,
        mesh=mesh,
        in_specs=(P("win", "chan", None), P(), P("win", "chan")),
        out_specs=P(None, None, "win", "chan"),
        check_vma=False,
    )
```

profile of v0, /device:TPU:8, one launch (start us, length us, event | category | flops | bytes accessed | tf_op | source)
XLA Modules:
  0.0 129.3 jit_solution(18297087746657090820)
XLA Ops:
  0.0 1.4 %fusion.11 = (s32[1]{0:T(128)}, s32[1]{0:T(128)}, s32[1]{0:T(128)}) fusion(s32[3]{0:T(128)} %param.4), kind=kLoop, calls=%fused_computation.40 | loop fusion | bytes 24 | tf_op jit(solution)/shard_map/slice | solution.py:105
  7.1 2.3 %collective-permute-done = bf16[96,16,256]{2,1,0:T(8,128)(2,1)S(1)} collective-permute-done((bf16[96,16,256]{2,1,0:T(8,128)(2,1)S(1)}, bf16[96,16,256]{2,1,0:T(8,128)(2,1)S(1)}, u32[]{:S(2)}, u32[]{:S(2)}) %collective-permute-start) | collective-permute-done | bytes 786464 | tf_op jit(solution)/shard_map/ppermute | solution.py:30
  9.5 2.0 %collective-permute-start.1 = (bf16[96,8,256]{2,1,0:T(8,128)(2,1)S(1)}, bf16[96,8,256]{2,1,0:T(8,128)(2,1)S(1)}, u32[]{:S(2)}, u32[]{:S(2)}) collective-permute-start(bf16[96,8,256]{2,1,0:T(8,128)(2,1)S(1)} %broadcast_select_fusion.4), channel_id=1, source_target_pairs={{0,16},{8,24},{16,0},{24,8},{32,48},{40,56},{48,32},{56,40},{64,80... | collective-permute-start | bytes 1179656 | tf_op jit(solution)/shard_map/ppermute | solution.py:30
  11.5 9.4 %collective-permute-done.1 = bf16[96,8,256]{2,1,0:T(8,128)(2,1)S(1)} collective-permute-done((bf16[96,8,256]{2,1,0:T(8,128)(2,1)S(1)}, bf16[96,8,256]{2,1,0:T(8,128)(2,1)S(1)}, u32[]{:S(2)}, u32[]{:S(2)}) %collective-permute-start.1) | collective-permute-done | bytes 393248 | tf_op jit(solution)/shard_map/ppermute | solution.py:30
  21.1 2.4 %collective-permute-start.2 = (bf16[96,4,256]{2,1,0:T(4,128)(2,1)S(1)}, bf16[96,4,256]{2,1,0:T(4,128)(2,1)S(1)}, u32[]{:S(2)}, u32[]{:S(2)}) collective-permute-start(bf16[96,4,256]{2,1,0:T(4,128)(2,1)S(1)} %broadcast_select_fusion.5), channel_id=1, source_target_pairs={{0,128},{8,136},{16,144},{24,152},{32,160},{40,168},{48,176},{56,1... | collective-permute-start | bytes 589832 | tf_op jit(solution)/shard_map/ppermute | solution.py:30
  23.5 5.5 %collective-permute-done.2 = bf16[96,4,256]{2,1,0:T(4,128)(2,1)S(1)} collective-permute-done((bf16[96,4,256]{2,1,0:T(4,128)(2,1)S(1)}, bf16[96,4,256]{2,1,0:T(4,128)(2,1)S(1)}, u32[]{:S(2)}, u32[]{:S(2)}) %collective-permute-start.2) | collective-permute-done | bytes 196640 | tf_op jit(solution)/shard_map/ppermute | solution.py:30
  29.4 3.4 %collective-permute-start.3 = (bf16[96,2,256]{2,1,0:T(2,128)(2,1)S(1)}, bf16[96,2,256]{2,1,0:T(2,128)(2,1)S(1)}, u32[]{:S(2)}, u32[]{:S(2)}) collective-permute-start(bf16[96,2,256]{2,1,0:T(2,128)(2,1)S(1)} %broadcast_select_fusion.6), channel_id=1, source_target_pairs={{0,32},{8,40},{16,48},{24,56},{32,0},{40,8},{48,16},{56,24},{64,96... | collective-permute-start | bytes 294920 | tf_op jit(solution)/shard_map/ppermute | solution.py:30
  32.7 2.6 %collective-permute-done.3 = bf16[96,2,256]{2,1,0:T(2,128)(2,1)S(1)} collective-permute-done((bf16[96,2,256]{2,1,0:T(2,128)(2,1)S(1)}, bf16[96,2,256]{2,1,0:T(2,128)(2,1)S(1)}, u32[]{:S(2)}, u32[]{:S(2)}) %collective-permute-start.3) | collective-permute-done | bytes 98336 | tf_op jit(solution)/shard_map/ppermute | solution.py:30
  35.7 7.7 %collective-permute-start.4 = (bf16[96,1,256]{2,1,0:T(2,128)(2,1)S(1)}, bf16[96,1,256]{2,1,0:T(2,128)(2,1)S(1)}, u32[]{:S(2)}, u32[]{:S(2)}) collective-permute-start(bf16[96,1,256]{2,1,0:T(2,128)(2,1)S(1)} %broadcast_select_fusion.8), channel_id=1, source_target_pairs={{0,64},{8,72},{16,80},{24,88},{32,96},{40,104},{48,112},{56,120},{... | collective-permute-start | bytes 147464 | tf_op jit(solution)/shard_map/ppermute | solution.py:30
  43.4 3.4 %collective-permute-done.4 = bf16[96,1,256]{2,1,0:T(2,128)(2,1)S(1)} collective-permute-done((bf16[96,1,256]{2,1,0:T(2,128)(2,1)S(1)}, bf16[96,1,256]{2,1,0:T(2,128)(2,1)S(1)}, u32[]{:S(2)}, u32[]{:S(2)}) %collective-permute-start.4) | collective-permute-done | bytes 49184 | tf_op jit(solution)/shard_map/ppermute | solution.py:30
  47.0 5.2 %collective-permute-start.5 = (bf16[96,1,256]{2,1,0:T(2,128)(2,1)S(1)}, bf16[96,1,256]{2,1,0:T(2,128)(2,1)S(1)}, u32[]{:S(2)}, u32[]{:S(2)}) collective-permute-start(bf16[96,1,256]{2,1,0:T(2,128)(2,1)S(1)} %fusion.8), channel_id=1, source_target_pairs={{0,64},{8,72},{16,80},{24,88},{32,96},{40,104},{48,112},{56,120},{... | collective-permute-start | bytes 147464 | tf_op jit(solution)/shard_map/ppermute | solution.py:33
  52.3 3.4 %collective-permute-done.5 = bf16[96,1,256]{2,1,0:T(2,128)(2,1)S(1)} collective-permute-done((bf16[96,1,256]{2,1,0:T(2,128)(2,1)S(1)}, bf16[96,1,256]{2,1,0:T(2,128)(2,1)S(1)}, u32[]{:S(2)}, u32[]{:S(2)}) %collective-permute-start.5) | collective-permute-done | bytes 49184 | tf_op jit(solution)/shard_map/ppermute | solution.py:33
  56.7 5.5 %collective-permute-done.6 = bf16[96,2,256]{2,1,0:T(2,128)(2,1)S(1)} collective-permute-done((bf16[96,2,256]{2,1,0:T(2,128)(2,1)S(1)}, bf16[96,2,256]{2,1,0:T(2,128)(2,1)S(1)}, u32[]{:S(2)}, u32[]{:S(2)}) %collective-permute-start.6) | collective-permute-done | bytes 98336 | tf_op jit(solution)/shard_map/ppermute | solution.py:33
  62.6 2.4 %collective-permute-start.7 = (bf16[96,4,256]{2,1,0:T(4,128)(2,1)S(1)}, bf16[96,4,256]{2,1,0:T(4,128)(2,1)S(1)}, u32[]{:S(2)}, u32[]{:S(2)}) collective-permute-start(bf16[96,4,256]{2,1,0:T(4,128)(2,1)S(1)} %maximum_select_fusion.3), channel_id=1, source_target_pairs={{0,128},{8,136},{16,144},{24,152},{32,160},{40,168},{48,176},{56,1... | collective-permute-start | bytes 589832 | tf_op jit(solution)/shard_map/ppermute | solution.py:33
  64.9 4.9 %collective-permute-done.7 = bf16[96,4,256]{2,1,0:T(4,128)(2,1)S(1)} collective-permute-done((bf16[96,4,256]{2,1,0:T(4,128)(2,1)S(1)}, bf16[96,4,256]{2,1,0:T(4,128)(2,1)S(1)}, u32[]{:S(2)}, u32[]{:S(2)}) %collective-permute-start.7) | collective-permute-done | bytes 196640 | tf_op jit(solution)/shard_map/ppermute | solution.py:33
  70.3 7.8 %collective-permute-done.8 = bf16[96,8,256]{2,1,0:T(8,128)(2,1)S(1)} collective-permute-done((bf16[96,8,256]{2,1,0:T(8,128)(2,1)S(1)}, bf16[96,8,256]{2,1,0:T(8,128)(2,1)S(1)}, u32[]{:S(2)}, u32[]{:S(2)}) %collective-permute-start.8) | collective-permute-done | bytes 393248 | tf_op jit(solution)/shard_map/ppermute | solution.py:33
  81.4 2.2 %copy.16 = bf16[12,8,32,256]{3,1,2,0:T(8,128)(2,1)} copy(bf16[12,8,32,256]{3,2,1,0:T(8,128)(2,1)S(1)} %bitcast.71) | data formatting | bytes 3145728
  83.6 14.9 %shard_map.37 = f32[2048,96]{1,0:T(8,128)} custom-call(bf16[96,8192]{1,0:T(8,128)(2,1)} %bitcast.70, bf16[32,8320]{1,0:T(8,128)(2,1)} %pad.4.w_ref), custom_call_target="tpu_custom_call" | custom-call | tf_op jit(solution)/shard_map/pallas_call | solution.py:79
  98.5 1.3 %broadcast_multiply_fusion = f32[2048,96]{1,0:T(8,128)S(1)} fusion(f32[2048,96]{1,0:T(8,128)} %shard_map.37, f32[]{:T(128)} %bitcast.5), kind=kLoop, calls=%fused_computation.16 | loop fusion | flops 196608 | bytes 1572868 | tf_op jit(solution)/shard_map/mul | solution.py:111
  100.4 13.5 %collective-permute-done.10 = f32[2,2,8,32,96]{4,3,2,1,0:T(8,128)S(1)} collective-permute-done((f32[2,2,8,32,96]{4,3,2,1,0:T(8,128)S(1)}, f32[2,2,8,32,96]{4,3,2,1,0:T(8,128)S(1)}, u32[]{:S(2)}, u32[]{:S(2)}) %collective-permute-start.10) | collective-permute-done | bytes 393248 | tf_op jit(solution)/shard_map/ppermute | solution.py:53
  114.1 1.6 %collective-permute-start.11 = (f32[2,8,32,96]{3,2,1,0:T(8,128)S(1)}, f32[2,8,32,96]{3,2,1,0:T(8,128)S(1)}, u32[]{:S(2)}, u32[]{:S(2)}) collective-permute-start(f32[2,8,32,96]{3,2,1,0:T(8,128)S(1)} %select_bitcast_fusion.1), channel_id=1, source_target_pairs={{0,2},{1,3},{2,0},{3,1},{4,6},{5,7},{6,4},{7,5},{8,10},{9,11},{10,... | collective-permute-start | bytes 589832 | tf_op jit(solution)/shard_map/ppermute | solution.py:53
  115.7 6.0 %collective-permute-done.11 = f32[2,8,32,96]{3,2,1,0:T(8,128)S(1)} collective-permute-done((f32[2,8,32,96]{3,2,1,0:T(8,128)S(1)}, f32[2,8,32,96]{3,2,1,0:T(8,128)S(1)}, u32[]{:S(2)}, u32[]{:S(2)}) %collective-permute-start.11) | collective-permute-done | bytes 196640 | tf_op jit(solution)/shard_map/ppermute | solution.py:53
  121.8 3.1 %collective-permute-start.12 = (f32[8,32,96]{2,1,0:T(8,128)S(1)}, f32[8,32,96]{2,1,0:T(8,128)S(1)}, u32[]{:S(2)}, u32[]{:S(2)}) collective-permute-start(f32[8,32,96]{2,1,0:T(8,128)S(1)} %select_bitcast_fusion.2), channel_id=1, source_target_pairs={{0,4},{1,5},{2,6},{3,7},{4,0},{5,1},{6,2},{7,3},{8,12},{9,13},{10,... | collective-permute-start | bytes 294920 | tf_op jit(solution)/shard_map/ppermute | solution.py:53
  124.9 3.4 %collective-permute-done.12 = f32[8,32,96]{2,1,0:T(8,128)S(1)} collective-permute-done((f32[8,32,96]{2,1,0:T(8,128)S(1)}, f32[8,32,96]{2,1,0:T(8,128)S(1)}, u32[]{:S(2)}, u32[]{:S(2)}) %collective-permute-start.12) | collective-permute-done | bytes 98336 | tf_op jit(solution)/shard_map/ppermute | solution.py:53
  (38 shorter events, 11.3 us)
Async XLA Ops:
  6.9 2.4 %collective-permute-start = (bf16[96,16,256]{2,1,0:T(8,128)(2,1)S(1)}, bf16[96,16,256]{2,1,0:T(8,128)(2,1)S(1)}, u32[]{:S(2)}, u32[]{:S(2)}) collective-permute-start(bf16[96,16,256]{2,1,0:T(8,128)(2,1)S(1)} %broadcast_select_fusion), channel_id=1, source_target_pairs={{0,8},{8,0},{16,24},{24,16},{32,40},{40,32},{48,56},{56,48},{64,72... | collective-permute-start | bytes 2359304 | tf_op jit(solution)/shard_map/ppermute | solution.py:30
  9.5 11.4 %collective-permute-start.1 = (bf16[96,8,256]{2,1,0:T(8,128)(2,1)S(1)}, bf16[96,8,256]{2,1,0:T(8,128)(2,1)S(1)}, u32[]{:S(2)}, u32[]{:S(2)}) collective-permute-start(bf16[96,8,256]{2,1,0:T(8,128)(2,1)S(1)} %broadcast_select_fusion.4), channel_id=1, source_target_pairs={{0,16},{8,24},{16,0},{24,8},{32,48},{40,56},{48,32},{56,40},{64,80... | collective-permute-start | bytes 1179656 | tf_op jit(solution)/shard_map/ppermute | solution.py:30
  21.1 7.9 %collective-permute-start.2 = (bf16[96,4,256]{2,1,0:T(4,128)(2,1)S(1)}, bf16[96,4,256]{2,1,0:T(4,128)(2,1)S(1)}, u32[]{:S(2)}, u32[]{:S(2)}) collective-permute-start(bf16[96,4,256]{2,1,0:T(4,128)(2,1)S(1)} %broadcast_select_fusion.5), channel_id=1, source_target_pairs={{0,128},{8,136},{16,144},{24,152},{32,160},{40,168},{48,176},{56,1... | collective-permute-start | bytes 589832 | tf_op jit(solution)/shard_map/ppermute | solution.py:30
  29.4 6.0 %collective-permute-start.3 = (bf16[96,2,256]{2,1,0:T(2,128)(2,1)S(1)}, bf16[96,2,256]{2,1,0:T(2,128)(2,1)S(1)}, u32[]{:S(2)}, u32[]{:S(2)}) collective-permute-start(bf16[96,2,256]{2,1,0:T(2,128)(2,1)S(1)} %broadcast_select_fusion.6), channel_id=1, source_target_pairs={{0,32},{8,40},{16,48},{24,56},{32,0},{40,8},{48,16},{56,24},{64,96... | collective-permute-start | bytes 294920 | tf_op jit(solution)/shard_map/ppermute | solution.py:30
  35.7 11.1 %collective-permute-start.4 = (bf16[96,1,256]{2,1,0:T(2,128)(2,1)S(1)}, bf16[96,1,256]{2,1,0:T(2,128)(2,1)S(1)}, u32[]{:S(2)}, u32[]{:S(2)}) collective-permute-start(bf16[96,1,256]{2,1,0:T(2,128)(2,1)S(1)} %broadcast_select_fusion.8), channel_id=1, source_target_pairs={{0,64},{8,72},{16,80},{24,88},{32,96},{40,104},{48,112},{56,120},{... | collective-permute-start | bytes 147464 | tf_op jit(solution)/shard_map/ppermute | solution.py:30
  47.0 31.7 %copy-start = (bf16[1,32,8192]{2,1,0:T(8,128)(2,1)S(1)}, bf16[1,32,8192]{2,1,0:T(8,128)(2,1)}, u32[]{:S(2)}) copy-start(bf16[1,32,8192]{2,1,0:T(8,128)(2,1)} %param.3) | copy-start | bytes 1572868
  47.0 8.6 %collective-permute-start.5 = (bf16[96,1,256]{2,1,0:T(2,128)(2,1)S(1)}, bf16[96,1,256]{2,1,0:T(2,128)(2,1)S(1)}, u32[]{:S(2)}, u32[]{:S(2)}) collective-permute-start(bf16[96,1,256]{2,1,0:T(2,128)(2,1)S(1)} %fusion.8), channel_id=1, source_target_pairs={{0,64},{8,72},{16,80},{24,88},{32,96},{40,104},{48,112},{56,120},{... | collective-permute-start | bytes 147464 | tf_op jit(solution)/shard_map/ppermute | solution.py:33
  56.1 6.1 %collective-permute-start.6 = (bf16[96,2,256]{2,1,0:T(2,128)(2,1)S(1)}, bf16[96,2,256]{2,1,0:T(2,128)(2,1)S(1)}, u32[]{:S(2)}, u32[]{:S(2)}) collective-permute-start(bf16[96,2,256]{2,1,0:T(2,128)(2,1)S(1)} %broadcast_select_fusion.10), channel_id=1, source_target_pairs={{0,32},{8,40},{16,48},{24,56},{32,0},{40,8},{48,16},{56,24},{64,96... | collective-permute-start | bytes 294920 | tf_op jit(solution)/shard_map/ppermute | solution.py:33
  62.6 7.3 %collective-permute-start.7 = (bf16[96,4,256]{2,1,0:T(4,128)(2,1)S(1)}, bf16[96,4,256]{2,1,0:T(4,128)(2,1)S(1)}, u32[]{:S(2)}, u32[]{:S(2)}) collective-permute-start(bf16[96,4,256]{2,1,0:T(4,128)(2,1)S(1)} %maximum_select_fusion.3), channel_id=1, source_target_pairs={{0,128},{8,136},{16,144},{24,152},{32,160},{40,168},{48,176},{56,1... | collective-permute-start | bytes 589832 | tf_op jit(solution)/shard_map/ppermute | solution.py:33
  70.2 7.9 %collective-permute-start.8 = (bf16[96,8,256]{2,1,0:T(8,128)(2,1)S(1)}, bf16[96,8,256]{2,1,0:T(8,128)(2,1)S(1)}, u32[]{:S(2)}, u32[]{:S(2)}) collective-permute-start(bf16[96,8,256]{2,1,0:T(8,128)(2,1)S(1)} %maximum_select_fusion.2), channel_id=1, source_target_pairs={{0,16},{8,24},{16,0},{24,8},{32,48},{40,56},{48,32},{56,40},{64,80... | collective-permute-start | bytes 1179656 | tf_op jit(solution)/shard_map/ppermute | solution.py:33
  78.4 2.6 %collective-permute-start.9 = (bf16[96,16,256]{2,1,0:T(8,128)(2,1)S(1)}, bf16[96,16,256]{2,1,0:T(8,128)(2,1)S(1)}, u32[]{:S(2)}, u32[]{:S(2)}) collective-permute-start(bf16[96,16,256]{2,1,0:T(8,128)(2,1)S(1)} %maximum_select_fusion.1), channel_id=1, source_target_pairs={{0,8},{8,0},{16,24},{24,16},{32,40},{40,32},{48,56},{56,48},{64,72... | collective-permute-start | bytes 2359304 | tf_op jit(solution)/shard_map/ppermute | solution.py:33
  99.9 14.0 %collective-permute-start.10 = (f32[2,2,8,32,96]{4,3,2,1,0:T(8,128)S(1)}, f32[2,2,8,32,96]{4,3,2,1,0:T(8,128)S(1)}, u32[]{:S(2)}, u32[]{:S(2)}) collective-permute-start(f32[2,2,8,32,96]{4,3,2,1,0:T(8,128)S(1)} %select_bitcast_fusion), channel_id=1, source_target_pairs={{0,1},{1,0},{2,3},{3,2},{4,5},{5,4},{6,7},{7,6},{8,9},{9,8},{10,11... | collective-permute-start | bytes 1179656 | tf_op jit(solution)/shard_map/ppermute | solution.py:53
  114.1 7.6 %collective-permute-start.11 = (f32[2,8,32,96]{3,2,1,0:T(8,128)S(1)}, f32[2,8,32,96]{3,2,1,0:T(8,128)S(1)}, u32[]{:S(2)}, u32[]{:S(2)}) collective-permute-start(f32[2,8,32,96]{3,2,1,0:T(8,128)S(1)} %select_bitcast_fusion.1), channel_id=1, source_target_pairs={{0,2},{1,3},{2,0},{3,1},{4,6},{5,7},{6,4},{7,5},{8,10},{9,11},{10,... | collective-permute-start | bytes 589832 | tf_op jit(solution)/shard_map/ppermute | solution.py:53
  121.8 6.6 %collective-permute-start.12 = (f32[8,32,96]{2,1,0:T(8,128)S(1)}, f32[8,32,96]{2,1,0:T(8,128)S(1)}, u32[]{:S(2)}, u32[]{:S(2)}) collective-permute-start(f32[8,32,96]{2,1,0:T(8,128)S(1)} %select_bitcast_fusion.2), channel_id=1, source_target_pairs={{0,4},{1,5},{2,6},{3,7},{4,0},{5,1},{6,2},{7,3},{8,12},{9,13},{10,... | collective-permute-start | bytes 294920 | tf_op jit(solution)/shard_map/ppermute | solution.py:53
where the time goes:
time: 130 us; the launch traced here: 129 us
  waiting for transfers between devices  68.7 us (53%)
  starting transfers between devices  29.4 us (23%)
  Pallas kernels  14.9 us (11%)
  other arithmetic  6.84 us (5%)
  local copies, waits for them, and re-layouts  6.74 us (5%)
  between operations  2.79 us (2%)
    ppermute x5, waiting for transfers between devices, broadcast(): pieces = keep + lax.ppermute(send, axis, xor_pairs(size, bit))  23.2 us
    ppermute x3, waiting for transfers between devices, scatter_lags(): parts = keep + lax.ppermute(send, axis, xor_pairs(size, bit))  22.9 us
    ppermute x5, waiting for transfers between devices, broadcast(): got = lax.ppermute(pieces, axis, xor_pairs(size, bit))  22.6 us
    ppermute x5, starting transfers between devices, broadcast(): pieces = keep + lax.ppermute(send, axis, xor_pairs(size, bit))  15.5 us
    pallas_call x1, Pallas kernels, correlate(): pl.pallas_call(kernel, out_shape=jax.ShapeDtypeStruct((LAGS * chan_dev, r...  14.9 us
    ppermute x5, starting transfers between devices, broadcast(): got = lax.ppermute(pieces, axis, xor_pairs(size, bit))  8.59 us
    ppermute x3, starting transfers between devices, scatter_lags(): parts = keep + lax.ppermute(send, axis, xor_pairs(size, bit))  5.23 us
    unnamed x4, local copies, waits for them, and re-layouts  3.38 us
  transfers between devices with their start and end apart: 13, of which 13 were waited for; matrix products, arithmetic and copies ran while one was open for 1% of the time, Pallas kernels for 0%

commit v1 on v0

--- a/solution.py
+++ b/solution.py
@@ -10,25 +10,25 @@
 LAGS = 64
 EDGE = 64
 TIME_BLOCK = 1024
-CHAN_BITS = (0, 1, 4, 2, 3)
-WIN_BITS = (0, 1, 2)
+CHAN_BITS = ((0, 1, 4, 2, 3), (0, 4, 1, 2, 3))
+WIN_BITS = ((0, 1, 2), (1, 0, 2))
 
 
 def xor_pairs(size, bit):
     return [(i, i ^ (1 << bit)) for i in range(size)]
 
 
-def broadcast(masked, me, axis, size):
+def broadcast(masked, me, axis, size, order):
     rows, samples = masked.shape
     pieces = masked.reshape(rows, size, samples // size)
-    for bit in CHAN_BITS:
+    for bit in order:
         half = pieces.shape[1] // 2
         low, high = pieces[:, :half], pieces[:, half:]
         mine = ((me >> bit) & 1) == 0
         send = jnp.where(mine, high, low)
         keep = jnp.where(mine, low, high)
         pieces = keep + lax.ppermute(send, axis, xor_pairs(size, bit))
-    for bit in reversed(CHAN_BITS):
+    for bit in reversed(order):
         mine = ((me >> bit) & 1) == 0
         got = lax.ppermute(pieces, axis, xor_pairs(size, bit))
         pieces = jnp.where(
@@ -37,12 +37,12 @@
     return pieces.reshape(rows, samples)
 
 
-def scatter_lags(complete, me, axis, size):
+def scatter_lags(complete, me, axis, size, order):
     lags = complete.shape[0]
     bits = size.bit_length() - 1
     parts = complete.reshape(*([2] * bits), lags // size, *complete.shape[1:])
     remaining = list(reversed(range(bits)))
-    for bit in WIN_BITS:
+    for bit in order:
         where = remaining.index(bit)
         remaining.remove(bit)
         mine = ((me >> bit) & 1) == 0
@@ -105,12 +105,26 @@
         [jnp.where(chan_me == owner[step], outgoing, jnp.zeros_like(outgoing)) for step in range(step_count)],
         0,
     )
-    sources = broadcast(masked, chan_me, "chan", chan_size)
+    rows = masked.shape[0] // 2
+    sources = jnp.concatenate(
+        [
+            broadcast(masked[which * rows : (which + 1) * rows], chan_me, "chan", chan_size, order)
+            for which, order in enumerate(CHAN_BITS)
+        ],
+        0,
+    )
     padded = jnp.pad(whitened, ((0, 0), (EDGE, EDGE)))
     factor = own_flag / math.sqrt(samples)
     complete = correlate(sources, padded, chan_dev) * factor
     complete = complete.reshape(LAGS, chan_dev, step_count * chan_dev)
-    reduced = scatter_lags(complete, win_me, "win", win_size)
+    cols = complete.shape[-1] // 2
+    reduced = jnp.concatenate(
+        [
+            scatter_lags(complete[..., which * cols : (which + 1) * cols], win_me, "win", win_size, order)
+            for which, order in enumerate(WIN_BITS)
+        ],
+        -1,
+    )
     per_dev = LAGS // win_size
     reduced = reduced.reshape(per_dev, chan_dev, step_count, chan_dev)
     return jnp.transpose(reduced, (2, 3, 0, 1))

time: 130 us -> 126 us (0.969)
  waiting for transfers between devices: 68.7 us -> 39.4 us
  starting transfers between devices: 29.4 us -> 52.6 us
  other arithmetic: 6.84 us -> 10.5 us
  local copies, waits for them, and re-layouts: 6.74 us -> 5.31 us
    ppermute x5 -> x10, waiting for transfers between devices: 23.2 us -> 6.5 us  [broadcast(): pieces = keep + lax.ppermute(send, axis, xor_pairs(size, bit))]
    ppermute x5 -> x10, waiting for transfers between devices: 22.6 us -> 11.3 us  [broadcast(): got = lax.ppermute(pieces, axis, xor_pairs(size, bit))]
    ppermute x5 -> x10, starting transfers between devices: 8.59 us -> 19.8 us  [broadcast(): got = lax.ppermute(pieces, axis, xor_pairs(size, bit))]
    ppermute x5 -> x10, starting transfers between devices: 15.5 us -> 23 us  [broadcast(): pieces = keep + lax.ppermute(send, axis, xor_pairs(size, bit))]
    ppermute x3 -> x6, starting transfers between devices: 5.23 us -> 9.86 us  [scatter_lags(): parts = keep + lax.ppermute(send, axis, xor_pairs(size, bit))]
    unnamed x4, local copies, waits for them, and re-layouts: 3.38 us -> 1.26 us
    concatenate x0 -> x2, other arithmetic: none -> 1.4 us  [the longest x1 1.3 us: body(): jnp.concatenate([broadcast(masked[which * rows:(which + 1) * rows], chan_...]
    ppermute x3 -> x6, waiting for transfers between devices: 22.9 us -> 21.6 us  [scatter_lags(): parts = keep + lax.ppermute(send, axis, xor_pairs(size, bit))]
  transfers between devices with their start and end apart: 13 -> 26, of which waited for: 13 -> 16; matrix products, arithmetic and copies ran while one was open for 1% -> 4% of each run, Pallas kernels for 0% -> 0%
where the time goes in v1:
time: 126 us
  starting transfers between devices  52.6 us (42%)
  waiting for transfers between devices  39.4 us (31%)
  Pallas kernels  14.9 us (12%)
  other arithmetic  10.5 us (8%)
  local copies, waits for them, and re-layouts  5.31 us (4%)
  between operations  2.93 us (2%)
    ppermute x10, starting transfers between devices, broadcast(): pieces = keep + lax.ppermute(send, axis, xor_pairs(size, bit))  23 us
    ppermute x6, waiting for transfers between devices, scatter_lags(): parts = keep + lax.ppermute(send, axis, xor_pairs(size, bit))  21.6 us
    ppermute x10, starting transfers between devices, broadcast(): got = lax.ppermute(pieces, axis, xor_pairs(size, bit))  19.8 us
    pallas_call x1, Pallas kernels, correlate(): pl.pallas_call(kernel, out_shape=jax.ShapeDtypeStruct((LAGS * chan_dev, r...  14.9 us
    ppermute x10, waiting for transfers between devices, broadcast(): got = lax.ppermute(pieces, axis, xor_pairs(size, bit))  11.3 us
    ppermute x6, starting transfers between devices, scatter_lags(): parts = keep + lax.ppermute(send, axis, xor_pairs(size, bit))  9.86 us
    ppermute x10, waiting for transfers between devices, broadcast(): pieces = keep + lax.ppermute(send, axis, xor_pairs(size, bit))  6.5 us
  transfers between devices with their start and end apart: 26, of which 16 were waited for; matrix products, arithmetic and copies ran while one was open for 4% of the time, Pallas kernels for 0%

profile of v1, /device:TPU:8, one launch (start us, length us, event | category | flops | bytes accessed | tf_op | source)
XLA Modules:
  0.0 125.7 jit_solution(4055691549210851783)
XLA Ops:
  9.7 2.0 %collective-permute-start.1 = (bf16[48,8,256]{2,1,0:T(8,128)(2,1)S(1)}, bf16[48,8,256]{2,1,0:T(8,128)(2,1)S(1)}, u32[]{:S(2)}, u32[]{:S(2)}) collective-permute-start(bf16[48,8,256]{2,1,0:T(8,128)(2,1)S(1)} %broadcast_select_fusion.5), channel_id=1, source_target_pairs={{0,16},{8,24},{16,0},{24,8},{32,48},{40,56},{48,32},{56,40},{64,80... | collective-permute-start | bytes 589832 | tf_op jit(solution)/shard_map/ppermute | solution.py:30
  11.8 2.4 %collective-permute-start.11 = (bf16[48,8,256]{2,1,0:T(8,128)(2,1)S(1)}, bf16[48,8,256]{2,1,0:T(8,128)(2,1)S(1)}, u32[]{:S(2)}, u32[]{:S(2)}) collective-permute-start(bf16[48,8,256]{2,1,0:T(8,128)(2,1)S(1)} %broadcast_select_fusion.6), channel_id=1, source_target_pairs={{0,128},{8,136},{16,144},{24,152},{32,160},{40,168},{48,176},{56,1... | collective-permute-start | bytes 589832 | tf_op jit(solution)/shard_map/ppermute | solution.py:30
  14.2 2.7 %collective-permute-done.1 = bf16[48,8,256]{2,1,0:T(8,128)(2,1)S(1)} collective-permute-done((bf16[48,8,256]{2,1,0:T(8,128)(2,1)S(1)}, bf16[48,8,256]{2,1,0:T(8,128)(2,1)S(1)}, u32[]{:S(2)}, u32[]{:S(2)}) %collective-permute-start.1) | collective-permute-done | bytes 196640 | tf_op jit(solution)/shard_map/ppermute | solution.py:30
  17.0 2.4 %collective-permute-start.2 = (bf16[48,4,256]{2,1,0:T(4,128)(2,1)S(1)}, bf16[48,4,256]{2,1,0:T(4,128)(2,1)S(1)}, u32[]{:S(2)}, u32[]{:S(2)}) collective-permute-start(bf16[48,4,256]{2,1,0:T(4,128)(2,1)S(1)} %broadcast_select_fusion.8), channel_id=1, source_target_pairs={{0,128},{8,136},{16,144},{24,152},{32,160},{40,168},{48,176},{56,1... | collective-permute-start | bytes 294920 | tf_op jit(solution)/shard_map/ppermute | solution.py:30
  21.4 1.9 %collective-permute-done.2 = bf16[48,4,256]{2,1,0:T(4,128)(2,1)S(1)} collective-permute-done((bf16[48,4,256]{2,1,0:T(4,128)(2,1)S(1)}, bf16[48,4,256]{2,1,0:T(4,128)(2,1)S(1)}, u32[]{:S(2)}, u32[]{:S(2)}) %collective-permute-start.2) | collective-permute-done | bytes 98336 | tf_op jit(solution)/shard_map/ppermute | solution.py:30
  23.4 3.4 %collective-permute-start.3 = (bf16[48,2,256]{2,1,0:T(2,128)(2,1)S(1)}, bf16[48,2,256]{2,1,0:T(2,128)(2,1)S(1)}, u32[]{:S(2)}, u32[]{:S(2)}) collective-permute-start(bf16[48,2,256]{2,1,0:T(2,128)(2,1)S(1)} %broadcast_select_fusion.11), channel_id=1, source_target_pairs={{0,32},{8,40},{16,48},{24,56},{32,0},{40,8},{48,16},{56,24},{64,96... | collective-permute-start | bytes 147464 | tf_op jit(solution)/shard_map/ppermute | solution.py:30
  27.0 2.0 %collective-permute-start.13 = (bf16[48,2,256]{2,1,0:T(2,128)(2,1)S(1)}, bf16[48,2,256]{2,1,0:T(2,128)(2,1)S(1)}, u32[]{:S(2)}, u32[]{:S(2)}) collective-permute-start(bf16[48,2,256]{2,1,0:T(2,128)(2,1)S(1)} %broadcast_select_fusion.9), channel_id=1, source_target_pairs={{0,32},{8,40},{16,48},{24,56},{32,0},{40,8},{48,16},{56,24},{64,96... | collective-permute-start | bytes 147464 | tf_op jit(solution)/shard_map/ppermute | solution.py:30
  29.3 6.5 %collective-permute-start.4 = (bf16[48,1,256]{2,1,0:T(2,128)(2,1)S(1)}, bf16[48,1,256]{2,1,0:T(2,128)(2,1)S(1)}, u32[]{:S(2)}, u32[]{:S(2)}) collective-permute-start(bf16[48,1,256]{2,1,0:T(2,128)(2,1)S(1)} %broadcast_select_fusion.15), channel_id=1, source_target_pairs={{0,64},{8,72},{16,80},{24,88},{32,96},{40,104},{48,112},{56,120},{... | collective-permute-start | bytes 73736 | tf_op jit(solution)/shard_map/ppermute | solution.py:30
  36.1 2.6 %collective-permute-start.14 = (bf16[48,1,256]{2,1,0:T(2,128)(2,1)S(1)}, bf16[48,1,256]{2,1,0:T(2,128)(2,1)S(1)}, u32[]{:S(2)}, u32[]{:S(2)}) collective-permute-start(bf16[48,1,256]{2,1,0:T(2,128)(2,1)S(1)} %broadcast_select_fusion.13), channel_id=1, source_target_pairs={{0,64},{8,72},{16,80},{24,88},{32,96},{40,104},{48,112},{56,120},{... | collective-permute-start | bytes 73736 | tf_op jit(solution)/shard_map/ppermute | solution.py:30
  38.8 6.2 %collective-permute-start.5 = (bf16[48,1,256]{2,1,0:T(2,128)(2,1)S(1)}, bf16[48,1,256]{2,1,0:T(2,128)(2,1)S(1)}, u32[]{:S(2)}, u32[]{:S(2)}) collective-permute-start(bf16[48,1,256]{2,1,0:T(2,128)(2,1)S(1)} %fusion.4), channel_id=1, source_target_pairs={{0,64},{8,72},{16,80},{24,88},{32,96},{40,104},{48,112},{56,120},{... | collective-permute-start | bytes 73736 | tf_op jit(solution)/shard_map/ppermute | solution.py:33
  45.0 2.1 %collective-permute-start.15 = (bf16[48,1,256]{2,1,0:T(2,128)(2,1)S(1)}, bf16[48,1,256]{2,1,0:T(2,128)(2,1)S(1)}, u32[]{:S(2)}, u32[]{:S(2)}) collective-permute-start(bf16[48,1,256]{2,1,0:T(2,128)(2,1)S(1)} %fusion.5), channel_id=1, source_target_pairs={{0,64},{8,72},{16,80},{24,88},{32,96},{40,104},{48,112},{56,120},{... | collective-permute-start | bytes 73736 | tf_op jit(solution)/shard_map/ppermute | solution.py:33
  47.7 2.0 %collective-permute-start.6 = (bf16[48,2,256]{2,1,0:T(2,128)(2,1)S(1)}, bf16[48,2,256]{2,1,0:T(2,128)(2,1)S(1)}, u32[]{:S(2)}, u32[]{:S(2)}) collective-permute-start(bf16[48,2,256]{2,1,0:T(2,128)(2,1)S(1)} %broadcast_select_fusion.18), channel_id=1, source_target_pairs={{0,32},{8,40},{16,48},{24,56},{32,0},{40,8},{48,16},{56,24},{64,96... | collective-permute-start | bytes 147464 | tf_op jit(solution)/shard_map/ppermute | solution.py:33
  49.8 3.4 %collective-permute-done.15 = bf16[48,1,256]{2,1,0:T(2,128)(2,1)S(1)} collective-permute-done((bf16[48,1,256]{2,1,0:T(2,128)(2,1)S(1)}, bf16[48,1,256]{2,1,0:T(2,128)(2,1)S(1)}, u32[]{:S(2)}, u32[]{:S(2)}) %collective-permute-start.15) | collective-permute-done | bytes 24608 | tf_op jit(solution)/shard_map/ppermute | solution.py:33
  55.1 2.4 %collective-permute-start.7 = (bf16[48,4,256]{2,1,0:T(4,128)(2,1)S(1)}, bf16[48,4,256]{2,1,0:T(4,128)(2,1)S(1)}, u32[]{:S(2)}, u32[]{:S(2)}) collective-permute-start(bf16[48,4,256]{2,1,0:T(4,128)(2,1)S(1)} %maximum_select_fusion.6), channel_id=1, source_target_pairs={{0,128},{8,136},{16,144},{24,152},{32,160},{40,168},{48,176},{56,1... | collective-permute-start | bytes 294920 | tf_op jit(solution)/shard_map/ppermute | solution.py:33
  58.7 2.4 %collective-permute-start.17 = (bf16[48,4,256]{2,1,0:T(4,128)(2,1)S(1)}, bf16[48,4,256]{2,1,0:T(4,128)(2,1)S(1)}, u32[]{:S(2)}, u32[]{:S(2)}) collective-permute-start(bf16[48,4,256]{2,1,0:T(4,128)(2,1)S(1)} %maximum_select_fusion.7), channel_id=1, source_target_pairs={{0,16},{8,24},{16,0},{24,8},{32,48},{40,56},{48,32},{56,40},{64,80... | collective-permute-start | bytes 294920 | tf_op jit(solution)/shard_map/ppermute | solution.py:33
  63.9 2.4 %collective-permute-start.18 = (bf16[48,8,256]{2,1,0:T(8,128)(2,1)S(1)}, bf16[48,8,256]{2,1,0:T(8,128)(2,1)S(1)}, u32[]{:S(2)}, u32[]{:S(2)}) collective-permute-start(bf16[48,8,256]{2,1,0:T(8,128)(2,1)S(1)} %maximum_select_fusion.5), channel_id=1, source_target_pairs={{0,128},{8,136},{16,144},{24,152},{32,160},{40,168},{48,176},{56,1... | collective-permute-start | bytes 589832 | tf_op jit(solution)/shard_map/ppermute | solution.py:33
  68.1 3.1 %collective-permute-done.18 = bf16[48,8,256]{2,1,0:T(8,128)(2,1)S(1)} collective-permute-done((bf16[48,8,256]{2,1,0:T(8,128)(2,1)S(1)}, bf16[48,8,256]{2,1,0:T(8,128)(2,1)S(1)}, u32[]{:S(2)}, u32[]{:S(2)}) %collective-permute-start.18) | collective-permute-done | bytes 196640 | tf_op jit(solution)/shard_map/ppermute | solution.py:33
  75.3 14.9 %shard_map.37 = f32[2048,96]{1,0:T(8,128)} custom-call(bf16[96,8192]{1,0:T(8,128)(2,1)} %pad_maximum_fusion.src_ref, bf16[32,8320]{1,0:T(8,128)(2,1)} %pad.4.w_ref), custom_call_target="tpu_custom_call" | custom-call | tf_op jit(solution)/shard_map/pallas_call | solution.py:79
  93.4 1.7 %collective-permute-start.23 = (f32[2,2,8,32,48]{4,3,2,1,0:T(8,128)S(1)}, f32[2,2,8,32,48]{4,3,2,1,0:T(8,128)S(1)}, u32[]{:S(2)}, u32[]{:S(2)}) collective-permute-start(f32[2,2,8,32,48]{4,3,2,1,0:T(8,128)S(1)} %copy.21), channel_id=1, source_target_pairs={{0,2},{1,3},{2,0},{3,1},{4,6},{5,7},{6,4},{7,5},{8,10},{9,11},{10,... | collective-permute-start | bytes 589832 | tf_op jit(solution)/shard_map/ppermute | solution.py:53
  95.0 11.3 %collective-permute-done.20 = f32[2,2,8,32,48]{4,3,2,1,0:T(8,128)S(1)} collective-permute-done((f32[2,2,8,32,48]{4,3,2,1,0:T(8,128)S(1)}, f32[2,2,8,32,48]{4,3,2,1,0:T(8,128)S(1)}, u32[]{:S(2)}, u32[]{:S(2)}) %collective-permute-start.20) | collective-permute-done | bytes 196640 | tf_op jit(solution)/shard_map/ppermute | solution.py:53
  109.6 4.9 %collective-permute-done.21 = f32[2,8,32,48]{3,2,1,0:T(8,128)S(1)} collective-permute-done((f32[2,8,32,48]{3,2,1,0:T(8,128)S(1)}, f32[2,8,32,48]{3,2,1,0:T(8,128)S(1)}, u32[]{:S(2)}, u32[]{:S(2)}) %collective-permute-start.21) | collective-permute-done | bytes 98336 | tf_op jit(solution)/shard_map/ppermute | solution.py:53
  114.6 3.1 %collective-permute-start.22 = (f32[8,32,48]{2,1,0:T(8,128)S(1)}, f32[8,32,48]{2,1,0:T(8,128)S(1)}, u32[]{:S(2)}, u32[]{:S(2)}) collective-permute-start(f32[8,32,48]{2,1,0:T(8,128)S(1)} %select_bitcast_fusion.5), channel_id=1, source_target_pairs={{0,4},{1,5},{2,6},{3,7},{4,0},{5,1},{6,2},{7,3},{8,12},{9,13},{10,... | collective-permute-start | bytes 147464 | tf_op jit(solution)/shard_map/ppermute | solution.py:53
  118.9 2.9 %collective-permute-done.22 = f32[8,32,48]{2,1,0:T(8,128)S(1)} collective-permute-done((f32[8,32,48]{2,1,0:T(8,128)S(1)}, f32[8,32,48]{2,1,0:T(8,128)S(1)}, u32[]{:S(2)}, u32[]{:S(2)}) %collective-permute-start.22) | collective-permute-done | bytes 49184 | tf_op jit(solution)/shard_map/ppermute | solution.py:53
  121.9 2.5 %collective-permute-done.25 = f32[8,32,48]{2,1,0:T(8,128)S(1)} collective-permute-done((f32[8,32,48]{2,1,0:T(8,128)S(1)}, f32[8,32,48]{2,1,0:T(8,128)S(1)}, u32[]{:S(2)}, u32[]{:S(2)}) %collective-permute-start.25) | collective-permute-done | bytes 49184 | tf_op jit(solution)/shard_map/ppermute | solution.py:53
  (90 shorter events, 31.7 us)
Async XLA Ops:
  7.9 3.8 %collective-permute-start.10 = (bf16[48,16,256]{2,1,0:T(8,128)(2,1)S(1)}, bf16[48,16,256]{2,1,0:T(8,128)(2,1)S(1)}, u32[]{:S(2)}, u32[]{:S(2)}) collective-permute-start(bf16[48,16,256]{2,1,0:T(8,128)(2,1)S(1)} %broadcast_select_fusion.3), channel_id=1, source_target_pairs={{0,8},{8,0},{16,24},{24,16},{32,40},{40,32},{48,56},{56,48},{64,72... | collective-permute-start | bytes 1179656 | tf_op jit(solution)/shard_map/ppermute | solution.py:30
  9.7 7.2 %collective-permute-start.1 = (bf16[48,8,256]{2,1,0:T(8,128)(2,1)S(1)}, bf16[48,8,256]{2,1,0:T(8,128)(2,1)S(1)}, u32[]{:S(2)}, u32[]{:S(2)}) collective-permute-start(bf16[48,8,256]{2,1,0:T(8,128)(2,1)S(1)} %broadcast_select_fusion.5), channel_id=1, source_target_pairs={{0,16},{8,24},{16,0},{24,8},{32,48},{40,56},{48,32},{56,40},{64,80... | collective-permute-start | bytes 589832 | tf_op jit(solution)/shard_map/ppermute | solution.py:30
  11.8 8.3 %collective-permute-start.11 = (bf16[48,8,256]{2,1,0:T(8,128)(2,1)S(1)}, bf16[48,8,256]{2,1,0:T(8,128)(2,1)S(1)}, u32[]{:S(2)}, u32[]{:S(2)}) collective-permute-start(bf16[48,8,256]{2,1,0:T(8,128)(2,1)S(1)} %broadcast_select_fusion.6), channel_id=1, source_target_pairs={{0,128},{8,136},{16,144},{24,152},{32,160},{40,168},{48,176},{56,1... | collective-permute-start | bytes 589832 | tf_op jit(solution)/shard_map/ppermute | solution.py:30
  17.0 6.2 %collective-permute-start.2 = (bf16[48,4,256]{2,1,0:T(4,128)(2,1)S(1)}, bf16[48,4,256]{2,1,0:T(4,128)(2,1)S(1)}, u32[]{:S(2)}, u32[]{:S(2)}) collective-permute-start(bf16[48,4,256]{2,1,0:T(4,128)(2,1)S(1)} %broadcast_select_fusion.8), channel_id=1, source_target_pairs={{0,128},{8,136},{16,144},{24,152},{32,160},{40,168},{48,176},{56,1... | collective-permute-start | bytes 294920 | tf_op jit(solution)/shard_map/ppermute | solution.py:30
  20.2 6.6 %collective-permute-start.12 = (bf16[48,4,256]{2,1,0:T(4,128)(2,1)S(1)}, bf16[48,4,256]{2,1,0:T(4,128)(2,1)S(1)}, u32[]{:S(2)}, u32[]{:S(2)}) collective-permute-start(bf16[48,4,256]{2,1,0:T(4,128)(2,1)S(1)} %broadcast_select_fusion.7), channel_id=1, source_target_pairs={{0,16},{8,24},{16,0},{24,8},{32,48},{40,56},{48,32},{56,40},{64,80... | collective-permute-start | bytes 294920 | tf_op jit(solution)/shard_map/ppermute | solution.py:30
  23.4 5.7 %collective-permute-start.3 = (bf16[48,2,256]{2,1,0:T(2,128)(2,1)S(1)}, bf16[48,2,256]{2,1,0:T(2,128)(2,1)S(1)}, u32[]{:S(2)}, u32[]{:S(2)}) collective-permute-start(bf16[48,2,256]{2,1,0:T(2,128)(2,1)S(1)} %broadcast_select_fusion.11), channel_id=1, source_target_pairs={{0,32},{8,40},{16,48},{24,56},{32,0},{40,8},{48,16},{56,24},{64,96... | collective-permute-start | bytes 147464 | tf_op jit(solution)/shard_map/ppermute | solution.py:30
  27.0 8.9 %collective-permute-start.13 = (bf16[48,2,256]{2,1,0:T(2,128)(2,1)S(1)}, bf16[48,2,256]{2,1,0:T(2,128)(2,1)S(1)}, u32[]{:S(2)}, u32[]{:S(2)}) collective-permute-start(bf16[48,2,256]{2,1,0:T(2,128)(2,1)S(1)} %broadcast_select_fusion.9), channel_id=1, source_target_pairs={{0,32},{8,40},{16,48},{24,56},{32,0},{40,8},{48,16},{56,24},{64,96... | collective-permute-start | bytes 147464 | tf_op jit(solution)/shard_map/ppermute | solution.py:30
  29.3 9.3 %collective-permute-start.4 = (bf16[48,1,256]{2,1,0:T(2,128)(2,1)S(1)}, bf16[48,1,256]{2,1,0:T(2,128)(2,1)S(1)}, u32[]{:S(2)}, u32[]{:S(2)}) collective-permute-start(bf16[48,1,256]{2,1,0:T(2,128)(2,1)S(1)} %broadcast_select_fusion.15), channel_id=1, source_target_pairs={{0,64},{8,72},{16,80},{24,88},{32,96},{40,104},{48,112},{56,120},{... | collective-permute-start | bytes 73736 | tf_op jit(solution)/shard_map/ppermute | solution.py:30
  36.1 8.9 %collective-permute-start.14 = (bf16[48,1,256]{2,1,0:T(2,128)(2,1)S(1)}, bf16[48,1,256]{2,1,0:T(2,128)(2,1)S(1)}, u32[]{:S(2)}, u32[]{:S(2)}) collective-permute-start(bf16[48,1,256]{2,1,0:T(2,128)(2,1)S(1)} %broadcast_select_fusion.13), channel_id=1, source_target_pairs={{0,64},{8,72},{16,80},{24,88},{32,96},{40,104},{48,112},{56,120},{... | collective-permute-start | bytes 73736 | tf_op jit(solution)/shard_map/ppermute | solution.py:30
  38.8 8.8 %collective-permute-start.5 = (bf16[48,1,256]{2,1,0:T(2,128)(2,1)S(1)}, bf16[48,1,256]{2,1,0:T(2,128)(2,1)S(1)}, u32[]{:S(2)}, u32[]{:S(2)}) collective-permute-start(bf16[48,1,256]{2,1,0:T(2,128)(2,1)S(1)} %fusion.4), channel_id=1, source_target_pairs={{0,64},{8,72},{16,80},{24,88},{32,96},{40,104},{48,112},{56,120},{... | collective-permute-start | bytes 73736 | tf_op jit(solution)/shard_map/ppermute | solution.py:33
  45.0 8.1 %collective-permute-start.15 = (bf16[48,1,256]{2,1,0:T(2,128)(2,1)S(1)}, bf16[48,1,256]{2,1,0:T(2,128)(2,1)S(1)}, u32[]{:S(2)}, u32[]{:S(2)}) collective-permute-start(bf16[48,1,256]{2,1,0:T(2,128)(2,1)S(1)} %fusion.5), channel_id=1, source_target_pairs={{0,64},{8,72},{16,80},{24,88},{32,96},{40,104},{48,112},{56,120},{... | collective-permute-start | bytes 73736 | tf_op jit(solution)/shard_map/ppermute | solution.py:33
  47.7 7.2 %collective-permute-start.6 = (bf16[48,2,256]{2,1,0:T(2,128)(2,1)S(1)}, bf16[48,2,256]{2,1,0:T(2,128)(2,1)S(1)}, u32[]{:S(2)}, u32[]{:S(2)}) collective-permute-start(bf16[48,2,256]{2,1,0:T(2,128)(2,1)S(1)} %broadcast_select_fusion.18), channel_id=1, source_target_pairs={{0,32},{8,40},{16,48},{24,56},{32,0},{40,8},{48,16},{56,24},{64,96... | collective-permute-start | bytes 147464 | tf_op jit(solution)/shard_map/ppermute | solution.py:33
  53.4 5.2 %collective-permute-start.16 = (bf16[48,2,256]{2,1,0:T(2,128)(2,1)S(1)}, bf16[48,2,256]{2,1,0:T(2,128)(2,1)S(1)}, u32[]{:S(2)}, u32[]{:S(2)}) collective-permute-start(bf16[48,2,256]{2,1,0:T(2,128)(2,1)S(1)} %broadcast_select_fusion.17), channel_id=1, source_target_pairs={{0,32},{8,40},{16,48},{24,56},{32,0},{40,8},{48,16},{56,24},{64,96... | collective-permute-start | bytes 147464 | tf_op jit(solution)/shard_map/ppermute | solution.py:33
  55.1 6.8 %collective-permute-start.7 = (bf16[48,4,256]{2,1,0:T(4,128)(2,1)S(1)}, bf16[48,4,256]{2,1,0:T(4,128)(2,1)S(1)}, u32[]{:S(2)}, u32[]{:S(2)}) collective-permute-start(bf16[48,4,256]{2,1,0:T(4,128)(2,1)S(1)} %maximum_select_fusion.6), channel_id=1, source_target_pairs={{0,128},{8,136},{16,144},{24,152},{32,160},{40,168},{48,176},{56,1... | collective-permute-start | bytes 294920 | tf_op jit(solution)/shard_map/ppermute | solution.py:33
  58.7 5.0 %collective-permute-start.17 = (bf16[48,4,256]{2,1,0:T(4,128)(2,1)S(1)}, bf16[48,4,256]{2,1,0:T(4,128)(2,1)S(1)}, u32[]{:S(2)}, u32[]{:S(2)}) collective-permute-start(bf16[48,4,256]{2,1,0:T(4,128)(2,1)S(1)} %maximum_select_fusion.7), channel_id=1, source_target_pairs={{0,16},{8,24},{16,0},{24,8},{32,48},{40,56},{48,32},{56,40},{64,80... | collective-permute-start | bytes 294920 | tf_op jit(solution)/shard_map/ppermute | solution.py:33
  62.1 5.8 %collective-permute-start.8 = (bf16[48,8,256]{2,1,0:T(8,128)(2,1)S(1)}, bf16[48,8,256]{2,1,0:T(8,128)(2,1)S(1)}, u32[]{:S(2)}, u32[]{:S(2)}) collective-permute-start(bf16[48,8,256]{2,1,0:T(8,128)(2,1)S(1)} %maximum_select_fusion.4), channel_id=1, source_target_pairs={{0,16},{8,24},{16,0},{24,8},{32,48},{40,56},{48,32},{56,40},{64,80... | collective-permute-start | bytes 589832 | tf_op jit(solution)/shard_map/ppermute | solution.py:33
  63.9 7.3 %collective-permute-start.18 = (bf16[48,8,256]{2,1,0:T(8,128)(2,1)S(1)}, bf16[48,8,256]{2,1,0:T(8,128)(2,1)S(1)}, u32[]{:S(2)}, u32[]{:S(2)}) collective-permute-start(bf16[48,8,256]{2,1,0:T(8,128)(2,1)S(1)} %maximum_select_fusion.5), channel_id=1, source_target_pairs={{0,128},{8,136},{16,144},{24,152},{32,160},{40,168},{48,176},{56,1... | collective-permute-start | bytes 589832 | tf_op jit(solution)/shard_map/ppermute | solution.py:33
  68.0 4.5 %collective-permute-start.9 = (bf16[48,16,256]{2,1,0:T(8,128)(2,1)S(1)}, bf16[48,16,256]{2,1,0:T(8,128)(2,1)S(1)}, u32[]{:S(2)}, u32[]{:S(2)}) collective-permute-start(bf16[48,16,256]{2,1,0:T(8,128)(2,1)S(1)} %maximum_select_fusion.2), channel_id=1, source_target_pairs={{0,8},{8,0},{16,24},{24,16},{32,40},{40,32},{48,56},{56,48},{64,72... | collective-permute-start | bytes 1179656 | tf_op jit(solution)/shard_map/ppermute | solution.py:33
  92.0 14.4 %collective-permute-start.20 = (f32[2,2,8,32,48]{4,3,2,1,0:T(8,128)S(1)}, f32[2,2,8,32,48]{4,3,2,1,0:T(8,128)S(1)}, u32[]{:S(2)}, u32[]{:S(2)}) collective-permute-start(f32[2,2,8,32,48]{4,3,2,1,0:T(8,128)S(1)} %select_bitcast_fusion.1), channel_id=1, source_target_pairs={{0,1},{1,0},{2,3},{3,2},{4,5},{5,4},{6,7},{7,6},{8,9},{9,8},{10,11... | collective-permute-start | bytes 589832 | tf_op jit(solution)/shard_map/ppermute | solution.py:53
  93.4 14.8 %collective-permute-start.23 = (f32[2,2,8,32,48]{4,3,2,1,0:T(8,128)S(1)}, f32[2,2,8,32,48]{4,3,2,1,0:T(8,128)S(1)}, u32[]{:S(2)}, u32[]{:S(2)}) collective-permute-start(f32[2,2,8,32,48]{4,3,2,1,0:T(8,128)S(1)} %copy.21), channel_id=1, source_target_pairs={{0,2},{1,3},{2,0},{3,1},{4,6},{5,7},{6,4},{7,5},{8,10},{9,11},{10,... | collective-permute-start | bytes 589832 | tf_op jit(solution)/shard_map/ppermute | solution.py:53
  106.6 7.9 %collective-permute-start.21 = (f32[2,8,32,48]{3,2,1,0:T(8,128)S(1)}, f32[2,8,32,48]{3,2,1,0:T(8,128)S(1)}, u32[]{:S(2)}, u32[]{:S(2)}) collective-permute-start(f32[2,8,32,48]{3,2,1,0:T(8,128)S(1)} %select_bitcast_fusion.3), channel_id=1, source_target_pairs={{0,2},{1,3},{2,0},{3,1},{4,6},{5,7},{6,4},{7,5},{8,10},{9,11},{10,... | collective-permute-start | bytes 294920 | tf_op jit(solution)/shard_map/ppermute | solution.py:53
  108.4 9.3 %collective-permute-start.24 = (f32[2,8,32,48]{3,2,1,0:T(8,128)S(1)}, f32[2,8,32,48]{3,2,1,0:T(8,128)S(1)}, u32[]{:S(2)}, u32[]{:S(2)}) collective-permute-start(f32[2,8,32,48]{3,2,1,0:T(8,128)S(1)} %select_bitcast_fusion.2), channel_id=1, source_target_pairs={{0,1},{1,0},{2,3},{3,2},{4,5},{5,4},{6,7},{7,6},{8,9},{9,8},{10,11... | collective-permute-start | bytes 294920 | tf_op jit(solution)/shard_map/ppermute | solution.py:53
  114.6 7.2 %collective-permute-start.22 = (f32[8,32,48]{2,1,0:T(8,128)S(1)}, f32[8,32,48]{2,1,0:T(8,128)S(1)}, u32[]{:S(2)}, u32[]{:S(2)}) collective-permute-start(f32[8,32,48]{2,1,0:T(8,128)S(1)} %select_bitcast_fusion.5), channel_id=1, source_target_pairs={{0,4},{1,5},{2,6},{3,7},{4,0},{5,1},{6,2},{7,3},{8,12},{9,13},{10,... | collective-permute-start | bytes 147464 | tf_op jit(solution)/shard_map/ppermute | solution.py:53
  117.8 6.6 %collective-permute-start.25 = (f32[8,32,48]{2,1,0:T(8,128)S(1)}, f32[8,32,48]{2,1,0:T(8,128)S(1)}, u32[]{:S(2)}, u32[]{:S(2)}) collective-permute-start(f32[8,32,48]{2,1,0:T(8,128)S(1)} %select_bitcast_fusion.4), channel_id=1, source_target_pairs={{0,4},{1,5},{2,6},{3,7},{4,0},{5,1},{6,2},{7,3},{8,12},{9,13},{10,... | collective-permute-start | bytes 147464 | tf_op jit(solution)/shard_map/ppermute | solution.py:53
  (2 other events, 3.8 us)

commit v2 on v1

--- a/solution.py
+++ b/solution.py
@@ -9,7 +9,7 @@
 
 LAGS = 64
 EDGE = 64
-TIME_BLOCK = 1024
+TIME_BLOCK = 2048
 CHAN_BITS = ((0, 1, 4, 2, 3), (0, 4, 1, 2, 3))
 WIN_BITS = ((0, 1, 2), (1, 0, 2))
 
@@ -19,11 +19,10 @@
 
 
 def broadcast(masked, me, axis, size, order):
-    rows, samples = masked.shape
-    pieces = masked.reshape(rows, size, samples // size)
+    pieces = masked
     for bit in order:
-        half = pieces.shape[1] // 2
-        low, high = pieces[:, :half], pieces[:, half:]
+        half = pieces.shape[0] // 2
+        low, high = pieces[:half], pieces[half:]
         mine = ((me >> bit) & 1) == 0
         send = jnp.where(mine, high, low)
         keep = jnp.where(mine, low, high)
@@ -32,18 +31,18 @@
         mine = ((me >> bit) & 1) == 0
         got = lax.ppermute(pieces, axis, xor_pairs(size, bit))
         pieces = jnp.where(
-            mine, jnp.concatenate([pieces, got], 1), jnp.concatenate([got, pieces], 1)
+            mine, jnp.concatenate([pieces, got], 0), jnp.concatenate([got, pieces], 0)
         )
-    return pieces.reshape(rows, samples)
+    return pieces
 
 
 def scatter_lags(complete, me, axis, size, order):
-    lags = complete.shape[0]
+    rows, width = complete.shape
     bits = size.bit_length() - 1
-    parts = complete.reshape(*([2] * bits), lags // size, *complete.shape[1:])
+    parts = complete.reshape(rows, *([2] * bits), width // size)
     remaining = list(reversed(range(bits)))
     for bit in order:
-        where = remaining.index(bit)
+        where = 1 + remaining.index(bit)
         remaining.remove(bit)
         mine = ((me >> bit) & 1) == 0
         low = lax.index_in_dim(parts, 0, where, keepdims=False)
@@ -55,7 +54,9 @@
 
 
 def correlate(sources, padded, chan_dev):
-    rows, samples = sources.shape
+    piece_count, rows, piece_width = sources.shape
+    samples = piece_count * piece_width
+    per_block = TIME_BLOCK // piece_width
     width = TIME_BLOCK + 128
 
     def kernel(src_ref, w_ref, out_ref):
@@ -67,18 +68,19 @@
                 for lag in range(LAGS)
             ]
             stacked = jnp.concatenate(parts, 0)
-            chunk = src_ref[:, pl.ds(base, TIME_BLOCK)]
+            first = pl.multiple_of(k * per_block, per_block)
+            chunk = jnp.concatenate([src_ref[first + j] for j in range(per_block)], 1)
             return acc + lax.dot_general(
                 stacked, chunk, (((1,), (1,)), ((), ())), preferred_element_type=jnp.float32
             )
 
         out_ref[...] = lax.fori_loop(
             0, samples // TIME_BLOCK, block, jnp.zeros((LAGS * chan_dev, rows), jnp.float32)
-        )
+        ).T
 
     return pl.pallas_call(
         kernel,
-        out_shape=jax.ShapeDtypeStruct((LAGS * chan_dev, rows), jnp.float32),
+        out_shape=jax.ShapeDtypeStruct((rows, LAGS * chan_dev), jnp.float32),
         in_specs=[
             pl.BlockSpec(memory_space=pltpu.VMEM),
             pl.BlockSpec(memory_space=pltpu.VMEM),
@@ -105,29 +107,28 @@
         [jnp.where(chan_me == owner[step], outgoing, jnp.zeros_like(outgoing)) for step in range(step_count)],
         0,
     )
-    rows = masked.shape[0] // 2
+    rows = masked.shape[0]
+    masked = masked.reshape(rows, chan_size, samples // chan_size).transpose(1, 0, 2)
+    half = rows // 2
     sources = jnp.concatenate(
         [
-            broadcast(masked[which * rows : (which + 1) * rows], chan_me, "chan", chan_size, order)
+            broadcast(masked[:, which * half : (which + 1) * half], chan_me, "chan", chan_size, order)
             for which, order in enumerate(CHAN_BITS)
         ],
-        0,
+        1,
     )
     padded = jnp.pad(whitened, ((0, 0), (EDGE, EDGE)))
     factor = own_flag / math.sqrt(samples)
     complete = correlate(sources, padded, chan_dev) * factor
-    complete = complete.reshape(LAGS, chan_dev, step_count * chan_dev)
-    cols = complete.shape[-1] // 2
     reduced = jnp.concatenate(
         [
-            scatter_lags(complete[..., which * cols : (which + 1) * cols], win_me, "win", win_size, order)
+            scatter_lags(complete[which * half : (which + 1) * half], win_me, "win", win_size, order)
             for which, order in enumerate(WIN_BITS)
         ],
-        -1,
+        0,
     )
     per_dev = LAGS // win_size
-    reduced = reduced.reshape(per_dev, chan_dev, step_count, chan_dev)
-    return jnp.transpose(reduced, (2, 3, 0, 1))
+    return reduced.reshape(step_count, chan_dev, per_dev, chan_dev)
 
 
 def solution(mesh):

time: 126 us -> 110 us (0.87)
  waiting for transfers between devices: 39.4 us -> 29.2 us
  other arithmetic: 10.5 us -> 6.48 us
  Pallas kernels: 14.9 us -> 13.3 us
    ppermute x6, waiting for transfers between devices: 21.6 us -> 9.76 us  [scatter_lags(): parts = keep + lax.ppermute(send, axis, xor_pairs(size, bit))]
    select_n x10, other arithmetic: 2.09 us -> 0.4 us  [broadcast(): jnp.where(mine, jnp.concatenate([pieces, got], 0), jnp.concatenate([got,...]
    pallas_call x1, Pallas kernels: 14.9 us -> 13.3 us  [correlate(): pl.pallas_call(kernel, out_shape=jax.ShapeDtypeStruct((rows, LAGS * chan_...]
    ppermute x10, waiting for transfers between devices: 6.5 us -> 7.82 us  [broadcast(): pieces = keep + lax.ppermute(send, axis, xor_pairs(size, bit))]
    reshape x1 -> x3, local copies, waits for them, and re-layouts: 0.23 us -> 1.54 us  [the longest x1 0.89 us: body(): return reduced.reshape(step_count, chan_dev, per_dev, chan_dev)]
  transfers between devices with their start and end apart: 26 -> 26, of which waited for: 16 -> 18; matrix products, arithmetic and copies ran while one was open for 4% -> 3% of each run, Pallas kernels for 0% -> 0%
where the time goes in v2:
time: 110 us
  starting transfers between devices  52.1 us (47%)
  waiting for transfers between devices  29.2 us (27%)
  Pallas kernels  13.3 us (12%)
  other arithmetic  6.48 us (6%)
  local copies, waits for them, and re-layouts  5.54 us (5%)
  between operations  2.93 us (3%)
    ppermute x10, starting transfers between devices, broadcast(): pieces = keep + lax.ppermute(send, axis, xor_pairs(size, bit))  22.7 us
    ppermute x10, starting transfers between devices, broadcast(): got = lax.ppermute(pieces, axis, xor_pairs(size, bit))  19.5 us
    pallas_call x1, Pallas kernels, correlate(): pl.pallas_call(kernel, out_shape=jax.ShapeDtypeStruct((rows, LAGS * chan_...  13.3 us
    ppermute x10, waiting for transfers between devices, broadcast(): got = lax.ppermute(pieces, axis, xor_pairs(size, bit))  11.6 us
    ppermute x6, starting transfers between devices, scatter_lags(): parts = keep + lax.ppermute(send, axis, xor_pairs(size, bit))  9.91 us
    ppermute x6, waiting for transfers between devices, scatter_lags(): parts = keep + lax.ppermute(send, axis, xor_pairs(size, bit))  9.76 us
    ppermute x10, waiting for transfers between devices, broadcast(): pieces = keep + lax.ppermute(send, axis, xor_pairs(size, bit))  7.82 us
  transfers between devices with their start and end apart: 26, of which 18 were waited for; matrix products, arithmetic and copies ran while one was open for 3% of the time, Pallas kernels for 0%

profile of v2, /device:TPU:8, one launch (start us, length us, event | category | flops | bytes accessed | tf_op | source)
XLA Modules:
  0.0 109.6 jit_solution(8605108941048079524)
XLA Ops:
  9.8 2.0 %collective-permute-start.1 = (bf16[8,48,256]{2,1,0:T(8,128)(2,1)S(1)}, bf16[8,48,256]{2,1,0:T(8,128)(2,1)S(1)}, u32[]{:S(2)}, u32[]{:S(2)}) collective-permute-start(bf16[8,48,256]{2,1,0:T(8,128)(2,1)S(1)} %broadcast_select_fusion.6), channel_id=1, source_target_pairs={{0,16},{8,24},{16,0},{24,8},{32,48},{40,56},{48,32},{56,40},{64,80... | collective-permute-start | bytes 589832 | tf_op jit(solution)/shard_map/ppermute | solution.py:29
  11.8 2.4 %collective-permute-start.11 = (bf16[8,48,256]{2,1,0:T(8,128)(2,1)S(1)}, bf16[8,48,256]{2,1,0:T(8,128)(2,1)S(1)}, u32[]{:S(2)}, u32[]{:S(2)}) collective-permute-start(bf16[8,48,256]{2,1,0:T(8,128)(2,1)S(1)} %broadcast_select_fusion.7), channel_id=1, source_target_pairs={{0,128},{8,136},{16,144},{24,152},{32,160},{40,168},{48,176},{56,1... | collective-permute-start | bytes 589832 | tf_op jit(solution)/shard_map/ppermute | solution.py:29
  14.2 2.8 %collective-permute-done.1 = bf16[8,48,256]{2,1,0:T(8,128)(2,1)S(1)} collective-permute-done((bf16[8,48,256]{2,1,0:T(8,128)(2,1)S(1)}, bf16[8,48,256]{2,1,0:T(8,128)(2,1)S(1)}, u32[]{:S(2)}, u32[]{:S(2)}) %collective-permute-start.1) | collective-permute-done | bytes 196640 | tf_op jit(solution)/shard_map/ppermute | solution.py:29
  17.1 2.4 %collective-permute-start.2 = (bf16[4,48,256]{2,1,0:T(8,128)(2,1)S(1)}, bf16[4,48,256]{2,1,0:T(8,128)(2,1)S(1)}, u32[]{:S(2)}, u32[]{:S(2)}) collective-permute-start(bf16[4,48,256]{2,1,0:T(8,128)(2,1)S(1)} %broadcast_select_fusion.10), channel_id=1, source_target_pairs={{0,128},{8,136},{16,144},{24,152},{32,160},{40,168},{48,176},{56,1... | collective-permute-start | bytes 294920 | tf_op jit(solution)/shard_map/ppermute | solution.py:29
  21.4 1.9 %collective-permute-done.2 = bf16[4,48,256]{2,1,0:T(8,128)(2,1)S(1)} collective-permute-done((bf16[4,48,256]{2,1,0:T(8,128)(2,1)S(1)}, bf16[4,48,256]{2,1,0:T(8,128)(2,1)S(1)}, u32[]{:S(2)}, u32[]{:S(2)}) %collective-permute-start.2) | collective-permute-done | bytes 98336 | tf_op jit(solution)/shard_map/ppermute | solution.py:29
  23.3 3.4 %collective-permute-start.3 = (bf16[2,48,256]{2,1,0:T(8,128)(2,1)S(1)}, bf16[2,48,256]{2,1,0:T(8,128)(2,1)S(1)}, u32[]{:S(2)}, u32[]{:S(2)}) collective-permute-start(bf16[2,48,256]{2,1,0:T(8,128)(2,1)S(1)} %broadcast_select_fusion.12), channel_id=1, source_target_pairs={{0,32},{8,40},{16,48},{24,56},{32,0},{40,8},{48,16},{56,24},{64,96... | collective-permute-start | bytes 147464 | tf_op jit(solution)/shard_map/ppermute | solution.py:29
  26.7 2.1 %collective-permute-start.13 = (bf16[2,48,256]{2,1,0:T(8,128)(2,1)S(1)}, bf16[2,48,256]{2,1,0:T(8,128)(2,1)S(1)}, u32[]{:S(2)}, u32[]{:S(2)}) collective-permute-start(bf16[2,48,256]{2,1,0:T(8,128)(2,1)S(1)} %broadcast_select_fusion.11), channel_id=1, source_target_pairs={{0,32},{8,40},{16,48},{24,56},{32,0},{40,8},{48,16},{56,24},{64,96... | collective-permute-start | bytes 147464 | tf_op jit(solution)/shard_map/ppermute | solution.py:29
  29.2 6.4 %collective-permute-start.4 = (bf16[1,48,256]{2,1,0:T(8,128)(2,1)S(1)}, bf16[1,48,256]{2,1,0:T(8,128)(2,1)S(1)}, u32[]{:S(2)}, u32[]{:S(2)}) collective-permute-start(bf16[1,48,256]{2,1,0:T(8,128)(2,1)S(1)} %broadcast_select_fusion.14), channel_id=1, source_target_pairs={{0,64},{8,72},{16,80},{24,88},{32,96},{40,104},{48,112},{56,120},{... | collective-permute-start | bytes 73736 | tf_op jit(solution)/shard_map/ppermute | solution.py:29
  35.6 2.3 %collective-permute-start.14 = (bf16[1,48,256]{2,1,0:T(8,128)(2,1)S(1)}, bf16[1,48,256]{2,1,0:T(8,128)(2,1)S(1)}, u32[]{:S(2)}, u32[]{:S(2)}) collective-permute-start(bf16[1,48,256]{2,1,0:T(8,128)(2,1)S(1)} %broadcast_select_fusion.13), channel_id=1, source_target_pairs={{0,64},{8,72},{16,80},{24,88},{32,96},{40,104},{48,112},{56,120},{... | collective-permute-start | bytes 73736 | tf_op jit(solution)/shard_map/ppermute | solution.py:29
  38.0 5.5 %collective-permute-start.5 = (bf16[1,48,256]{2,1,0:T(8,128)(2,1)S(1)}, bf16[1,48,256]{2,1,0:T(8,128)(2,1)S(1)}, u32[]{:S(2)}, u32[]{:S(2)}) collective-permute-start(bf16[1,48,256]{2,1,0:T(8,128)(2,1)S(1)} %select_add_fusion.9), channel_id=1, source_target_pairs={{0,64},{8,72},{16,80},{24,88},{32,96},{40,104},{48,112},{56,120},{... | collective-permute-start | bytes 73736 | tf_op jit(solution)/shard_map/ppermute | solution.py:32
  43.7 2.0 %collective-permute-start.15 = (bf16[1,48,256]{2,1,0:T(8,128)(2,1)S(1)}, bf16[1,48,256]{2,1,0:T(8,128)(2,1)S(1)}, u32[]{:S(2)}, u32[]{:S(2)}) collective-permute-start(bf16[1,48,256]{2,1,0:T(8,128)(2,1)S(1)} %select_add_fusion.8), channel_id=1, source_target_pairs={{0,64},{8,72},{16,80},{24,88},{32,96},{40,104},{48,112},{56,120},{... | collective-permute-start | bytes 73736 | tf_op jit(solution)/shard_map/ppermute | solution.py:32
  45.8 2.1 %collective-permute-start.6 = (bf16[2,48,256]{2,1,0:T(8,128)(2,1)S(1)}, bf16[2,48,256]{2,1,0:T(8,128)(2,1)S(1)}, u32[]{:S(2)}, u32[]{:S(2)}) collective-permute-start(bf16[2,48,256]{2,1,0:T(8,128)(2,1)S(1)} %maximum_select_fusion.8), channel_id=1, source_target_pairs={{0,32},{8,40},{16,48},{24,56},{32,0},{40,8},{48,16},{56,24},{64,96... | collective-permute-start | bytes 147464 | tf_op jit(solution)/shard_map/ppermute | solution.py:32
  47.9 3.8 %collective-permute-done.15 = bf16[1,48,256]{2,1,0:T(8,128)(2,1)S(1)} collective-permute-done((bf16[1,48,256]{2,1,0:T(8,128)(2,1)S(1)}, bf16[1,48,256]{2,1,0:T(8,128)(2,1)S(1)}, u32[]{:S(2)}, u32[]{:S(2)}) %collective-permute-start.15) | collective-permute-done | bytes 24608 | tf_op jit(solution)/shard_map/ppermute | solution.py:32
  51.7 1.9 %collective-permute-start.16 = (bf16[2,48,256]{2,1,0:T(8,128)(2,1)S(1)}, bf16[2,48,256]{2,1,0:T(8,128)(2,1)S(1)}, u32[]{:S(2)}, u32[]{:S(2)}) collective-permute-start(bf16[2,48,256]{2,1,0:T(8,128)(2,1)S(1)} %maximum_select_fusion.9), channel_id=1, source_target_pairs={{0,32},{8,40},{16,48},{24,56},{32,0},{40,8},{48,16},{56,24},{64,96... | collective-permute-start | bytes 147464 | tf_op jit(solution)/shard_map/ppermute | solution.py:32
  53.6 2.4 %collective-permute-start.7 = (bf16[4,48,256]{2,1,0:T(8,128)(2,1)S(1)}, bf16[4,48,256]{2,1,0:T(8,128)(2,1)S(1)}, u32[]{:S(2)}, u32[]{:S(2)}) collective-permute-start(bf16[4,48,256]{2,1,0:T(8,128)(2,1)S(1)} %maximum_select_fusion.6), channel_id=1, source_target_pairs={{0,128},{8,136},{16,144},{24,152},{32,160},{40,168},{48,176},{56,1... | collective-permute-start | bytes 294920 | tf_op jit(solution)/shard_map/ppermute | solution.py:32
  59.8 1.9 %collective-permute-start.8 = (bf16[8,48,256]{2,1,0:T(8,128)(2,1)S(1)}, bf16[8,48,256]{2,1,0:T(8,128)(2,1)S(1)}, u32[]{:S(2)}, u32[]{:S(2)}) collective-permute-start(bf16[8,48,256]{2,1,0:T(8,128)(2,1)S(1)} %maximum_select_fusion.4), channel_id=1, source_target_pairs={{0,16},{8,24},{16,0},{24,8},{32,48},{40,56},{48,32},{56,40},{64,80... | collective-permute-start | bytes 589832 | tf_op jit(solution)/shard_map/ppermute | solution.py:32
  61.9 2.4 %collective-permute-start.18 = (bf16[8,48,256]{2,1,0:T(8,128)(2,1)S(1)}, bf16[8,48,256]{2,1,0:T(8,128)(2,1)S(1)}, u32[]{:S(2)}, u32[]{:S(2)}) collective-permute-start(bf16[8,48,256]{2,1,0:T(8,128)(2,1)S(1)} %maximum_select_fusion.5), channel_id=1, source_target_pairs={{0,128},{8,136},{16,144},{24,152},{32,160},{40,168},{48,176},{56,1... | collective-permute-start | bytes 589832 | tf_op jit(solution)/shard_map/ppermute | solution.py:32
  65.9 3.2 %collective-permute-done.18 = bf16[8,48,256]{2,1,0:T(8,128)(2,1)S(1)} collective-permute-done((bf16[8,48,256]{2,1,0:T(8,128)(2,1)S(1)}, bf16[8,48,256]{2,1,0:T(8,128)(2,1)S(1)}, u32[]{:S(2)}, u32[]{:S(2)}) %collective-permute-start.18) | collective-permute-done | bytes 196640 | tf_op jit(solution)/shard_map/ppermute | solution.py:32
  72.5 13.3 %shard_map.37 = f32[96,2048]{1,0:T(8,128)} custom-call(bf16[32,96,256]{2,1,0:T(8,128)(2,1)} %pad_maximum_fusion.src_ref, bf16[32,8320]{1,0:T(8,128)(2,1)} %pad.4.w_ref), custom_call_target="tpu_custom_call" | custom-call | tf_op jit(solution)/shard_map/pallas_call | solution.py:81
  90.8 4.0 %collective-permute-done.20 = f32[48,2,2,256]{3,0,1,2:T(8,128)S(1)} collective-permute-done((f32[48,2,2,256]{3,0,1,2:T(8,128)S(1)}, f32[48,2,2,256]{3,0,1,2:T(8,128)S(1)}, u32[]{:S(2)}, u32[]{:S(2)}) %collective-permute-start.20) | collective-permute-done | bytes 196640 | tf_op jit(solution)/shard_map/ppermute | solution.py:52
  97.9 1.7 %collective-permute-done.21 = f32[48,2,256]{2,0,1:T(8,128)S(1)} collective-permute-done((f32[48,2,256]{2,0,1:T(8,128)S(1)}, f32[48,2,256]{2,0,1:T(8,128)S(1)}, u32[]{:S(2)}, u32[]{:S(2)}) %collective-permute-start.21) | collective-permute-done | bytes 98336 | tf_op jit(solution)/shard_map/ppermute | solution.py:52
  99.6 3.1 %collective-permute-start.22 = (f32[48,256]{1,0:T(8,128)S(1)}, f32[48,256]{1,0:T(8,128)S(1)}, u32[]{:S(2)}, u32[]{:S(2)}) collective-permute-start(f32[48,256]{1,0:T(8,128)S(1)} %select_bitcast_fusion.2), channel_id=1, source_target_pairs={{0,4},{1,5},{2,6},{3,7},{4,0},{5,1},{6,2},{7,3},{8,12},{9,13},{10,... | collective-permute-start | bytes 147464 | tf_op jit(solution)/shard_map/ppermute | solution.py:52
  103.0 1.6 %collective-permute-start.25 = (f32[48,256]{1,0:T(8,128)S(1)}, f32[48,256]{1,0:T(8,128)S(1)}, u32[]{:S(2)}, u32[]{:S(2)}) collective-permute-start(f32[48,256]{1,0:T(8,128)S(1)} %bitcast.67), channel_id=1, source_target_pairs={{0,4},{1,5},{2,6},{3,7},{4,0},{5,1},{6,2},{7,3},{8,12},{9,13},{10,... | collective-permute-start | bytes 147464 | tf_op jit(solution)/shard_map/ppermute | solution.py:52
  105.6 3.0 %collective-permute-done.25 = f32[48,256]{1,0:T(8,128)S(1)} collective-permute-done((f32[48,256]{1,0:T(8,128)S(1)}, f32[48,256]{1,0:T(8,128)S(1)}, u32[]{:S(2)}, u32[]{:S(2)}) %collective-permute-start.25) | collective-permute-done | bytes 49184 | tf_op jit(solution)/shard_map/ppermute | solution.py:52
  (90 shorter events, 29.2 us)
Async XLA Ops:
  7.4 2.3 %collective-permute-start.10 = (bf16[16,48,256]{2,1,0:T(8,128)(2,1)S(1)}, bf16[16,48,256]{2,1,0:T(8,128)(2,1)S(1)}, u32[]{:S(2)}, u32[]{:S(2)}) collective-permute-start(bf16[16,48,256]{2,1,0:T(8,128)(2,1)S(1)} %get-tuple-element.10), channel_id=1, source_target_pairs={{0,8},{8,0},{16,24},{24,16},{32,40},{40,32},{48,56},{56,48},{64,72... | collective-permute-start | bytes 1179656 | tf_op jit(solution)/shard_map/ppermute | solution.py:29
  9.8 7.2 %collective-permute-start.1 = (bf16[8,48,256]{2,1,0:T(8,128)(2,1)S(1)}, bf16[8,48,256]{2,1,0:T(8,128)(2,1)S(1)}, u32[]{:S(2)}, u32[]{:S(2)}) collective-permute-start(bf16[8,48,256]{2,1,0:T(8,128)(2,1)S(1)} %broadcast_select_fusion.6), channel_id=1, source_target_pairs={{0,16},{8,24},{16,0},{24,8},{32,48},{40,56},{48,32},{56,40},{64,80... | collective-permute-start | bytes 589832 | tf_op jit(solution)/shard_map/ppermute | solution.py:29
  11.8 8.3 %collective-permute-start.11 = (bf16[8,48,256]{2,1,0:T(8,128)(2,1)S(1)}, bf16[8,48,256]{2,1,0:T(8,128)(2,1)S(1)}, u32[]{:S(2)}, u32[]{:S(2)}) collective-permute-start(bf16[8,48,256]{2,1,0:T(8,128)(2,1)S(1)} %broadcast_select_fusion.7), channel_id=1, source_target_pairs={{0,128},{8,136},{16,144},{24,152},{32,160},{40,168},{48,176},{56,1... | collective-permute-start | bytes 589832 | tf_op jit(solution)/shard_map/ppermute | solution.py:29
  17.1 6.2 %collective-permute-start.2 = (bf16[4,48,256]{2,1,0:T(8,128)(2,1)S(1)}, bf16[4,48,256]{2,1,0:T(8,128)(2,1)S(1)}, u32[]{:S(2)}, u32[]{:S(2)}) collective-permute-start(bf16[4,48,256]{2,1,0:T(8,128)(2,1)S(1)} %broadcast_select_fusion.10), channel_id=1, source_target_pairs={{0,128},{8,136},{16,144},{24,152},{32,160},{40,168},{48,176},{56,1... | collective-permute-start | bytes 294920 | tf_op jit(solution)/shard_map/ppermute | solution.py:29
  20.2 6.5 %collective-permute-start.12 = (bf16[4,48,256]{2,1,0:T(8,128)(2,1)S(1)}, bf16[4,48,256]{2,1,0:T(8,128)(2,1)S(1)}, u32[]{:S(2)}, u32[]{:S(2)}) collective-permute-start(bf16[4,48,256]{2,1,0:T(8,128)(2,1)S(1)} %broadcast_select_fusion.9), channel_id=1, source_target_pairs={{0,16},{8,24},{16,0},{24,8},{32,48},{40,56},{48,32},{56,40},{64,80... | collective-permute-start | bytes 294920 | tf_op jit(solution)/shard_map/ppermute | solution.py:29
  23.3 5.8 %collective-permute-start.3 = (bf16[2,48,256]{2,1,0:T(8,128)(2,1)S(1)}, bf16[2,48,256]{2,1,0:T(8,128)(2,1)S(1)}, u32[]{:S(2)}, u32[]{:S(2)}) collective-permute-start(bf16[2,48,256]{2,1,0:T(8,128)(2,1)S(1)} %broadcast_select_fusion.12), channel_id=1, source_target_pairs={{0,32},{8,40},{16,48},{24,56},{32,0},{40,8},{48,16},{56,24},{64,96... | collective-permute-start | bytes 147464 | tf_op jit(solution)/shard_map/ppermute | solution.py:29
  26.7 8.9 %collective-permute-start.13 = (bf16[2,48,256]{2,1,0:T(8,128)(2,1)S(1)}, bf16[2,48,256]{2,1,0:T(8,128)(2,1)S(1)}, u32[]{:S(2)}, u32[]{:S(2)}) collective-permute-start(bf16[2,48,256]{2,1,0:T(8,128)(2,1)S(1)} %broadcast_select_fusion.11), channel_id=1, source_target_pairs={{0,32},{8,40},{16,48},{24,56},{32,0},{40,8},{48,16},{56,24},{64,96... | collective-permute-start | bytes 147464 | tf_op jit(solution)/shard_map/ppermute | solution.py:29
  29.2 8.7 %collective-permute-start.4 = (bf16[1,48,256]{2,1,0:T(8,128)(2,1)S(1)}, bf16[1,48,256]{2,1,0:T(8,128)(2,1)S(1)}, u32[]{:S(2)}, u32[]{:S(2)}) collective-permute-start(bf16[1,48,256]{2,1,0:T(8,128)(2,1)S(1)} %broadcast_select_fusion.14), channel_id=1, source_target_pairs={{0,64},{8,72},{16,80},{24,88},{32,96},{40,104},{48,112},{56,120},{... | collective-permute-start | bytes 73736 | tf_op jit(solution)/shard_map/ppermute | solution.py:29
  35.6 8.1 %collective-permute-start.14 = (bf16[1,48,256]{2,1,0:T(8,128)(2,1)S(1)}, bf16[1,48,256]{2,1,0:T(8,128)(2,1)S(1)}, u32[]{:S(2)}, u32[]{:S(2)}) collective-permute-start(bf16[1,48,256]{2,1,0:T(8,128)(2,1)S(1)} %broadcast_select_fusion.13), channel_id=1, source_target_pairs={{0,64},{8,72},{16,80},{24,88},{32,96},{40,104},{48,112},{56,120},{... | collective-permute-start | bytes 73736 | tf_op jit(solution)/shard_map/ppermute | solution.py:29
  38.0 7.8 %collective-permute-start.5 = (bf16[1,48,256]{2,1,0:T(8,128)(2,1)S(1)}, bf16[1,48,256]{2,1,0:T(8,128)(2,1)S(1)}, u32[]{:S(2)}, u32[]{:S(2)}) collective-permute-start(bf16[1,48,256]{2,1,0:T(8,128)(2,1)S(1)} %select_add_fusion.9), channel_id=1, source_target_pairs={{0,64},{8,72},{16,80},{24,88},{32,96},{40,104},{48,112},{56,120},{... | collective-permute-start | bytes 73736 | tf_op jit(solution)/shard_map/ppermute | solution.py:32
  43.7 8.0 %collective-permute-start.15 = (bf16[1,48,256]{2,1,0:T(8,128)(2,1)S(1)}, bf16[1,48,256]{2,1,0:T(8,128)(2,1)S(1)}, u32[]{:S(2)}, u32[]{:S(2)}) collective-permute-start(bf16[1,48,256]{2,1,0:T(8,128)(2,1)S(1)} %select_add_fusion.8), channel_id=1, source_target_pairs={{0,64},{8,72},{16,80},{24,88},{32,96},{40,104},{48,112},{56,120},{... | collective-permute-start | bytes 73736 | tf_op jit(solution)/shard_map/ppermute | solution.py:32
  45.8 7.8 %collective-permute-start.6 = (bf16[2,48,256]{2,1,0:T(8,128)(2,1)S(1)}, bf16[2,48,256]{2,1,0:T(8,128)(2,1)S(1)}, u32[]{:S(2)}, u32[]{:S(2)}) collective-permute-start(bf16[2,48,256]{2,1,0:T(8,128)(2,1)S(1)} %maximum_select_fusion.8), channel_id=1, source_target_pairs={{0,32},{8,40},{16,48},{24,56},{32,0},{40,8},{48,16},{56,24},{64,96... | collective-permute-start | bytes 147464 | tf_op jit(solution)/shard_map/ppermute | solution.py:32
  51.7 5.4 %collective-permute-start.16 = (bf16[2,48,256]{2,1,0:T(8,128)(2,1)S(1)}, bf16[2,48,256]{2,1,0:T(8,128)(2,1)S(1)}, u32[]{:S(2)}, u32[]{:S(2)}) collective-permute-start(bf16[2,48,256]{2,1,0:T(8,128)(2,1)S(1)} %maximum_select_fusion.9), channel_id=1, source_target_pairs={{0,32},{8,40},{16,48},{24,56},{32,0},{40,8},{48,16},{56,24},{64,96... | collective-permute-start | bytes 147464 | tf_op jit(solution)/shard_map/ppermute | solution.py:32
  53.6 6.2 %collective-permute-start.7 = (bf16[4,48,256]{2,1,0:T(8,128)(2,1)S(1)}, bf16[4,48,256]{2,1,0:T(8,128)(2,1)S(1)}, u32[]{:S(2)}, u32[]{:S(2)}) collective-permute-start(bf16[4,48,256]{2,1,0:T(8,128)(2,1)S(1)} %maximum_select_fusion.6), channel_id=1, source_target_pairs={{0,128},{8,136},{16,144},{24,152},{32,160},{40,168},{48,176},{56,1... | collective-permute-start | bytes 294920 | tf_op jit(solution)/shard_map/ppermute | solution.py:32
  57.1 4.7 %collective-permute-start.17 = (bf16[4,48,256]{2,1,0:T(8,128)(2,1)S(1)}, bf16[4,48,256]{2,1,0:T(8,128)(2,1)S(1)}, u32[]{:S(2)}, u32[]{:S(2)}) collective-permute-start(bf16[4,48,256]{2,1,0:T(8,128)(2,1)S(1)} %maximum_select_fusion.7), channel_id=1, source_target_pairs={{0,16},{8,24},{16,0},{24,8},{32,48},{40,56},{48,32},{56,40},{64,80... | collective-permute-start | bytes 294920 | tf_op jit(solution)/shard_map/ppermute | solution.py:32
  59.8 5.8 %collective-permute-start.8 = (bf16[8,48,256]{2,1,0:T(8,128)(2,1)S(1)}, bf16[8,48,256]{2,1,0:T(8,128)(2,1)S(1)}, u32[]{:S(2)}, u32[]{:S(2)}) collective-permute-start(bf16[8,48,256]{2,1,0:T(8,128)(2,1)S(1)} %maximum_select_fusion.4), channel_id=1, source_target_pairs={{0,16},{8,24},{16,0},{24,8},{32,48},{40,56},{48,32},{56,40},{64,80... | collective-permute-start | bytes 589832 | tf_op jit(solution)/shard_map/ppermute | solution.py:32
  61.9 7.3 %collective-permute-start.18 = (bf16[8,48,256]{2,1,0:T(8,128)(2,1)S(1)}, bf16[8,48,256]{2,1,0:T(8,128)(2,1)S(1)}, u32[]{:S(2)}, u32[]{:S(2)}) collective-permute-start(bf16[8,48,256]{2,1,0:T(8,128)(2,1)S(1)} %maximum_select_fusion.5), channel_id=1, source_target_pairs={{0,128},{8,136},{16,144},{24,152},{32,160},{40,168},{48,176},{56,1... | collective-permute-start | bytes 589832 | tf_op jit(solution)/shard_map/ppermute | solution.py:32
  65.6 4.8 %collective-permute-start.9 = (bf16[16,48,256]{2,1,0:T(8,128)(2,1)S(1)}, bf16[16,48,256]{2,1,0:T(8,128)(2,1)S(1)}, u32[]{:S(2)}, u32[]{:S(2)}) collective-permute-start(bf16[16,48,256]{2,1,0:T(8,128)(2,1)S(1)} %maximum_select_fusion.2), channel_id=1, source_target_pairs={{0,8},{8,0},{16,24},{24,16},{32,40},{40,32},{48,56},{56,48},{64,72... | collective-permute-start | bytes 1179656 | tf_op jit(solution)/shard_map/ppermute | solution.py:32
  87.8 7.0 %collective-permute-start.20 = (f32[48,2,2,256]{3,0,1,2:T(8,128)S(1)}, f32[48,2,2,256]{3,0,1,2:T(8,128)S(1)}, u32[]{:S(2)}, u32[]{:S(2)}) collective-permute-start(f32[48,2,2,256]{3,0,1,2:T(8,128)S(1)} %select_bitcast_fusion), channel_id=1, source_target_pairs={{0,1},{1,0},{2,3},{3,2},{4,5},{5,4},{6,7},{7,6},{8,9},{9,8},{10,11... | collective-permute-start | bytes 589832 | tf_op jit(solution)/shard_map/ppermute | solution.py:52
  89.2 7.3 %collective-permute-start.23 = (f32[48,2,2,256]{3,2,1,0:T(2,128)S(1)}, f32[48,2,2,256]{3,2,1,0:T(2,128)S(1)}, u32[]{:S(2)}, u32[]{:S(2)}) collective-permute-start(f32[48,2,2,256]{3,2,1,0:T(2,128)S(1)} %fusion.4), channel_id=1, source_target_pairs={{0,2},{1,3},{2,0},{3,1},{4,6},{5,7},{6,4},{7,5},{8,10},{9,11},{10,... | collective-permute-start | bytes 589832 | tf_op jit(solution)/shard_map/ppermute | solution.py:52
  94.9 4.7 %collective-permute-start.21 = (f32[48,2,256]{2,0,1:T(8,128)S(1)}, f32[48,2,256]{2,0,1:T(8,128)S(1)}, u32[]{:S(2)}, u32[]{:S(2)}) collective-permute-start(f32[48,2,256]{2,0,1:T(8,128)S(1)} %select_bitcast_fusion.1), channel_id=1, source_target_pairs={{0,2},{1,3},{2,0},{3,1},{4,6},{5,7},{6,4},{7,5},{8,10},{9,11},{10,... | collective-permute-start | bytes 294920 | tf_op jit(solution)/shard_map/ppermute | solution.py:52
  96.9 5.9 %collective-permute-start.24 = (f32[48,2,256]{2,1,0:T(2,128)S(1)}, f32[48,2,256]{2,1,0:T(2,128)S(1)}, u32[]{:S(2)}, u32[]{:S(2)}) collective-permute-start(f32[48,2,256]{2,1,0:T(2,128)S(1)} %bitcast.66), channel_id=1, source_target_pairs={{0,1},{1,0},{2,3},{3,2},{4,5},{5,4},{6,7},{7,6},{8,9},{9,8},{10,11... | collective-permute-start | bytes 294920 | tf_op jit(solution)/shard_map/ppermute | solution.py:52
  99.6 6.0 %collective-permute-start.22 = (f32[48,256]{1,0:T(8,128)S(1)}, f32[48,256]{1,0:T(8,128)S(1)}, u32[]{:S(2)}, u32[]{:S(2)}) collective-permute-start(f32[48,256]{1,0:T(8,128)S(1)} %select_bitcast_fusion.2), channel_id=1, source_target_pairs={{0,4},{1,5},{2,6},{3,7},{4,0},{5,1},{6,2},{7,3},{8,12},{9,13},{10,... | collective-permute-start | bytes 147464 | tf_op jit(solution)/shard_map/ppermute | solution.py:52
  103.0 5.7 %collective-permute-start.25 = (f32[48,256]{1,0:T(8,128)S(1)}, f32[48,256]{1,0:T(8,128)S(1)}, u32[]{:S(2)}, u32[]{:S(2)}) collective-permute-start(f32[48,256]{1,0:T(8,128)S(1)} %bitcast.67), channel_id=1, source_target_pairs={{0,4},{1,5},{2,6},{3,7},{4,0},{5,1},{6,2},{7,3},{8,12},{9,13},{10,... | collective-permute-start | bytes 147464 | tf_op jit(solution)/shard_map/ppermute | solution.py:52
  (3 other events, 37.3 us)

commit v3 on v2

v3 whole, which is shorter than its diff:
```python
import math

import jax
import jax.numpy as jnp
from jax import lax
from jax.experimental import pallas as pl
from jax.experimental.pallas import tpu as pltpu
from jax.sharding import PartitionSpec as P

LAGS = 64
EDGE = 128
TIME_BLOCK = 2048
CHAN_BITS = ((0, 1, 4, 2, 3), (0, 4, 1, 2, 3))

def xor_pairs(size, bit):
    return [(i, i ^ (1 << bit)) for i in range(size)]


def broadcast(masked, me, axis, size, order):
    pieces = masked
    for bit in order:
        half = pieces.shape[0] // 2
        low, high = pieces[:half], pieces[half:]
        mine = ((me >> bit) & 1) == 0
        send = jnp.where(mine, high, low)
        keep = jnp.where(mine, low, high)
        pieces = keep + lax.ppermute(send, axis, xor_pairs(size, bit))
    for bit in reversed(order):
        mine = ((me >> bit) & 1) == 0
        got = lax.ppermute(pieces, axis, xor_pairs(size, bit))
        pieces = jnp.where(
            mine, jnp.concatenate([pieces, got], 0), jnp.concatenate([got, pieces], 0)
        )
    return pieces


def correlate(halves, whitened, factor, blocks):
    piece_count, rows_half, piece_width = halves[0].shape
    rows = rows_half * len(halves)
    chan_dev, samples = whitened.shape
    per_block = TIME_BLOCK // piece_width
    width = TIME_BLOCK + 2 * EDGE
    out_width = LAGS * chan_dev // blocks

    def kernel(factor_ref, *refs):
        src_refs, w_ref, out_ref, pad_ref = refs[: len(halves)], refs[len(halves)], refs[-2], refs[-1]
        pad_ref[:, :EDGE] = jnp.zeros((chan_dev, EDGE), pad_ref.dtype)
        pad_ref[:, EDGE + samples :] = jnp.zeros((chan_dev, EDGE), pad_ref.dtype)
        pad_ref[:, EDGE : EDGE + samples] = w_ref[...]

        def block(k, acc):
            base = pl.multiple_of(k * TIME_BLOCK, TIME_BLOCK)
            window = pad_ref[:, pl.ds(base, width)]
            parts = [
                pltpu.roll(window, width - (EDGE - LAGS // 2 + lag), 1)[:, :TIME_BLOCK]
                for lag in range(LAGS)
            ]
            stacked = jnp.concatenate(parts, 0)
            first = pl.multiple_of(k * per_block, per_block)
            chunk = jnp.concatenate(
                [
                    jnp.concatenate([src_ref[first + j] for j in range(per_block)], 1)
                    for src_ref in src_refs
                ],
                0,
            )
            return acc + lax.dot_general(
                stacked, chunk, (((1,), (1,)), ((), ())), preferred_element_type=jnp.float32
            )

        acc = lax.fori_loop(
            0, samples // TIME_BLOCK, block, jnp.zeros((LAGS * chan_dev, rows), jnp.float32)
        )
        result = acc.T * factor_ref[0, 0]
        for j in range(blocks):
            out_ref[j] = result[:, j * out_width : (j + 1) * out_width]

    return pl.pallas_call(
        kernel,
        out_shape=jax.ShapeDtypeStruct((blocks, rows, out_width), jnp.float32),
        in_specs=[pl.BlockSpec(memory_space=pltpu.SMEM)]
        + [pl.BlockSpec(memory_space=pltpu.VMEM) for _ in range(len(halves) + 1)],
        out_specs=pl.BlockSpec(memory_space=pltpu.VMEM),
        scratch_shapes=[pltpu.VMEM((chan_dev, samples + 2 * EDGE), whitened.dtype)],
    )(factor.reshape(1, 1), *halves, whitened)


def body(traces, owner, window_mask):
    chan_dev = traces.shape[1]
    samples = traces.shape[2]
    step_count = owner.shape[0]
    chan_size = lax.axis_size("chan")
    win_size = lax.axis_size("win")
    chan_me = lax.axis_index("chan")
    win_me = lax.axis_index("win")
    signal = traces[0].astype(jnp.float32)
    whitened = (
        signal * lax.rsqrt(jnp.mean(signal * signal, axis=-1, keepdims=True) + 1e-06)
    ).astype(jnp.bfloat16)
    own_flag = window_mask[0, 0].astype(jnp.float32)
    outgoing = whitened * own_flag.astype(jnp.bfloat16)
    masked = jnp.concatenate(
        [jnp.where(chan_me == owner[step], outgoing, jnp.zeros_like(outgoing)) for step in range(step_count)],
        0,
    )
    rows = masked.shape[0]
    masked = masked.reshape(rows, chan_size, samples // chan_size).transpose(1, 0, 2)
    half = rows // 2
    halves = [
        broadcast(masked[:, which * half : (which + 1) * half], chan_me, "chan", chan_size, order)
        for which, order in enumerate(CHAN_BITS)
    ]
    factor = own_flag / math.sqrt(samples)
    complete = correlate(halves, whitened, factor, win_size)
    reduced = jnp.sum(lax.all_to_all(complete, "win", 0, 0, tiled=True), 0)
    per_dev = LAGS // win_size
    return reduced.reshape(step_count, chan_dev, per_dev, chan_dev)


def solution(mesh):
    return jax.shard_map(
        body,
        mesh=mesh,
        in_specs=(P("win", "chan", None), P(), P("win", "chan")),
        out_specs=P(None, None, "win", "chan"),
        check_vma=False,
    )
```

time: 110 us -> 113 us (1.027)
  blocking collectives: 0 us -> 18.1 us
  starting transfers between devices: 52.1 us -> 44.1 us
  waiting for transfers between devices: 29.2 us -> 24.8 us
  local copies, waits for them, and re-layouts: 5.54 us -> 3.51 us
    all_to_all x0 -> x1, blocking collectives: none -> 18.1 us  [body(): reduced = jnp.sum(lax.all_to_all(complete, 'win', 0, 0, tiled=True), 0)]
    ppermute x6 -> x0, starting transfers between devices: 9.91 us -> none  [scatter_lags(): parts = keep + lax.ppermute(send, axis, xor_pairs(size, bit))]
    ppermute x6 -> x0, waiting for transfers between devices: 9.76 us -> none  [scatter_lags(): parts = keep + lax.ppermute(send, axis, xor_pairs(size, bit))]
    ppermute x10, waiting for transfers between devices: 7.82 us -> 15.3 us  [broadcast(): pieces = keep + lax.ppermute(send, axis, xor_pairs(size, bit))]
    ppermute x10, starting transfers between devices: 22.7 us -> 25.4 us  [broadcast(): pieces = keep + lax.ppermute(send, axis, xor_pairs(size, bit))]
    ppermute x10, waiting for transfers between devices: 11.6 us -> 9.45 us  [broadcast(): got = lax.ppermute(pieces, axis, xor_pairs(size, bit))]
    select_n x10, other arithmetic: 0.4 us -> 2.2 us  [broadcast(): jnp.where(mine, jnp.concatenate([pieces, got], 0), jnp.concatenate([got,...]
    concatenate x2 -> x0, other arithmetic: 1.4 us -> none  [the longest x1 1.39 us: body(): jnp.concatenate([broadcast(masked[:, which * half:(which + 1) * half], ch...]
  transfers between devices with their start and end apart: 26 -> 20, of which waited for: 18 -> 12; matrix products, arithmetic and copies ran while one was open for 3% -> 2% of each run, Pallas kernels for 0% -> 0%
where the time goes in v3:
time: 113 us; the launch traced here: 112 us
  starting transfers between devices  44.1 us (39%)
  waiting for transfers between devices  24.8 us (22%)
  blocking collectives  18.1 us (16%)
  Pallas kernels  13.3 us (12%)
  other arithmetic  5.72 us (5%)
  local copies, waits for them, and re-layouts  3.51 us (3%)
  between operations  2.81 us (2%)
    ppermute x10, starting transfers between devices, broadcast(): pieces = keep + lax.ppermute(send, axis, xor_pairs(size, bit))  25.4 us
    ppermute x10, starting transfers between devices, broadcast(): got = lax.ppermute(pieces, axis, xor_pairs(size, bit))  18.7 us
    all_to_all x1, blocking collectives, body(): reduced = jnp.sum(lax.all_to_all(complete, 'win', 0, 0, tiled=True), 0)  18.1 us
    ppermute x10, waiting for transfers between devices, broadcast(): pieces = keep + lax.ppermute(send, axis, xor_pairs(size, bit))  15.3 us
    pallas_call x1, Pallas kernels, correlate(): pl.pallas_call(kernel, out_shape=jax.ShapeDtypeStruct((blocks, rows, out_...  13.3 us
    ppermute x10, waiting for transfers between devices, broadcast(): got = lax.ppermute(pieces, axis, xor_pairs(size, bit))  9.45 us
  transfers between devices with their start and end apart: 20, of which 12 were waited for; matrix products, arithmetic and copies ran while one was open for 2% of the time, Pallas kernels for 0%

profile of v3, /device:TPU:8, one launch (start us, length us, event | category | flops | bytes accessed | tf_op | source)
XLA Modules:
  0.0 112.3 jit_solution(16529514678908459619)
XLA Ops:
  7.4 1.7 %collective-permute-done.10 = bf16[16,48,256]{2,1,0:T(8,128)(2,1)S(1)} collective-permute-done((bf16[16,48,256]{2,1,0:T(8,128)(2,1)S(1)}, bf16[16,48,256]{2,1,0:T(8,128)(2,1)S(1)}, u32[]{:S(2)}, u32[]{:S(2)}) %collective-permute-start.10) | collective-permute-done | bytes 393248 | tf_op jit(solution)/shard_map/ppermute | solution.py:27
  9.3 2.4 %collective-permute-start.11 = (bf16[8,48,256]{2,1,0:T(8,128)(2,1)S(1)}, bf16[8,48,256]{2,1,0:T(8,128)(2,1)S(1)}, u32[]{:S(2)}, u32[]{:S(2)}) collective-permute-start(bf16[8,48,256]{2,1,0:T(8,128)(2,1)S(1)} %broadcast_select_fusion.6), channel_id=1, source_target_pairs={{0,128},{8,136},{16,144},{24,152},{32,160},{40,168},{48,176},{56,1... | collective-permute-start | bytes 589832 | tf_op jit(solution)/shard_map/ppermute | solution.py:27
  11.7 6.1 %collective-permute-done.11 = bf16[8,48,256]{2,1,0:T(8,128)(2,1)S(1)} collective-permute-done((bf16[8,48,256]{2,1,0:T(8,128)(2,1)S(1)}, bf16[8,48,256]{2,1,0:T(8,128)(2,1)S(1)}, u32[]{:S(2)}, u32[]{:S(2)}) %collective-permute-start.11) | collective-permute-done | bytes 196640 | tf_op jit(solution)/shard_map/ppermute | solution.py:27
  17.9 2.0 %collective-permute-start.12 = (bf16[4,48,256]{2,1,0:T(8,128)(2,1)S(1)}, bf16[4,48,256]{2,1,0:T(8,128)(2,1)S(1)}, u32[]{:S(2)}, u32[]{:S(2)}) collective-permute-start(bf16[4,48,256]{2,1,0:T(8,128)(2,1)S(1)} %broadcast_select_fusion.7), channel_id=1, source_target_pairs={{0,16},{8,24},{16,0},{24,8},{32,48},{40,56},{48,32},{56,40},{64,80... | collective-permute-start | bytes 294920 | tf_op jit(solution)/shard_map/ppermute | solution.py:27
  19.9 2.7 %collective-permute-done.12 = bf16[4,48,256]{2,1,0:T(8,128)(2,1)S(1)} collective-permute-done((bf16[4,48,256]{2,1,0:T(8,128)(2,1)S(1)}, bf16[4,48,256]{2,1,0:T(8,128)(2,1)S(1)}, u32[]{:S(2)}, u32[]{:S(2)}) %collective-permute-start.12) | collective-permute-done | bytes 98336 | tf_op jit(solution)/shard_map/ppermute | solution.py:27
  22.7 2.0 %collective-permute-start.1 = (bf16[8,48,256]{2,1,0:T(8,128)(2,1)S(1)}, bf16[8,48,256]{2,1,0:T(8,128)(2,1)S(1)}, u32[]{:S(2)}, u32[]{:S(2)}) collective-permute-start(bf16[8,48,256]{2,1,0:T(8,128)(2,1)S(1)} %broadcast_select_fusion.5), channel_id=1, source_target_pairs={{0,16},{8,24},{16,0},{24,8},{32,48},{40,56},{48,32},{56,40},{64,80... | collective-permute-start | bytes 589832 | tf_op jit(solution)/shard_map/ppermute | solution.py:27
  24.7 3.4 %collective-permute-start.13 = (bf16[2,48,256]{2,1,0:T(8,128)(2,1)S(1)}, bf16[2,48,256]{2,1,0:T(8,128)(2,1)S(1)}, u32[]{:S(2)}, u32[]{:S(2)}) collective-permute-start(bf16[2,48,256]{2,1,0:T(8,128)(2,1)S(1)} %broadcast_select_fusion.9), channel_id=1, source_target_pairs={{0,32},{8,40},{16,48},{24,56},{32,0},{40,8},{48,16},{56,24},{64,96... | collective-permute-start | bytes 147464 | tf_op jit(solution)/shard_map/ppermute | solution.py:27
  29.0 2.4 %collective-permute-start.2 = (bf16[4,48,256]{2,1,0:T(8,128)(2,1)S(1)}, bf16[4,48,256]{2,1,0:T(8,128)(2,1)S(1)}, u32[]{:S(2)}, u32[]{:S(2)}) collective-permute-start(bf16[4,48,256]{2,1,0:T(8,128)(2,1)S(1)} %broadcast_select_fusion.8), channel_id=1, source_target_pairs={{0,128},{8,136},{16,144},{24,152},{32,160},{40,168},{48,176},{56,1... | collective-permute-start | bytes 294920 | tf_op jit(solution)/shard_map/ppermute | solution.py:27
  31.4 3.8 %collective-permute-done.2 = bf16[4,48,256]{2,1,0:T(8,128)(2,1)S(1)} collective-permute-done((bf16[4,48,256]{2,1,0:T(8,128)(2,1)S(1)}, bf16[4,48,256]{2,1,0:T(8,128)(2,1)S(1)}, u32[]{:S(2)}, u32[]{:S(2)}) %collective-permute-start.2) | collective-permute-done | bytes 98336 | tf_op jit(solution)/shard_map/ppermute | solution.py:27
  35.3 2.8 %collective-permute-start.3 = (bf16[2,48,256]{2,1,0:T(8,128)(2,1)S(1)}, bf16[2,48,256]{2,1,0:T(8,128)(2,1)S(1)}, u32[]{:S(2)}, u32[]{:S(2)}) collective-permute-start(bf16[2,48,256]{2,1,0:T(8,128)(2,1)S(1)} %broadcast_select_fusion.10), channel_id=1, source_target_pairs={{0,32},{8,40},{16,48},{24,56},{32,0},{40,8},{48,16},{56,24},{64,96... | collective-permute-start | bytes 147464 | tf_op jit(solution)/shard_map/ppermute | solution.py:27
  38.1 5.4 %collective-permute-start.14 = (bf16[1,48,256]{2,1,0:T(8,128)(2,1)S(1)}, bf16[1,48,256]{2,1,0:T(8,128)(2,1)S(1)}, u32[]{:S(2)}, u32[]{:S(2)}) collective-permute-start(bf16[1,48,256]{2,1,0:T(8,128)(2,1)S(1)} %broadcast_select_fusion.11), channel_id=1, source_target_pairs={{0,64},{8,72},{16,80},{24,88},{32,96},{40,104},{48,112},{56,120},{... | collective-permute-start | bytes 73736 | tf_op jit(solution)/shard_map/ppermute | solution.py:27
  43.6 5.0 %collective-permute-start.4 = (bf16[1,48,256]{2,1,0:T(8,128)(2,1)S(1)}, bf16[1,48,256]{2,1,0:T(8,128)(2,1)S(1)}, u32[]{:S(2)}, u32[]{:S(2)}) collective-permute-start(bf16[1,48,256]{2,1,0:T(8,128)(2,1)S(1)} %broadcast_select_fusion.12), channel_id=1, source_target_pairs={{0,64},{8,72},{16,80},{24,88},{32,96},{40,104},{48,112},{56,120},{... | collective-permute-start | bytes 73736 | tf_op jit(solution)/shard_map/ppermute | solution.py:27
  48.5 2.8 %collective-permute-start.15 = (bf16[1,48,256]{2,1,0:T(8,128)(2,1)S(1)}, bf16[1,48,256]{2,1,0:T(8,128)(2,1)S(1)}, u32[]{:S(2)}, u32[]{:S(2)}) collective-permute-start(bf16[1,48,256]{2,1,0:T(8,128)(2,1)S(1)} %select_add_fusion.8), channel_id=1, source_target_pairs={{0,64},{8,72},{16,80},{24,88},{32,96},{40,104},{48,112},{56,120},{... | collective-permute-start | bytes 73736 | tf_op jit(solution)/shard_map/ppermute | solution.py:30
  51.4 5.0 %collective-permute-start.5 = (bf16[1,48,256]{2,1,0:T(8,128)(2,1)S(1)}, bf16[1,48,256]{2,1,0:T(8,128)(2,1)S(1)}, u32[]{:S(2)}, u32[]{:S(2)}) collective-permute-start(bf16[1,48,256]{2,1,0:T(8,128)(2,1)S(1)} %select_add_fusion.9), channel_id=1, source_target_pairs={{0,64},{8,72},{16,80},{24,88},{32,96},{40,104},{48,112},{56,120},{... | collective-permute-start | bytes 73736 | tf_op jit(solution)/shard_map/ppermute | solution.py:30
  56.7 2.5 %collective-permute-done.5 = bf16[1,48,256]{2,1,0:T(8,128)(2,1)S(1)} collective-permute-done((bf16[1,48,256]{2,1,0:T(8,128)(2,1)S(1)}, bf16[1,48,256]{2,1,0:T(8,128)(2,1)S(1)}, u32[]{:S(2)}, u32[]{:S(2)}) %collective-permute-start.5) | collective-permute-done | bytes 24608 | tf_op jit(solution)/shard_map/ppermute | solution.py:30
  59.2 2.7 %collective-permute-start.6 = (bf16[2,48,256]{2,1,0:T(8,128)(2,1)S(1)}, bf16[2,48,256]{2,1,0:T(8,128)(2,1)S(1)}, u32[]{:S(2)}, u32[]{:S(2)}) collective-permute-start(bf16[2,48,256]{2,1,0:T(8,128)(2,1)S(1)} %maximum_select_fusion.8), channel_id=1, source_target_pairs={{0,32},{8,40},{16,48},{24,56},{32,0},{40,8},{48,16},{56,24},{64,96... | collective-permute-start | bytes 147464 | tf_op jit(solution)/shard_map/ppermute | solution.py:30
  62.3 2.1 %collective-permute-done.6 = bf16[2,48,256]{2,1,0:T(8,128)(2,1)S(1)} collective-permute-done((bf16[2,48,256]{2,1,0:T(8,128)(2,1)S(1)}, bf16[2,48,256]{2,1,0:T(8,128)(2,1)S(1)}, u32[]{:S(2)}, u32[]{:S(2)}) %collective-permute-start.6) | collective-permute-done | bytes 49184 | tf_op jit(solution)/shard_map/ppermute | solution.py:30
  64.3 2.4 %collective-permute-start.7 = (bf16[4,48,256]{2,1,0:T(8,128)(2,1)S(1)}, bf16[4,48,256]{2,1,0:T(8,128)(2,1)S(1)}, u32[]{:S(2)}, u32[]{:S(2)}) collective-permute-start(bf16[4,48,256]{2,1,0:T(8,128)(2,1)S(1)} %maximum_select_fusion.6), channel_id=1, source_target_pairs={{0,128},{8,136},{16,144},{24,152},{32,160},{40,168},{48,176},{56,1... | collective-permute-start | bytes 294920 | tf_op jit(solution)/shard_map/ppermute | solution.py:30
  67.8 2.3 %collective-permute-start.18 = (bf16[8,48,256]{2,1,0:T(8,128)(2,1)S(1)}, bf16[8,48,256]{2,1,0:T(8,128)(2,1)S(1)}, u32[]{:S(2)}, u32[]{:S(2)}) collective-permute-start(bf16[8,48,256]{2,1,0:T(8,128)(2,1)S(1)} %maximum_select_fusion.5), channel_id=1, source_target_pairs={{0,128},{8,136},{16,144},{24,152},{32,160},{40,168},{48,176},{56,1... | collective-permute-start | bytes 589832 | tf_op jit(solution)/shard_map/ppermute | solution.py:30
  70.6 2.6 %collective-permute-start.8 = (bf16[8,48,256]{2,1,0:T(8,128)(2,1)S(1)}, bf16[8,48,256]{2,1,0:T(8,128)(2,1)S(1)}, u32[]{:S(2)}, u32[]{:S(2)}) collective-permute-start(bf16[8,48,256]{2,1,0:T(8,128)(2,1)S(1)} %maximum_select_fusion.4), channel_id=1, source_target_pairs={{0,16},{8,24},{16,0},{24,8},{32,48},{40,56},{48,32},{56,40},{64,80... | collective-permute-start | bytes 589832 | tf_op jit(solution)/shard_map/ppermute | solution.py:30
  73.2 1.9 %collective-permute-done.18 = bf16[8,48,256]{2,1,0:T(8,128)(2,1)S(1)} collective-permute-done((bf16[8,48,256]{2,1,0:T(8,128)(2,1)S(1)}, bf16[8,48,256]{2,1,0:T(8,128)(2,1)S(1)}, u32[]{:S(2)}, u32[]{:S(2)}) %collective-permute-start.18) | collective-permute-done | bytes 196640 | tf_op jit(solution)/shard_map/ppermute | solution.py:30
  75.4 1.5 %collective-permute-done.8 = bf16[8,48,256]{2,1,0:T(8,128)(2,1)S(1)} collective-permute-done((bf16[8,48,256]{2,1,0:T(8,128)(2,1)S(1)}, bf16[8,48,256]{2,1,0:T(8,128)(2,1)S(1)}, u32[]{:S(2)}, u32[]{:S(2)}) %collective-permute-start.8) | collective-permute-done | bytes 196640 | tf_op jit(solution)/shard_map/ppermute | solution.py:30
  80.0 13.3 %shard_map.37 = f32[8,96,256]{2,1,0:T(8,128)} custom-call(f32[1,1]{1,0:T(1,128)S(6)} %div.9.factor_ref, bf16[32,48,256]{2,1,0:T(8,128)(2,1)} %maximum_select_fusion.refs_0_, bf16[32,48,256]{2,1,0:T(8,128)(2,1)} %maximum_select_fusion.1.refs_1_, bf16[32,8192]{1,0:T(8,128)(2,1)} %fusion.1.refs_2_), custom_call_target="tpu_custom_call" | custom-call | tf_op jit(solution)/shard_map/pallas_call | solution.py:78
  93.3 18.1 %all_to_all.5 = f32[8,96,256]{2,1,0:T(8,128)S(1)} all-to-all(f32[8,96,256]{2,1,0:T(8,128)} %shard_map.37), channel_id=1, replica_groups=mesh['chan'=32,'win'=8] {'win'}, dimensions={0} | all-to-all | bytes 1572864 | tf_op jit(solution)/shard_map/all_to_all | solution.py:115
  (59 shorter events, 12.8 us)
Async XLA Ops:
  7.3 1.8 %collective-permute-start.10 = (bf16[16,48,256]{2,1,0:T(8,128)(2,1)S(1)}, bf16[16,48,256]{2,1,0:T(8,128)(2,1)S(1)}, u32[]{:S(2)}, u32[]{:S(2)}) collective-permute-start(bf16[16,48,256]{2,1,0:T(8,128)(2,1)S(1)} %broadcast_select_fusion.3), channel_id=1, source_target_pairs={{0,8},{8,0},{16,24},{24,16},{32,40},{40,32},{48,56},{56,48},{64,72... | collective-permute-start | bytes 1179656 | tf_op jit(solution)/shard_map/ppermute | solution.py:27
  9.3 8.5 %collective-permute-start.11 = (bf16[8,48,256]{2,1,0:T(8,128)(2,1)S(1)}, bf16[8,48,256]{2,1,0:T(8,128)(2,1)S(1)}, u32[]{:S(2)}, u32[]{:S(2)}) collective-permute-start(bf16[8,48,256]{2,1,0:T(8,128)(2,1)S(1)} %broadcast_select_fusion.6), channel_id=1, source_target_pairs={{0,128},{8,136},{16,144},{24,152},{32,160},{40,168},{48,176},{56,1... | collective-permute-start | bytes 589832 | tf_op jit(solution)/shard_map/ppermute | solution.py:27
  11.7 10.9 %collective-permute-start = (bf16[16,48,256]{2,1,0:T(8,128)(2,1)S(1)}, bf16[16,48,256]{2,1,0:T(8,128)(2,1)S(1)}, u32[]{:S(2)}, u32[]{:S(2)}) collective-permute-start(bf16[16,48,256]{2,1,0:T(8,128)(2,1)S(1)} %get-tuple-element.8), channel_id=1, source_target_pairs={{0,8},{8,0},{16,24},{24,16},{32,40},{40,32},{48,56},{56,48},{64,72... | collective-permute-start | bytes 1179656 | tf_op jit(solution)/shard_map/ppermute | solution.py:27
  17.9 4.7 %collective-permute-start.12 = (bf16[4,48,256]{2,1,0:T(8,128)(2,1)S(1)}, bf16[4,48,256]{2,1,0:T(8,128)(2,1)S(1)}, u32[]{:S(2)}, u32[]{:S(2)}) collective-permute-start(bf16[4,48,256]{2,1,0:T(8,128)(2,1)S(1)} %broadcast_select_fusion.7), channel_id=1, source_target_pairs={{0,16},{8,24},{16,0},{24,8},{32,48},{40,56},{48,32},{56,40},{64,80... | collective-permute-start | bytes 294920 | tf_op jit(solution)/shard_map/ppermute | solution.py:27
  22.7 6.3 %collective-permute-start.1 = (bf16[8,48,256]{2,1,0:T(8,128)(2,1)S(1)}, bf16[8,48,256]{2,1,0:T(8,128)(2,1)S(1)}, u32[]{:S(2)}, u32[]{:S(2)}) collective-permute-start(bf16[8,48,256]{2,1,0:T(8,128)(2,1)S(1)} %broadcast_select_fusion.5), channel_id=1, source_target_pairs={{0,16},{8,24},{16,0},{24,8},{32,48},{40,56},{48,32},{56,40},{64,80... | collective-permute-start | bytes 589832 | tf_op jit(solution)/shard_map/ppermute | solution.py:27
  24.7 6.7 %collective-permute-start.13 = (bf16[2,48,256]{2,1,0:T(8,128)(2,1)S(1)}, bf16[2,48,256]{2,1,0:T(8,128)(2,1)S(1)}, u32[]{:S(2)}, u32[]{:S(2)}) collective-permute-start(bf16[2,48,256]{2,1,0:T(8,128)(2,1)S(1)} %broadcast_select_fusion.9), channel_id=1, source_target_pairs={{0,32},{8,40},{16,48},{24,56},{32,0},{40,8},{48,16},{56,24},{64,96... | collective-permute-start | bytes 147464 | tf_op jit(solution)/shard_map/ppermute | solution.py:27
  29.0 6.2 %collective-permute-start.2 = (bf16[4,48,256]{2,1,0:T(8,128)(2,1)S(1)}, bf16[4,48,256]{2,1,0:T(8,128)(2,1)S(1)}, u32[]{:S(2)}, u32[]{:S(2)}) collective-permute-start(bf16[4,48,256]{2,1,0:T(8,128)(2,1)S(1)} %broadcast_select_fusion.8), channel_id=1, source_target_pairs={{0,128},{8,136},{16,144},{24,152},{32,160},{40,168},{48,176},{56,1... | collective-permute-start | bytes 294920 | tf_op jit(solution)/shard_map/ppermute | solution.py:27
  35.3 8.2 %collective-permute-start.3 = (bf16[2,48,256]{2,1,0:T(8,128)(2,1)S(1)}, bf16[2,48,256]{2,1,0:T(8,128)(2,1)S(1)}, u32[]{:S(2)}, u32[]{:S(2)}) collective-permute-start(bf16[2,48,256]{2,1,0:T(8,128)(2,1)S(1)} %broadcast_select_fusion.10), channel_id=1, source_target_pairs={{0,32},{8,40},{16,48},{24,56},{32,0},{40,8},{48,16},{56,24},{64,96... | collective-permute-start | bytes 147464 | tf_op jit(solution)/shard_map/ppermute | solution.py:27
  38.1 10.4 %collective-permute-start.14 = (bf16[1,48,256]{2,1,0:T(8,128)(2,1)S(1)}, bf16[1,48,256]{2,1,0:T(8,128)(2,1)S(1)}, u32[]{:S(2)}, u32[]{:S(2)}) collective-permute-start(bf16[1,48,256]{2,1,0:T(8,128)(2,1)S(1)} %broadcast_select_fusion.11), channel_id=1, source_target_pairs={{0,64},{8,72},{16,80},{24,88},{32,96},{40,104},{48,112},{56,120},{... | collective-permute-start | bytes 73736 | tf_op jit(solution)/shard_map/ppermute | solution.py:27
  43.6 33.4 %copy-start = (bf16[1,32,8192]{2,1,0:T(8,128)(2,1)S(1)}, bf16[1,32,8192]{2,1,0:T(8,128)(2,1)}, u32[]{:S(2)}) copy-start(bf16[1,32,8192]{2,1,0:T(8,128)(2,1)} %param.3) | copy-start | bytes 1572868
  43.6 7.8 %collective-permute-start.4 = (bf16[1,48,256]{2,1,0:T(8,128)(2,1)S(1)}, bf16[1,48,256]{2,1,0:T(8,128)(2,1)S(1)}, u32[]{:S(2)}, u32[]{:S(2)}) collective-permute-start(bf16[1,48,256]{2,1,0:T(8,128)(2,1)S(1)} %broadcast_select_fusion.12), channel_id=1, source_target_pairs={{0,64},{8,72},{16,80},{24,88},{32,96},{40,104},{48,112},{56,120},{... | collective-permute-start | bytes 73736 | tf_op jit(solution)/shard_map/ppermute | solution.py:27
  48.5 7.8 %collective-permute-start.15 = (bf16[1,48,256]{2,1,0:T(8,128)(2,1)S(1)}, bf16[1,48,256]{2,1,0:T(8,128)(2,1)S(1)}, u32[]{:S(2)}, u32[]{:S(2)}) collective-permute-start(bf16[1,48,256]{2,1,0:T(8,128)(2,1)S(1)} %select_add_fusion.8), channel_id=1, source_target_pairs={{0,64},{8,72},{16,80},{24,88},{32,96},{40,104},{48,112},{56,120},{... | collective-permute-start | bytes 73736 | tf_op jit(solution)/shard_map/ppermute | solution.py:30
  51.4 7.8 %collective-permute-start.5 = (bf16[1,48,256]{2,1,0:T(8,128)(2,1)S(1)}, bf16[1,48,256]{2,1,0:T(8,128)(2,1)S(1)}, u32[]{:S(2)}, u32[]{:S(2)}) collective-permute-start(bf16[1,48,256]{2,1,0:T(8,128)(2,1)S(1)} %select_add_fusion.9), channel_id=1, source_target_pairs={{0,64},{8,72},{16,80},{24,88},{32,96},{40,104},{48,112},{56,120},{... | collective-permute-start | bytes 73736 | tf_op jit(solution)/shard_map/ppermute | solution.py:30
  56.4 5.6 %collective-permute-start.16 = (bf16[2,48,256]{2,1,0:T(8,128)(2,1)S(1)}, bf16[2,48,256]{2,1,0:T(8,128)(2,1)S(1)}, u32[]{:S(2)}, u32[]{:S(2)}) collective-permute-start(bf16[2,48,256]{2,1,0:T(8,128)(2,1)S(1)} %maximum_select_fusion.9), channel_id=1, source_target_pairs={{0,32},{8,40},{16,48},{24,56},{32,0},{40,8},{48,16},{56,24},{64,96... | collective-permute-start | bytes 147464 | tf_op jit(solution)/shard_map/ppermute | solution.py:30
  59.2 5.1 %collective-permute-start.6 = (bf16[2,48,256]{2,1,0:T(8,128)(2,1)S(1)}, bf16[2,48,256]{2,1,0:T(8,128)(2,1)S(1)}, u32[]{:S(2)}, u32[]{:S(2)}) collective-permute-start(bf16[2,48,256]{2,1,0:T(8,128)(2,1)S(1)} %maximum_select_fusion.8), channel_id=1, source_target_pairs={{0,32},{8,40},{16,48},{24,56},{32,0},{40,8},{48,16},{56,24},{64,96... | collective-permute-start | bytes 147464 | tf_op jit(solution)/shard_map/ppermute | solution.py:30
  62.0 5.8 %collective-permute-start.17 = (bf16[4,48,256]{2,1,0:T(8,128)(2,1)S(1)}, bf16[4,48,256]{2,1,0:T(8,128)(2,1)S(1)}, u32[]{:S(2)}, u32[]{:S(2)}) collective-permute-start(bf16[4,48,256]{2,1,0:T(8,128)(2,1)S(1)} %maximum_select_fusion.7), channel_id=1, source_target_pairs={{0,16},{8,24},{16,0},{24,8},{32,48},{40,56},{48,32},{56,40},{64,80... | collective-permute-start | bytes 294920 | tf_op jit(solution)/shard_map/ppermute | solution.py:30
  64.3 6.2 %collective-permute-start.7 = (bf16[4,48,256]{2,1,0:T(8,128)(2,1)S(1)}, bf16[4,48,256]{2,1,0:T(8,128)(2,1)S(1)}, u32[]{:S(2)}, u32[]{:S(2)}) collective-permute-start(bf16[4,48,256]{2,1,0:T(8,128)(2,1)S(1)} %maximum_select_fusion.6), channel_id=1, source_target_pairs={{0,128},{8,136},{16,144},{24,152},{32,160},{40,168},{48,176},{56,1... | collective-permute-start | bytes 294920 | tf_op jit(solution)/shard_map/ppermute | solution.py:30
  67.8 7.3 %collective-permute-start.18 = (bf16[8,48,256]{2,1,0:T(8,128)(2,1)S(1)}, bf16[8,48,256]{2,1,0:T(8,128)(2,1)S(1)}, u32[]{:S(2)}, u32[]{:S(2)}) collective-permute-start(bf16[8,48,256]{2,1,0:T(8,128)(2,1)S(1)} %maximum_select_fusion.5), channel_id=1, source_target_pairs={{0,128},{8,136},{16,144},{24,152},{32,160},{40,168},{48,176},{56,1... | collective-permute-start | bytes 589832 | tf_op jit(solution)/shard_map/ppermute | solution.py:30
  70.6 6.3 %collective-permute-start.8 = (bf16[8,48,256]{2,1,0:T(8,128)(2,1)S(1)}, bf16[8,48,256]{2,1,0:T(8,128)(2,1)S(1)}, u32[]{:S(2)}, u32[]{:S(2)}) collective-permute-start(bf16[8,48,256]{2,1,0:T(8,128)(2,1)S(1)} %maximum_select_fusion.4), channel_id=1, source_target_pairs={{0,16},{8,24},{16,0},{24,8},{32,48},{40,56},{48,32},{56,40},{64,80... | collective-permute-start | bytes 589832 | tf_op jit(solution)/shard_map/ppermute | solution.py:30
  75.1 2.9 %collective-permute-start.19 = (bf16[16,48,256]{2,1,0:T(8,128)(2,1)S(1)}, bf16[16,48,256]{2,1,0:T(8,128)(2,1)S(1)}, u32[]{:S(2)}, u32[]{:S(2)}) collective-permute-start(bf16[16,48,256]{2,1,0:T(8,128)(2,1)S(1)} %maximum_select_fusion.3), channel_id=1, source_target_pairs={{0,8},{8,0},{16,24},{24,16},{32,40},{40,32},{48,56},{56,48},{64,72... | collective-permute-start | bytes 1179656 | tf_op jit(solution)/shard_map/ppermute | solution.py:30
  76.9 2.1 %collective-permute-start.9 = (bf16[16,48,256]{2,1,0:T(8,128)(2,1)S(1)}, bf16[16,48,256]{2,1,0:T(8,128)(2,1)S(1)}, u32[]{:S(2)}, u32[]{:S(2)}) collective-permute-start(bf16[16,48,256]{2,1,0:T(8,128)(2,1)S(1)} %maximum_select_fusion.2), channel_id=1, source_target_pairs={{0,8},{8,0},{16,24},{24,16},{32,40},{40,32},{48,56},{56,48},{64,72... | collective-permute-start | bytes 1179656 | tf_op jit(solution)/shard_map/ppermute | solution.py:30

commit v4 on v3

--- a/solution.py
+++ b/solution.py
@@ -10,27 +10,52 @@
 LAGS = 64
 EDGE = 128
 TIME_BLOCK = 2048
-CHAN_BITS = ((0, 1, 4, 2, 3), (0, 4, 1, 2, 3))
+CHAN_BITS = (((0,), (1,), (4,), (2, 3)), ((0,), (4,), (1,), (2, 3)))
 
-def xor_pairs(size, bit):
-    return [(i, i ^ (1 << bit)) for i in range(size)]
+def digit_of(me, bits):
+    digit = 0
+    for bit in bits:
+        digit = digit * 2 + ((me >> bit) & 1)
+    return digit
+
+
+def flip_mask(bits, offset):
+    mask = 0
+    for place, bit in enumerate(bits):
+        if (offset >> (len(bits) - 1 - place)) & 1:
+            mask |= 1 << bit
+    return mask
+
+
+def xor_pairs(size, mask):
+    return [(i, i ^ mask) for i in range(size)]
 
 
 def broadcast(masked, me, axis, size, order):
     pieces = masked
-    for bit in order:
-        half = pieces.shape[0] // 2
-        low, high = pieces[:half], pieces[half:]
-        mine = ((me >> bit) & 1) == 0
-        send = jnp.where(mine, high, low)
-        keep = jnp.where(mine, low, high)
-        pieces = keep + lax.ppermute(send, axis, xor_pairs(size, bit))
-    for bit in reversed(order):
-        mine = ((me >> bit) & 1) == 0
-        got = lax.ppermute(pieces, axis, xor_pairs(size, bit))
-        pieces = jnp.where(
-            mine, jnp.concatenate([pieces, got], 0), jnp.concatenate([got, pieces], 0)
-        )
+    for bits in order:
+        radix = 1 << len(bits)
+        quarters = pieces.reshape(radix, pieces.shape[0] // radix, *pieces.shape[1:])
+        digit = digit_of(me, bits)
+        pieces = lax.dynamic_index_in_dim(quarters, digit, 0, keepdims=False)
+        for offset in range(1, radix):
+            send = lax.dynamic_index_in_dim(quarters, digit ^ offset, 0, keepdims=False)
+            pieces = pieces + lax.ppermute(send, axis, xor_pairs(size, flip_mask(bits, offset)))
+    for bits in reversed(order):
+        radix = 1 << len(bits)
+        digit = digit_of(me, bits)
+        got = [pieces] + [
+            lax.ppermute(pieces, axis, xor_pairs(size, flip_mask(bits, offset)))
+            for offset in range(1, radix)
+        ]
+        slots = []
+        for slot in range(radix):
+            offset = slot ^ digit
+            value = got[0]
+            for other in range(1, radix):
+                value = jnp.where(offset == other, got[other], value)
+            slots.append(value)
+        pieces = jnp.concatenate(slots, 0)
     return pieces
 
 

time: 113 us -> 107 us (0.947)
  waiting for transfers between devices: 24.8 us -> 17.6 us
    ppermute x20 -> x24, waiting for transfers between devices: 24.8 us -> 17.6 us  [the longest x12 12.4 us: broadcast(): lax.ppermute(pieces, axis, xor_pairs(size, flip_mask(bits, offset)))]
    concatenate x0 -> x8, other arithmetic: none -> 2.12 us  [broadcast(): pieces = jnp.concatenate(slots, 0)]
    select_n x19 -> x8, other arithmetic: 2.35 us -> 0.26 us  [broadcast(): value = jnp.where(offset == other, got[other], value)]
    ppermute x20 -> x24, starting transfers between devices: 44.1 us -> 44.3 us  [the longest x12 24.8 us: broadcast(): lax.ppermute(send, axis, xor_pairs(size, flip_mask(bits, offset)))]
  transfers between devices with their start and end apart: 20 -> 24, of which waited for: 12 -> 9; matrix products, arithmetic and copies ran while one was open for 2% -> 3% of each run, Pallas kernels for 0% -> 0%
where the time goes in v4:
time: 107 us; the launch traced here: 106 us
  starting transfers between devices  44.3 us (41%)
  blocking collectives  18.1 us (17%)
  waiting for transfers between devices  17.6 us (16%)
  Pallas kernels  13.3 us (12%)
  other arithmetic  5.4 us (5%)
  local copies, waits for them, and re-layouts  4.11 us (4%)
  between operations  2.79 us (3%)
    ppermute x12, starting transfers between devices, broadcast(): lax.ppermute(send, axis, xor_pairs(size, flip_mask(bits, offset)))  24.8 us
    ppermute x12, starting transfers between devices, broadcast(): lax.ppermute(pieces, axis, xor_pairs(size, flip_mask(bits, offset)))  19.5 us
    all_to_all x1, blocking collectives, body(): reduced = jnp.sum(lax.all_to_all(complete, 'win', 0, 0, tiled=True), 0)  18.1 us
    pallas_call x1, Pallas kernels, correlate(): pl.pallas_call(kernel, out_shape=jax.ShapeDtypeStruct((blocks, rows, out_...  13.3 us
    ppermute x12, waiting for transfers between devices, broadcast(): lax.ppermute(pieces, axis, xor_pairs(size, flip_mask(bits, offset)))  12.4 us
    ppermute x12, waiting for transfers between devices, broadcast(): lax.ppermute(send, axis, xor_pairs(size, flip_mask(bits, offset)))  5.27 us
  transfers between devices with their start and end apart: 24, of which 9 were waited for; matrix products, arithmetic and copies ran while one was open for 3% of the time, Pallas kernels for 0%

profile of v4, /device:TPU:8, one launch (start us, length us, event | category | flops | bytes accessed | tf_op | source)
XLA Modules:
  0.0 105.6 jit_solution(3848156659753924354)
XLA Ops:
  0.0 1.4 %fusion.8 = (s32[1]{0:T(128)}, s32[1]{0:T(128)}, s32[1]{0:T(128)}) fusion(s32[3]{0:T(128)} %param.4), kind=kLoop, calls=%fused_computation.67 | loop fusion | bytes 24 | tf_op jit(solution)/shard_map/slice | solution.py:128
  2.6 1.3 %fusion.1 = f32[32]{0:T(128)S(1)} fusion(bf16[1,32,8192]{2,1,0:T(8,128)(2,1)} %param.3), kind=kLoop, calls=%fused_computation.5 | loop fusion | flops 786400 | bytes 524416 | tf_op jit(solution)/shard_map/reduce_sum | solution.py:123
  9.2 2.4 %collective-permute-start.13 = (bf16[8,48,256]{2,1,0:T(8,128)(2,1)S(1)}, bf16[8,48,256]{2,1,0:T(8,128)(2,1)S(1)}, u32[]{:S(2)}, u32[]{:S(2)}) collective-permute-start(bf16[8,48,256]{2,1,0:T(8,128)(2,1)S(1)} %dynamic-slice_bitcast_fusion), channel_id=1, source_target_pairs={{0,128},{8,136},{16,144},{24,152},{32,160},{40,168},{48,176},{56,1... | collective-permute-start | bytes 589832 | tf_op jit(solution)/shard_map/ppermute | solution.py:43
  11.7 2.0 %collective-permute-start.1 = (bf16[8,48,256]{2,1,0:T(8,128)(2,1)S(1)}, bf16[8,48,256]{2,1,0:T(8,128)(2,1)S(1)}, u32[]{:S(2)}, u32[]{:S(2)}) collective-permute-start(bf16[8,48,256]{2,1,0:T(8,128)(2,1)S(1)} %dynamic-slice_bitcast_fusion.1), channel_id=1, source_target_pairs={{0,16},{8,24},{16,0},{24,8},{32,48},{40,56},{48,32},{56,40},{64,80... | collective-permute-start | bytes 589832 | tf_op jit(solution)/shard_map/ppermute | solution.py:43
  13.7 4.0 %collective-permute-done.13 = bf16[8,48,256]{2,1,0:T(8,128)(2,1)S(1)} collective-permute-done((bf16[8,48,256]{2,1,0:T(8,128)(2,1)S(1)}, bf16[8,48,256]{2,1,0:T(8,128)(2,1)S(1)}, u32[]{:S(2)}, u32[]{:S(2)}) %collective-permute-start.13) | collective-permute-done | bytes 196640 | tf_op jit(solution)/shard_map/ppermute | solution.py:43
  17.7 2.0 %collective-permute-start.14 = (bf16[4,48,256]{2,1,0:T(8,128)(2,1)S(1)}, bf16[4,48,256]{2,1,0:T(8,128)(2,1)S(1)}, u32[]{:S(2)}, u32[]{:S(2)}) collective-permute-start(bf16[4,48,256]{2,1,0:T(8,128)(2,1)S(1)} %dynamic-slice_bitcast_fusion.2), channel_id=1, source_target_pairs={{0,16},{8,24},{16,0},{24,8},{32,48},{40,56},{48,32},{56,40},{64,80... | collective-permute-start | bytes 294920 | tf_op jit(solution)/shard_map/ppermute | solution.py:43
  19.8 2.4 %collective-permute-start.2 = (bf16[4,48,256]{2,1,0:T(8,128)(2,1)S(1)}, bf16[4,48,256]{2,1,0:T(8,128)(2,1)S(1)}, u32[]{:S(2)}, u32[]{:S(2)}) collective-permute-start(bf16[4,48,256]{2,1,0:T(8,128)(2,1)S(1)} %dynamic-slice_bitcast_fusion.3), channel_id=1, source_target_pairs={{0,128},{8,136},{16,144},{24,152},{32,160},{40,168},{48,176},{56,1... | collective-permute-start | bytes 294920 | tf_op jit(solution)/shard_map/ppermute | solution.py:43
  22.5 7.3 %collective-permute-start.15 = (bf16[1,48,256]{2,1,0:T(8,128)(2,1)S(1)}, bf16[1,48,256]{2,1,0:T(8,128)(2,1)S(1)}, u32[]{:S(2)}, u32[]{:S(2)}) collective-permute-start(bf16[1,48,256]{2,1,0:T(8,128)(2,1)S(1)} %get-tuple-element.31), channel_id=1, source_target_pairs={{0,64},{8,72},{16,80},{24,88},{32,96},{40,104},{48,112},{56,120},{... | collective-permute-start | bytes 73736 | tf_op jit(solution)/shard_map/ppermute | solution.py:43
  29.8 1.5 %collective-permute-start.16 = (bf16[1,48,256]{2,1,0:T(8,128)(2,1)S(1)}, bf16[1,48,256]{2,1,0:T(8,128)(2,1)S(1)}, u32[]{:S(2)}, u32[]{:S(2)}) collective-permute-start(bf16[1,48,256]{2,1,0:T(8,128)(2,1)S(1)} %get-tuple-element.33), channel_id=1, source_target_pairs={{0,32},{8,40},{16,48},{24,56},{32,0},{40,8},{48,16},{56,24},{64,96... | collective-permute-start | bytes 73736 | tf_op jit(solution)/shard_map/ppermute | solution.py:43
  31.3 5.1 %collective-permute-start.3 = (bf16[1,48,256]{2,1,0:T(8,128)(2,1)S(1)}, bf16[1,48,256]{2,1,0:T(8,128)(2,1)S(1)}, u32[]{:S(2)}, u32[]{:S(2)}) collective-permute-start(bf16[1,48,256]{2,1,0:T(8,128)(2,1)S(1)} %get-tuple-element.38), channel_id=1, source_target_pairs={{0,64},{8,72},{16,80},{24,88},{32,96},{40,104},{48,112},{56,120},{... | collective-permute-start | bytes 73736 | tf_op jit(solution)/shard_map/ppermute | solution.py:43
  36.4 1.5 %collective-permute-start.4 = (bf16[1,48,256]{2,1,0:T(8,128)(2,1)S(1)}, bf16[1,48,256]{2,1,0:T(8,128)(2,1)S(1)}, u32[]{:S(2)}, u32[]{:S(2)}) collective-permute-start(bf16[1,48,256]{2,1,0:T(8,128)(2,1)S(1)} %get-tuple-element.40), channel_id=1, source_target_pairs={{0,32},{8,40},{16,48},{24,56},{32,0},{40,8},{48,16},{56,24},{64,96... | collective-permute-start | bytes 73736 | tf_op jit(solution)/shard_map/ppermute | solution.py:43
  37.9 4.2 %collective-permute-start.18 = (bf16[1,48,256]{2,1,0:T(8,128)(2,1)S(1)}, bf16[1,48,256]{2,1,0:T(8,128)(2,1)S(1)}, u32[]{:S(2)}, u32[]{:S(2)}) collective-permute-start(bf16[1,48,256]{2,1,0:T(8,128)(2,1)S(1)} %add_add_fusion), channel_id=1, source_target_pairs={{0,96},{8,104},{16,112},{24,120},{32,64},{40,72},{48,80},{56,88},{... | collective-permute-start | bytes 73736 | tf_op jit(solution)/shard_map/ppermute | solution.py:48
  42.1 1.5 %collective-permute-start.19 = (bf16[1,48,256]{2,1,0:T(8,128)(2,1)S(1)}, bf16[1,48,256]{2,1,0:T(8,128)(2,1)S(1)}, u32[]{:S(2)}, u32[]{:S(2)}) collective-permute-start(bf16[1,48,256]{2,1,0:T(8,128)(2,1)S(1)} %add_add_fusion), channel_id=1, source_target_pairs={{0,32},{8,40},{16,48},{24,56},{32,0},{40,8},{48,16},{56,24},{64,96... | collective-permute-start | bytes 73736 | tf_op jit(solution)/shard_map/ppermute | solution.py:48
  44.6 4.1 %collective-permute-start.6 = (bf16[1,48,256]{2,1,0:T(8,128)(2,1)S(1)}, bf16[1,48,256]{2,1,0:T(8,128)(2,1)S(1)}, u32[]{:S(2)}, u32[]{:S(2)}) collective-permute-start(bf16[1,48,256]{2,1,0:T(8,128)(2,1)S(1)} %add_add_fusion.1), channel_id=1, source_target_pairs={{0,96},{8,104},{16,112},{24,120},{32,64},{40,72},{48,80},{56,88},{... | collective-permute-start | bytes 73736 | tf_op jit(solution)/shard_map/ppermute | solution.py:48
  48.7 1.5 %collective-permute-start.7 = (bf16[1,48,256]{2,1,0:T(8,128)(2,1)S(1)}, bf16[1,48,256]{2,1,0:T(8,128)(2,1)S(1)}, u32[]{:S(2)}, u32[]{:S(2)}) collective-permute-start(bf16[1,48,256]{2,1,0:T(8,128)(2,1)S(1)} %add_add_fusion.1), channel_id=1, source_target_pairs={{0,32},{8,40},{16,48},{24,56},{32,0},{40,8},{48,16},{56,24},{64,96... | collective-permute-start | bytes 73736 | tf_op jit(solution)/shard_map/ppermute | solution.py:48
  51.4 1.2 %collective-permute-start.21 = (bf16[4,48,256]{2,1,0:T(8,128)(2,1)S(1)}, bf16[4,48,256]{2,1,0:T(8,128)(2,1)S(1)}, u32[]{:S(2)}, u32[]{:S(2)}) collective-permute-start(bf16[4,48,256]{2,1,0:T(8,128)(2,1)S(1)} %pad_maximum_fusion.7), channel_id=1, source_target_pairs={{0,16},{8,24},{16,0},{24,8},{32,48},{40,56},{48,32},{56,40},{64,80... | collective-permute-start | bytes 294920 | tf_op jit(solution)/shard_map/ppermute | solution.py:48
  53.5 4.5 %collective-permute-done.8 = bf16[1,48,256]{2,1,0:T(8,128)(2,1)S(1)} collective-permute-done((bf16[1,48,256]{2,1,0:T(8,128)(2,1)S(1)}, bf16[1,48,256]{2,1,0:T(8,128)(2,1)S(1)}, u32[]{:S(2)}, u32[]{:S(2)}) %collective-permute-start.8) | collective-permute-done | bytes 24608 | tf_op jit(solution)/shard_map/ppermute | solution.py:48
  58.0 2.4 %collective-permute-start.9 = (bf16[4,48,256]{2,1,0:T(8,128)(2,1)S(1)}, bf16[4,48,256]{2,1,0:T(8,128)(2,1)S(1)}, u32[]{:S(2)}, u32[]{:S(2)}) collective-permute-start(bf16[4,48,256]{2,1,0:T(8,128)(2,1)S(1)} %pad_maximum_fusion.6), channel_id=1, source_target_pairs={{0,128},{8,136},{16,144},{24,152},{32,160},{40,168},{48,176},{56,1... | collective-permute-start | bytes 294920 | tf_op jit(solution)/shard_map/ppermute | solution.py:48
  60.4 1.3 %collective-permute-start.22 = (bf16[8,48,256]{2,1,0:T(8,128)(2,1)S(1)}, bf16[8,48,256]{2,1,0:T(8,128)(2,1)S(1)}, u32[]{:S(2)}, u32[]{:S(2)}) collective-permute-start(bf16[8,48,256]{2,1,0:T(8,128)(2,1)S(1)} %pad_maximum_fusion.5), channel_id=1, source_target_pairs={{0,128},{8,136},{16,144},{24,152},{32,160},{40,168},{48,176},{56,1... | collective-permute-start | bytes 589832 | tf_op jit(solution)/shard_map/ppermute | solution.py:48
  61.7 2.4 %collective-permute-done.9 = bf16[4,48,256]{2,1,0:T(8,128)(2,1)S(1)} collective-permute-done((bf16[4,48,256]{2,1,0:T(8,128)(2,1)S(1)}, bf16[4,48,256]{2,1,0:T(8,128)(2,1)S(1)}, u32[]{:S(2)}, u32[]{:S(2)}) %collective-permute-start.9) | collective-permute-done | bytes 98336 | tf_op jit(solution)/shard_map/ppermute | solution.py:48
  65.3 2.3 %collective-permute-done.22 = bf16[8,48,256]{2,1,0:T(8,128)(2,1)S(1)} collective-permute-done((bf16[8,48,256]{2,1,0:T(8,128)(2,1)S(1)}, bf16[8,48,256]{2,1,0:T(8,128)(2,1)S(1)}, u32[]{:S(2)}, u32[]{:S(2)}) %collective-permute-start.22) | collective-permute-done | bytes 196640 | tf_op jit(solution)/shard_map/ppermute | solution.py:48
  67.9 2.1 %collective-permute-done.10 = bf16[8,48,256]{2,1,0:T(8,128)(2,1)S(1)} collective-permute-done((bf16[8,48,256]{2,1,0:T(8,128)(2,1)S(1)}, bf16[8,48,256]{2,1,0:T(8,128)(2,1)S(1)}, u32[]{:S(2)}, u32[]{:S(2)}) %collective-permute-start.10) | collective-permute-done | bytes 196640 | tf_op jit(solution)/shard_map/ppermute | solution.py:48
  73.2 13.3 %shard_map.37 = f32[8,96,256]{2,1,0:T(8,128)} custom-call(f32[1,1]{1,0:T(1,128)S(6)} %div.9.factor_ref, bf16[32,48,256]{2,1,0:T(8,128)(2,1)} %pad_maximum_fusion.refs_0_, bf16[32,48,256]{2,1,0:T(8,128)(2,1)} %pad_maximum_fusion.1.refs_1_, bf16[32,8192]{1,0:T(8,128)(2,1)} %fusion.2.refs_2_), custom_call_target="tpu_custom_call" | custom-call | tf_op jit(solution)/shard_map/pallas_call | solution.py:103
  86.6 18.1 %all_to_all.5 = f32[8,96,256]{2,1,0:T(8,128)S(1)} all-to-all(f32[8,96,256]{2,1,0:T(8,128)} %shard_map.37), channel_id=1, replica_groups=mesh['chan'=32,'win'=8] {'win'}, dimensions={0} | all-to-all | bytes 1572864 | tf_op jit(solution)/shard_map/all_to_all | solution.py:140
  (72 shorter events, 13.1 us)
Async XLA Ops:
  7.2 1.8 %collective-permute-start.12 = (bf16[16,48,256]{2,1,0:T(8,128)(2,1)S(1)}, bf16[16,48,256]{2,1,0:T(8,128)(2,1)S(1)}, u32[]{:S(2)}, u32[]{:S(2)}) collective-permute-start(bf16[16,48,256]{2,1,0:T(8,128)(2,1)S(1)} %bitcast.71), channel_id=1, source_target_pairs={{0,8},{8,0},{16,24},{24,16},{32,40},{40,32},{48,56},{56,48},{64,72... | collective-permute-start | bytes 1179656 | tf_op jit(solution)/shard_map/ppermute | solution.py:43
  7.4 4.1 %collective-permute-start = (bf16[16,48,256]{2,1,0:T(8,128)(2,1)S(1)}, bf16[16,48,256]{2,1,0:T(8,128)(2,1)S(1)}, u32[]{:S(2)}, u32[]{:S(2)}) collective-permute-start(bf16[16,48,256]{2,1,0:T(8,128)(2,1)S(1)} %bitcast.70), channel_id=1, source_target_pairs={{0,8},{8,0},{16,24},{24,16},{32,40},{40,32},{48,56},{56,48},{64,72... | collective-permute-start | bytes 1179656 | tf_op jit(solution)/shard_map/ppermute | solution.py:43
  9.2 8.5 %collective-permute-start.13 = (bf16[8,48,256]{2,1,0:T(8,128)(2,1)S(1)}, bf16[8,48,256]{2,1,0:T(8,128)(2,1)S(1)}, u32[]{:S(2)}, u32[]{:S(2)}) collective-permute-start(bf16[8,48,256]{2,1,0:T(8,128)(2,1)S(1)} %dynamic-slice_bitcast_fusion), channel_id=1, source_target_pairs={{0,128},{8,136},{16,144},{24,152},{32,160},{40,168},{48,176},{56,1... | collective-permute-start | bytes 589832 | tf_op jit(solution)/shard_map/ppermute | solution.py:43
  11.7 8.0 %collective-permute-start.1 = (bf16[8,48,256]{2,1,0:T(8,128)(2,1)S(1)}, bf16[8,48,256]{2,1,0:T(8,128)(2,1)S(1)}, u32[]{:S(2)}, u32[]{:S(2)}) collective-permute-start(bf16[8,48,256]{2,1,0:T(8,128)(2,1)S(1)} %dynamic-slice_bitcast_fusion.1), channel_id=1, source_target_pairs={{0,16},{8,24},{16,0},{24,8},{32,48},{40,56},{48,32},{56,40},{64,80... | collective-permute-start | bytes 589832 | tf_op jit(solution)/shard_map/ppermute | solution.py:43
  17.7 4.7 %collective-permute-start.14 = (bf16[4,48,256]{2,1,0:T(8,128)(2,1)S(1)}, bf16[4,48,256]{2,1,0:T(8,128)(2,1)S(1)}, u32[]{:S(2)}, u32[]{:S(2)}) collective-permute-start(bf16[4,48,256]{2,1,0:T(8,128)(2,1)S(1)} %dynamic-slice_bitcast_fusion.2), channel_id=1, source_target_pairs={{0,16},{8,24},{16,0},{24,8},{32,48},{40,56},{48,32},{56,40},{64,80... | collective-permute-start | bytes 294920 | tf_op jit(solution)/shard_map/ppermute | solution.py:43
  19.8 11.4 %collective-permute-start.2 = (bf16[4,48,256]{2,1,0:T(8,128)(2,1)S(1)}, bf16[4,48,256]{2,1,0:T(8,128)(2,1)S(1)}, u32[]{:S(2)}, u32[]{:S(2)}) collective-permute-start(bf16[4,48,256]{2,1,0:T(8,128)(2,1)S(1)} %dynamic-slice_bitcast_fusion.3), channel_id=1, source_target_pairs={{0,128},{8,136},{16,144},{24,152},{32,160},{40,168},{48,176},{56,1... | collective-permute-start | bytes 294920 | tf_op jit(solution)/shard_map/ppermute | solution.py:43
  22.5 15.4 %collective-permute-start.15 = (bf16[1,48,256]{2,1,0:T(8,128)(2,1)S(1)}, bf16[1,48,256]{2,1,0:T(8,128)(2,1)S(1)}, u32[]{:S(2)}, u32[]{:S(2)}) collective-permute-start(bf16[1,48,256]{2,1,0:T(8,128)(2,1)S(1)} %get-tuple-element.31), channel_id=1, source_target_pairs={{0,64},{8,72},{16,80},{24,88},{32,96},{40,104},{48,112},{56,120},{... | collective-permute-start | bytes 73736 | tf_op jit(solution)/shard_map/ppermute | solution.py:43
  29.8 8.1 %collective-permute-start.16 = (bf16[1,48,256]{2,1,0:T(8,128)(2,1)S(1)}, bf16[1,48,256]{2,1,0:T(8,128)(2,1)S(1)}, u32[]{:S(2)}, u32[]{:S(2)}) collective-permute-start(bf16[1,48,256]{2,1,0:T(8,128)(2,1)S(1)} %get-tuple-element.33), channel_id=1, source_target_pairs={{0,32},{8,40},{16,48},{24,56},{32,0},{40,8},{48,16},{56,24},{64,96... | collective-permute-start | bytes 73736 | tf_op jit(solution)/shard_map/ppermute | solution.py:43
  31.2 6.6 %collective-permute-start.17 = (bf16[1,48,256]{2,1,0:T(8,128)(2,1)S(1)}, bf16[1,48,256]{2,1,0:T(8,128)(2,1)S(1)}, u32[]{:S(2)}, u32[]{:S(2)}) collective-permute-start(bf16[1,48,256]{2,1,0:T(8,128)(2,1)S(1)} %get-tuple-element.32), channel_id=1, source_target_pairs={{0,96},{8,104},{16,112},{24,120},{32,64},{40,72},{48,80},{56,88},{... | collective-permute-start | bytes 73736 | tf_op jit(solution)/shard_map/ppermute | solution.py:43
  31.3 12.3 %collective-permute-start.3 = (bf16[1,48,256]{2,1,0:T(8,128)(2,1)S(1)}, bf16[1,48,256]{2,1,0:T(8,128)(2,1)S(1)}, u32[]{:S(2)}, u32[]{:S(2)}) collective-permute-start(bf16[1,48,256]{2,1,0:T(8,128)(2,1)S(1)} %get-tuple-element.38), channel_id=1, source_target_pairs={{0,64},{8,72},{16,80},{24,88},{32,96},{40,104},{48,112},{56,120},{... | collective-permute-start | bytes 73736 | tf_op jit(solution)/shard_map/ppermute | solution.py:43
  36.4 8.2 %collective-permute-start.4 = (bf16[1,48,256]{2,1,0:T(8,128)(2,1)S(1)}, bf16[1,48,256]{2,1,0:T(8,128)(2,1)S(1)}, u32[]{:S(2)}, u32[]{:S(2)}) collective-permute-start(bf16[1,48,256]{2,1,0:T(8,128)(2,1)S(1)} %get-tuple-element.40), channel_id=1, source_target_pairs={{0,32},{8,40},{16,48},{24,56},{32,0},{40,8},{48,16},{56,24},{64,96... | collective-permute-start | bytes 73736 | tf_op jit(solution)/shard_map/ppermute | solution.py:43
  37.9 6.7 %collective-permute-start.5 = (bf16[1,48,256]{2,1,0:T(8,128)(2,1)S(1)}, bf16[1,48,256]{2,1,0:T(8,128)(2,1)S(1)}, u32[]{:S(2)}, u32[]{:S(2)}) collective-permute-start(bf16[1,48,256]{2,1,0:T(8,128)(2,1)S(1)} %get-tuple-element.39), channel_id=1, source_target_pairs={{0,96},{8,104},{16,112},{24,120},{32,64},{40,72},{48,80},{56,88},{... | collective-permute-start | bytes 73736 | tf_op jit(solution)/shard_map/ppermute | solution.py:43
  37.9 12.3 %collective-permute-start.18 = (bf16[1,48,256]{2,1,0:T(8,128)(2,1)S(1)}, bf16[1,48,256]{2,1,0:T(8,128)(2,1)S(1)}, u32[]{:S(2)}, u32[]{:S(2)}) collective-permute-start(bf16[1,48,256]{2,1,0:T(8,128)(2,1)S(1)} %add_add_fusion), channel_id=1, source_target_pairs={{0,96},{8,104},{16,112},{24,120},{32,64},{40,72},{48,80},{56,88},{... | collective-permute-start | bytes 73736 | tf_op jit(solution)/shard_map/ppermute | solution.py:48
  42.1 9.1 %collective-permute-start.19 = (bf16[1,48,256]{2,1,0:T(8,128)(2,1)S(1)}, bf16[1,48,256]{2,1,0:T(8,128)(2,1)S(1)}, u32[]{:S(2)}, u32[]{:S(2)}) collective-permute-start(bf16[1,48,256]{2,1,0:T(8,128)(2,1)S(1)} %add_add_fusion), channel_id=1, source_target_pairs={{0,32},{8,40},{16,48},{24,56},{32,0},{40,8},{48,16},{56,24},{64,96... | collective-permute-start | bytes 73736 | tf_op jit(solution)/shard_map/ppermute | solution.py:48
  43.6 7.8 %collective-permute-start.20 = (bf16[1,48,256]{2,1,0:T(8,128)(2,1)S(1)}, bf16[1,48,256]{2,1,0:T(8,128)(2,1)S(1)}, u32[]{:S(2)}, u32[]{:S(2)}) collective-permute-start(bf16[1,48,256]{2,1,0:T(8,128)(2,1)S(1)} %add_add_fusion), channel_id=1, source_target_pairs={{0,64},{8,72},{16,80},{24,88},{32,96},{40,104},{48,112},{56,120},{... | collective-permute-start | bytes 73736 | tf_op jit(solution)/shard_map/ppermute | solution.py:48
  44.6 8.1 %collective-permute-start.6 = (bf16[1,48,256]{2,1,0:T(8,128)(2,1)S(1)}, bf16[1,48,256]{2,1,0:T(8,128)(2,1)S(1)}, u32[]{:S(2)}, u32[]{:S(2)}) collective-permute-start(bf16[1,48,256]{2,1,0:T(8,128)(2,1)S(1)} %add_add_fusion.1), channel_id=1, source_target_pairs={{0,96},{8,104},{16,112},{24,120},{32,64},{40,72},{48,80},{56,88},{... | collective-permute-start | bytes 73736 | tf_op jit(solution)/shard_map/ppermute | solution.py:48
  48.7 4.7 %collective-permute-start.7 = (bf16[1,48,256]{2,1,0:T(8,128)(2,1)S(1)}, bf16[1,48,256]{2,1,0:T(8,128)(2,1)S(1)}, u32[]{:S(2)}, u32[]{:S(2)}) collective-permute-start(bf16[1,48,256]{2,1,0:T(8,128)(2,1)S(1)} %add_add_fusion.1), channel_id=1, source_target_pairs={{0,32},{8,40},{16,48},{24,56},{32,0},{40,8},{48,16},{56,24},{64,96... | collective-permute-start | bytes 73736 | tf_op jit(solution)/shard_map/ppermute | solution.py:48
  50.2 7.7 %collective-permute-start.8 = (bf16[1,48,256]{2,1,0:T(8,128)(2,1)S(1)}, bf16[1,48,256]{2,1,0:T(8,128)(2,1)S(1)}, u32[]{:S(2)}, u32[]{:S(2)}) collective-permute-start(bf16[1,48,256]{2,1,0:T(8,128)(2,1)S(1)} %add_add_fusion.1), channel_id=1, source_target_pairs={{0,64},{8,72},{16,80},{24,88},{32,96},{40,104},{48,112},{56,120},{... | collective-permute-start | bytes 73736 | tf_op jit(solution)/shard_map/ppermute | solution.py:48
  51.4 8.9 %collective-permute-start.21 = (bf16[4,48,256]{2,1,0:T(8,128)(2,1)S(1)}, bf16[4,48,256]{2,1,0:T(8,128)(2,1)S(1)}, u32[]{:S(2)}, u32[]{:S(2)}) collective-permute-start(bf16[4,48,256]{2,1,0:T(8,128)(2,1)S(1)} %pad_maximum_fusion.7), channel_id=1, source_target_pairs={{0,16},{8,24},{16,0},{24,8},{32,48},{40,56},{48,32},{56,40},{64,80... | collective-permute-start | bytes 294920 | tf_op jit(solution)/shard_map/ppermute | solution.py:48
  58.0 6.2 %collective-permute-start.9 = (bf16[4,48,256]{2,1,0:T(8,128)(2,1)S(1)}, bf16[4,48,256]{2,1,0:T(8,128)(2,1)S(1)}, u32[]{:S(2)}, u32[]{:S(2)}) collective-permute-start(bf16[4,48,256]{2,1,0:T(8,128)(2,1)S(1)} %pad_maximum_fusion.6), channel_id=1, source_target_pairs={{0,128},{8,136},{16,144},{24,152},{32,160},{40,168},{48,176},{56,1... | collective-permute-start | bytes 294920 | tf_op jit(solution)/shard_map/ppermute | solution.py:48
  60.4 7.3 %collective-permute-start.22 = (bf16[8,48,256]{2,1,0:T(8,128)(2,1)S(1)}, bf16[8,48,256]{2,1,0:T(8,128)(2,1)S(1)}, u32[]{:S(2)}, u32[]{:S(2)}) collective-permute-start(bf16[8,48,256]{2,1,0:T(8,128)(2,1)S(1)} %pad_maximum_fusion.5), channel_id=1, source_target_pairs={{0,128},{8,136},{16,144},{24,152},{32,160},{40,168},{48,176},{56,1... | collective-permute-start | bytes 589832 | tf_op jit(solution)/shard_map/ppermute | solution.py:48
  64.2 5.8 %collective-permute-start.10 = (bf16[8,48,256]{2,1,0:T(8,128)(2,1)S(1)}, bf16[8,48,256]{2,1,0:T(8,128)(2,1)S(1)}, u32[]{:S(2)}, u32[]{:S(2)}) collective-permute-start(bf16[8,48,256]{2,1,0:T(8,128)(2,1)S(1)} %pad_maximum_fusion.4), channel_id=1, source_target_pairs={{0,16},{8,24},{16,0},{24,8},{32,48},{40,56},{48,32},{56,40},{64,80... | collective-permute-start | bytes 589832 | tf_op jit(solution)/shard_map/ppermute | solution.py:48
  67.8 3.4 %collective-permute-start.23 = (bf16[16,48,256]{2,1,0:T(8,128)(2,1)S(1)}, bf16[16,48,256]{2,1,0:T(8,128)(2,1)S(1)}, u32[]{:S(2)}, u32[]{:S(2)}) collective-permute-start(bf16[16,48,256]{2,1,0:T(8,128)(2,1)S(1)} %pad_maximum_fusion.3), channel_id=1, source_target_pairs={{0,8},{8,0},{16,24},{24,16},{32,40},{40,32},{48,56},{56,48},{64,72... | collective-permute-start | bytes 1179656 | tf_op jit(solution)/shard_map/ppermute | solution.py:48
  70.1 2.1 %collective-permute-start.11 = (bf16[16,48,256]{2,1,0:T(8,128)(2,1)S(1)}, bf16[16,48,256]{2,1,0:T(8,128)(2,1)S(1)}, u32[]{:S(2)}, u32[]{:S(2)}) collective-permute-start(bf16[16,48,256]{2,1,0:T(8,128)(2,1)S(1)} %pad_maximum_fusion.2), channel_id=1, source_target_pairs={{0,8},{8,0},{16,24},{24,16},{32,40},{40,32},{48,56},{56,48},{64,72... | collective-permute-start | bytes 1179656 | tf_op jit(solution)/shard_map/ppermute | solution.py:48
  (1 other events, 6.0 us)

commit v5 on v4

--- a/solution.py
+++ b/solution.py
@@ -41,13 +41,15 @@
         for offset in range(1, radix):
             send = lax.dynamic_index_in_dim(quarters, digit ^ offset, 0, keepdims=False)
             pieces = pieces + lax.ppermute(send, axis, xor_pairs(size, flip_mask(bits, offset)))
-    for bits in reversed(order):
+    for place, bits in enumerate(reversed(order)):
         radix = 1 << len(bits)
         digit = digit_of(me, bits)
         got = [pieces] + [
             lax.ppermute(pieces, axis, xor_pairs(size, flip_mask(bits, offset)))
             for offset in range(1, radix)
         ]
+        if place == len(order) - 1 and radix == 2:
+            return got[0], got[1], digit
         slots = []
         for slot in range(radix):
             offset = slot ^ digit
@@ -59,43 +61,48 @@
     return pieces
 
 
-def correlate(halves, whitened, factor, blocks):
-    piece_count, rows_half, piece_width = halves[0].shape
+def correlate(halves, digit, whitened, factor, blocks):
+    piece_half, rows_half, piece_width = halves[0][0].shape
     rows = rows_half * len(halves)
     chan_dev, samples = whitened.shape
     per_block = TIME_BLOCK // piece_width
     width = TIME_BLOCK + 2 * EDGE
     out_width = LAGS * chan_dev // blocks
+    count = 2 * len(halves)
 
-    def kernel(factor_ref, *refs):
-        src_refs, w_ref, out_ref, pad_ref = refs[: len(halves)], refs[len(halves)], refs[-2], refs[-1]
+    def kernel(factor_ref, digit_ref, *refs):
+        src_refs, w_ref, out_ref, pad_ref = refs[:count], refs[count], refs[-2], refs[-1]
+        low_is_mine = digit_ref[0, 0] == 0
         pad_ref[:, :EDGE] = jnp.zeros((chan_dev, EDGE), pad_ref.dtype)
         pad_ref[:, EDGE + samples :] = jnp.zeros((chan_dev, EDGE), pad_ref.dtype)
         pad_ref[:, EDGE : EDGE + samples] = w_ref[...]
 
-        def block(k, acc):
-            base = pl.multiple_of(k * TIME_BLOCK, TIME_BLOCK)
-            window = pad_ref[:, pl.ds(base, width)]
+        def piece(which, index):
+            mine, other = src_refs[2 * which], src_refs[2 * which + 1]
+            local = index % piece_half
+            if index < piece_half:
+                return jnp.where(low_is_mine, mine[local], other[local])
+            return jnp.where(low_is_mine, other[local], mine[local])
+
+        acc = jnp.zeros((LAGS * chan_dev, rows), jnp.float32)
+        for k in range(samples // TIME_BLOCK):
+            base = k * TIME_BLOCK
+            window = pad_ref[:, base : base + width]
             parts = [
                 pltpu.roll(window, width - (EDGE - LAGS // 2 + lag), 1)[:, :TIME_BLOCK]
                 for lag in range(LAGS)
             ]
             stacked = jnp.concatenate(parts, 0)
-            first = pl.multiple_of(k * per_block, per_block)
             chunk = jnp.concatenate(
                 [
-                    jnp.concatenate([src_ref[first + j] for j in range(per_block)], 1)
-                    for src_ref in src_refs
+                    jnp.concatenate([piece(which, k * per_block + j) for j in range(per_block)], 1)
+                    for which in range(len(halves))
                 ],
                 0,
             )
-            return acc + lax.dot_general(
+            acc = acc + lax.dot_general(
                 stacked, chunk, (((1,), (1,)), ((), ())), preferred_element_type=jnp.float32
             )
-
-        acc = lax.fori_loop(
-            0, samples // TIME_BLOCK, block, jnp.zeros((LAGS * chan_dev, rows), jnp.float32)
-        )
         result = acc.T * factor_ref[0, 0]
         for j in range(blocks):
             out_ref[j] = result[:, j * out_width : (j + 1) * out_width]
@@ -103,11 +110,16 @@
     return pl.pallas_call(
         kernel,
         out_shape=jax.ShapeDtypeStruct((blocks, rows, out_width), jnp.float32),
-        in_specs=[pl.BlockSpec(memory_space=pltpu.SMEM)]
-        + [pl.BlockSpec(memory_space=pltpu.VMEM) for _ in range(len(halves) + 1)],
+        in_specs=[pl.BlockSpec(memory_space=pltpu.SMEM), pl.BlockSpec(memory_space=pltpu.SMEM)]
+        + [pl.BlockSpec(memory_space=pltpu.VMEM) for _ in range(count + 1)],
         out_specs=pl.BlockSpec(memory_space=pltpu.VMEM),
         scratch_shapes=[pltpu.VMEM((chan_dev, samples + 2 * EDGE), whitened.dtype)],
-    )(factor.reshape(1, 1), *halves, whitened)
+    )(
+        factor.reshape(1, 1),
+        digit.astype(jnp.int32).reshape(1, 1),
+        *[part for half in halves for part in half],
+        whitened,
+    )
 
 
 def body(traces, owner, window_mask):
@@ -131,12 +143,15 @@
     rows = masked.shape[0]
     masked = masked.reshape(rows, chan_size, samples // chan_size).transpose(1, 0, 2)
     half = rows // 2
-    halves = [
-        broadcast(masked[:, which * half : (which + 1) * half], chan_me, "chan", chan_size, order)
-        for which, order in enumerate(CHAN_BITS)
-    ]
+    whitened, masked = lax.optimization_barrier((whitened, masked))
+    halves = []
+    for which, order in enumerate(CHAN_BITS):
+        mine, other, digit = broadcast(
+            masked[:, which * half : (which + 1) * half], chan_me, "chan", chan_size, order
+        )
+        halves.append((mine, other))
     factor = own_flag / math.sqrt(samples)
-    complete = correlate(halves, whitened, factor, win_size)
+    complete = correlate(halves, digit, whitened, factor, win_size)
     reduced = jnp.sum(lax.all_to_all(complete, "win", 0, 0, tiled=True), 0)
     per_dev = LAGS // win_size
     return reduced.reshape(step_count, chan_dev, per_dev, chan_dev)

time: 107 us -> 105 us (0.981); the launches traced: 106 us -> 105 us
  other arithmetic: 5.4 us -> 3.34 us
  waiting for transfers between devices: 17.6 us -> 19.3 us
  Pallas kernels: 13.3 us -> 12.2 us
    concatenate x8 -> x6, other arithmetic: 2.12 us -> 0.15 us  [broadcast(): pieces = jnp.concatenate(slots, 0)]
    ppermute x12, waiting for transfers between devices: 12.4 us -> 14 us  [broadcast(): lax.ppermute(pieces, axis, xor_pairs(size, flip_mask(bits, offset)))]
    pallas_call x1, Pallas kernels: 13.3 us -> 12.2 us  [correlate(): pl.pallas_call(kernel, out_shape=jax.ShapeDtypeStruct((blocks, rows, out_...]
    unnamed x5 -> x13, local copies, waits for them, and re-layouts: 1.43 us -> 2.19 us
  transfers between devices with their start and end apart: 24 -> 24, of which waited for: 9 -> 10; matrix products, arithmetic and copies ran while one was open for 3% -> 1% of each run, Pallas kernels for 0% -> 0%
where the time goes in v5:
time: 105 us
  starting transfers between devices  44.5 us (42%)
  waiting for transfers between devices  19.3 us (18%)
  blocking collectives  17.8 us (17%)
  Pallas kernels  12.2 us (12%)
  local copies, waits for them, and re-layouts  4.91 us (5%)
  other arithmetic  3.34 us (3%)
  between operations  3 us (3%)
    ppermute x12, starting transfers between devices, broadcast(): lax.ppermute(send, axis, xor_pairs(size, flip_mask(bits, offset)))  24.8 us
    ppermute x12, starting transfers between devices, broadcast(): lax.ppermute(pieces, axis, xor_pairs(size, flip_mask(bits, offset)))  19.7 us
    all_to_all x1, blocking collectives, body(): reduced = jnp.sum(lax.all_to_all(complete, 'win', 0, 0, tiled=True), 0)  17.8 us
    ppermute x12, waiting for transfers between devices, broadcast(): lax.ppermute(pieces, axis, xor_pairs(size, flip_mask(bits, offset)))  14 us
    pallas_call x1, Pallas kernels, correlate(): pl.pallas_call(kernel, out_shape=jax.ShapeDtypeStruct((blocks, rows, out_...  12.2 us
    ppermute x12, waiting for transfers between devices, broadcast(): lax.ppermute(send, axis, xor_pairs(size, flip_mask(bits, offset)))  5.27 us
    unnamed x13, local copies, waits for them, and re-layouts  2.19 us
  transfers between devices with their start and end apart: 24, of which 10 were waited for; matrix products, arithmetic and copies ran while one was open for 1% of the time, Pallas kernels for 0%

profile of v5, /device:TPU:8, one launch (start us, length us, event | category | flops | bytes accessed | tf_op | source)
XLA Modules:
  0.0 105.0 jit_solution(16808486345980496970)
XLA Ops:
  0.0 1.4 %fusion.8 = (s32[1]{0:T(128)}, s32[1]{0:T(128)}, s32[1]{0:T(128)}) fusion(s32[3]{0:T(128)} %param.4), kind=kLoop, calls=%fused_computation.61 | loop fusion | bytes 24 | tf_op jit(solution)/shard_map/slice | solution.py:140
  2.8 1.3 %fusion.1 = f32[32]{0:T(128)S(1)} fusion(bf16[1,32,8192]{2,1,0:T(8,128)(2,1)} %param.3), kind=kLoop, calls=%fused_computation.5 | loop fusion | flops 786400 | bytes 524416 | tf_op jit(solution)/shard_map/reduce_sum | solution.py:135
  10.4 2.4 %collective-permute-start.13 = (bf16[8,48,256]{2,1,0:T(8,128)(2,1)S(1)}, bf16[8,48,256]{2,1,0:T(8,128)(2,1)S(1)}, u32[]{:S(2)}, u32[]{:S(2)}) collective-permute-start(bf16[8,48,256]{2,1,0:T(8,128)(2,1)S(1)} %dynamic-slice_bitcast_fusion), channel_id=1, source_target_pairs={{0,128},{8,136},{16,144},{24,152},{32,160},{40,168},{48,176},{56,1... | collective-permute-start | bytes 589832 | tf_op jit(solution)/shard_map/ppermute | solution.py:43
  12.9 2.0 %collective-permute-start.1 = (bf16[8,48,256]{2,1,0:T(8,128)(2,1)S(1)}, bf16[8,48,256]{2,1,0:T(8,128)(2,1)S(1)}, u32[]{:S(2)}, u32[]{:S(2)}) collective-permute-start(bf16[8,48,256]{2,1,0:T(8,128)(2,1)S(1)} %dynamic-slice_bitcast_fusion.1), channel_id=1, source_target_pairs={{0,16},{8,24},{16,0},{24,8},{32,48},{40,56},{48,32},{56,40},{64,80... | collective-permute-start | bytes 589832 | tf_op jit(solution)/shard_map/ppermute | solution.py:43
  14.9 4.0 %collective-permute-done.13 = bf16[8,48,256]{2,1,0:T(8,128)(2,1)S(1)} collective-permute-done((bf16[8,48,256]{2,1,0:T(8,128)(2,1)S(1)}, bf16[8,48,256]{2,1,0:T(8,128)(2,1)S(1)}, u32[]{:S(2)}, u32[]{:S(2)}) %collective-permute-start.13) | collective-permute-done | bytes 196640 | tf_op jit(solution)/shard_map/ppermute | solution.py:43
  18.9 2.0 %collective-permute-start.14 = (bf16[4,48,256]{2,1,0:T(8,128)(2,1)S(1)}, bf16[4,48,256]{2,1,0:T(8,128)(2,1)S(1)}, u32[]{:S(2)}, u32[]{:S(2)}) collective-permute-start(bf16[4,48,256]{2,1,0:T(8,128)(2,1)S(1)} %dynamic-slice_bitcast_fusion.2), channel_id=1, source_target_pairs={{0,16},{8,24},{16,0},{24,8},{32,48},{40,56},{48,32},{56,40},{64,80... | collective-permute-start | bytes 294920 | tf_op jit(solution)/shard_map/ppermute | solution.py:43
  21.0 2.4 %collective-permute-start.2 = (bf16[4,48,256]{2,1,0:T(8,128)(2,1)S(1)}, bf16[4,48,256]{2,1,0:T(8,128)(2,1)S(1)}, u32[]{:S(2)}, u32[]{:S(2)}) collective-permute-start(bf16[4,48,256]{2,1,0:T(8,128)(2,1)S(1)} %dynamic-slice_bitcast_fusion.3), channel_id=1, source_target_pairs={{0,128},{8,136},{16,144},{24,152},{32,160},{40,168},{48,176},{56,1... | collective-permute-start | bytes 294920 | tf_op jit(solution)/shard_map/ppermute | solution.py:43
  23.7 7.3 %collective-permute-start.15 = (bf16[1,48,256]{2,1,0:T(8,128)(2,1)S(1)}, bf16[1,48,256]{2,1,0:T(8,128)(2,1)S(1)}, u32[]{:S(2)}, u32[]{:S(2)}) collective-permute-start(bf16[1,48,256]{2,1,0:T(8,128)(2,1)S(1)} %get-tuple-element.31), channel_id=1, source_target_pairs={{0,64},{8,72},{16,80},{24,88},{32,96},{40,104},{48,112},{56,120},{... | collective-permute-start | bytes 73736 | tf_op jit(solution)/shard_map/ppermute | solution.py:43
  31.0 1.5 %collective-permute-start.16 = (bf16[1,48,256]{2,1,0:T(8,128)(2,1)S(1)}, bf16[1,48,256]{2,1,0:T(8,128)(2,1)S(1)}, u32[]{:S(2)}, u32[]{:S(2)}) collective-permute-start(bf16[1,48,256]{2,1,0:T(8,128)(2,1)S(1)} %get-tuple-element.33), channel_id=1, source_target_pairs={{0,32},{8,40},{16,48},{24,56},{32,0},{40,8},{48,16},{56,24},{64,96... | collective-permute-start | bytes 73736 | tf_op jit(solution)/shard_map/ppermute | solution.py:43
  32.5 5.1 %collective-permute-start.3 = (bf16[1,48,256]{2,1,0:T(8,128)(2,1)S(1)}, bf16[1,48,256]{2,1,0:T(8,128)(2,1)S(1)}, u32[]{:S(2)}, u32[]{:S(2)}) collective-permute-start(bf16[1,48,256]{2,1,0:T(8,128)(2,1)S(1)} %get-tuple-element.38), channel_id=1, source_target_pairs={{0,64},{8,72},{16,80},{24,88},{32,96},{40,104},{48,112},{56,120},{... | collective-permute-start | bytes 73736 | tf_op jit(solution)/shard_map/ppermute | solution.py:43
  37.6 1.5 %collective-permute-start.4 = (bf16[1,48,256]{2,1,0:T(8,128)(2,1)S(1)}, bf16[1,48,256]{2,1,0:T(8,128)(2,1)S(1)}, u32[]{:S(2)}, u32[]{:S(2)}) collective-permute-start(bf16[1,48,256]{2,1,0:T(8,128)(2,1)S(1)} %get-tuple-element.40), channel_id=1, source_target_pairs={{0,32},{8,40},{16,48},{24,56},{32,0},{40,8},{48,16},{56,24},{64,96... | collective-permute-start | bytes 73736 | tf_op jit(solution)/shard_map/ppermute | solution.py:43
  39.1 4.2 %collective-permute-start.18 = (bf16[1,48,256]{2,1,0:T(8,128)(2,1)S(1)}, bf16[1,48,256]{2,1,0:T(8,128)(2,1)S(1)}, u32[]{:S(2)}, u32[]{:S(2)}) collective-permute-start(bf16[1,48,256]{2,1,0:T(8,128)(2,1)S(1)} %add_add_fusion), channel_id=1, source_target_pairs={{0,96},{8,104},{16,112},{24,120},{32,64},{40,72},{48,80},{56,88},{... | collective-permute-start | bytes 73736 | tf_op jit(solution)/shard_map/ppermute | solution.py:48
  43.3 1.5 %collective-permute-start.19 = (bf16[1,48,256]{2,1,0:T(8,128)(2,1)S(1)}, bf16[1,48,256]{2,1,0:T(8,128)(2,1)S(1)}, u32[]{:S(2)}, u32[]{:S(2)}) collective-permute-start(bf16[1,48,256]{2,1,0:T(8,128)(2,1)S(1)} %add_add_fusion), channel_id=1, source_target_pairs={{0,32},{8,40},{16,48},{24,56},{32,0},{40,8},{48,16},{56,24},{64,96... | collective-permute-start | bytes 73736 | tf_op jit(solution)/shard_map/ppermute | solution.py:48
  45.8 4.1 %collective-permute-start.6 = (bf16[1,48,256]{2,1,0:T(8,128)(2,1)S(1)}, bf16[1,48,256]{2,1,0:T(8,128)(2,1)S(1)}, u32[]{:S(2)}, u32[]{:S(2)}) collective-permute-start(bf16[1,48,256]{2,1,0:T(8,128)(2,1)S(1)} %add_add_fusion.1), channel_id=1, source_target_pairs={{0,96},{8,104},{16,112},{24,120},{32,64},{40,72},{48,80},{56,88},{... | collective-permute-start | bytes 73736 | tf_op jit(solution)/shard_map/ppermute | solution.py:48
  49.9 1.5 %collective-permute-start.7 = (bf16[1,48,256]{2,1,0:T(8,128)(2,1)S(1)}, bf16[1,48,256]{2,1,0:T(8,128)(2,1)S(1)}, u32[]{:S(2)}, u32[]{:S(2)}) collective-permute-start(bf16[1,48,256]{2,1,0:T(8,128)(2,1)S(1)} %add_add_fusion.1), channel_id=1, source_target_pairs={{0,32},{8,40},{16,48},{24,56},{32,0},{40,8},{48,16},{56,24},{64,96... | collective-permute-start | bytes 73736 | tf_op jit(solution)/shard_map/ppermute | solution.py:48
  54.7 4.5 %collective-permute-done.8 = bf16[1,48,256]{2,1,0:T(8,128)(2,1)S(1)} collective-permute-done((bf16[1,48,256]{2,1,0:T(8,128)(2,1)S(1)}, bf16[1,48,256]{2,1,0:T(8,128)(2,1)S(1)}, u32[]{:S(2)}, u32[]{:S(2)}) %collective-permute-start.8) | collective-permute-done | bytes 24608 | tf_op jit(solution)/shard_map/ppermute | solution.py:48
  59.2 2.4 %collective-permute-start.9 = (bf16[4,48,256]{2,1,0:T(8,128)(2,1)S(1)}, bf16[4,48,256]{2,1,0:T(8,128)(2,1)S(1)}, u32[]{:S(2)}, u32[]{:S(2)}) collective-permute-start(bf16[4,48,256]{2,1,0:T(8,128)(2,1)S(1)} %pad_maximum_fusion.4), channel_id=1, source_target_pairs={{0,128},{8,136},{16,144},{24,152},{32,160},{40,168},{48,176},{56,1... | collective-permute-start | bytes 294920 | tf_op jit(solution)/shard_map/ppermute | solution.py:48
  61.6 1.3 %collective-permute-start.22 = (bf16[8,48,256]{2,1,0:T(8,128)(2,1)S(1)}, bf16[8,48,256]{2,1,0:T(8,128)(2,1)S(1)}, u32[]{:S(2)}, u32[]{:S(2)}) collective-permute-start(bf16[8,48,256]{2,1,0:T(8,128)(2,1)S(1)} %pad_maximum_fusion.3), channel_id=1, source_target_pairs={{0,128},{8,136},{16,144},{24,152},{32,160},{40,168},{48,176},{56,1... | collective-permute-start | bytes 589832 | tf_op jit(solution)/shard_map/ppermute | solution.py:48
  62.9 2.4 %collective-permute-done.9 = bf16[4,48,256]{2,1,0:T(8,128)(2,1)S(1)} collective-permute-done((bf16[4,48,256]{2,1,0:T(8,128)(2,1)S(1)}, bf16[4,48,256]{2,1,0:T(8,128)(2,1)S(1)}, u32[]{:S(2)}, u32[]{:S(2)}) %collective-permute-start.9) | collective-permute-done | bytes 98336 | tf_op jit(solution)/shard_map/ppermute | solution.py:48
  66.5 2.3 %collective-permute-done.22 = bf16[8,48,256]{2,1,0:T(8,128)(2,1)S(1)} collective-permute-done((bf16[8,48,256]{2,1,0:T(8,128)(2,1)S(1)}, bf16[8,48,256]{2,1,0:T(8,128)(2,1)S(1)}, u32[]{:S(2)}, u32[]{:S(2)}) %collective-permute-start.22) | collective-permute-done | bytes 196640 | tf_op jit(solution)/shard_map/ppermute | solution.py:48
  69.1 2.1 %collective-permute-done.10 = bf16[8,48,256]{2,1,0:T(8,128)(2,1)S(1)} collective-permute-done((bf16[8,48,256]{2,1,0:T(8,128)(2,1)S(1)}, bf16[8,48,256]{2,1,0:T(8,128)(2,1)S(1)}, u32[]{:S(2)}, u32[]{:S(2)}) %collective-permute-start.10) | collective-permute-done | bytes 196640 | tf_op jit(solution)/shard_map/ppermute | solution.py:48
  71.6 1.7 %collective-permute-done.11.refs_1_ = bf16[16,48,256]{2,1,0:T(8,128)(2,1)S(1)} collective-permute-done((bf16[16,48,256]{2,1,0:T(8,128)(2,1)S(1)}, bf16[16,48,256]{2,1,0:T(8,128)(2,1)S(1)}, u32[]{:S(2)}, u32[]{:S(2)}) %collective-permute-start.11) | collective-permute-done | bytes 393248 | tf_op jit(solution)/shard_map/ppermute | solution.py:48
  74.1 12.2 %shard_map.37 = f32[8,96,256]{2,1,0:T(8,128)} custom-call(f32[1,1]{1,0:T(1,128)S(6)} %div.9.factor_ref, s32[1,1]{1,0:T(1,128)} %bitcast.digit_ref, bf16[16,48,256]{2,1,0:T(8,128)(2,1)} %copy-done.2, bf16[16,48,256]{2,1,0:T(8,128)(2,1)} %copy-done.4, bf16[16,48,256]{2,1,0:T(8,128)(2,1)} %copy-done.1, bf16[16,48,256]{2,1,0:T(8,128)(2,1)} %copy-done.3, ...), custom_call_target="tpu_custom_call" | custom-call | tf_op jit(solution)/shard_map/pallas_call | solution.py:110
  86.3 17.8 %all_to_all.5 = f32[8,96,256]{2,1,0:T(8,128)S(1)} all-to-all(f32[8,96,256]{2,1,0:T(8,128)} %shard_map.37), channel_id=1, replica_groups=mesh['chan'=32,'win'=8] {'win'}, dimensions={0} | all-to-all | bytes 1572864 | tf_op jit(solution)/shard_map/all_to_all | solution.py:155
  (76 shorter events, 13.3 us)
Async XLA Ops:
  8.4 1.8 %collective-permute-start.12 = (bf16[16,48,256]{2,1,0:T(8,128)(2,1)S(1)}, bf16[16,48,256]{2,1,0:T(8,128)(2,1)S(1)}, u32[]{:S(2)}, u32[]{:S(2)}) collective-permute-start(bf16[16,48,256]{2,1,0:T(8,128)(2,1)S(1)} %bitcast.72), channel_id=1, source_target_pairs={{0,8},{8,0},{16,24},{24,16},{32,40},{40,32},{48,56},{56,48},{64,72... | collective-permute-start | bytes 1179656 | tf_op jit(solution)/shard_map/ppermute | solution.py:43
  8.6 4.1 %collective-permute-start = (bf16[16,48,256]{2,1,0:T(8,128)(2,1)S(1)}, bf16[16,48,256]{2,1,0:T(8,128)(2,1)S(1)}, u32[]{:S(2)}, u32[]{:S(2)}) collective-permute-start(bf16[16,48,256]{2,1,0:T(8,128)(2,1)S(1)} %bitcast.71), channel_id=1, source_target_pairs={{0,8},{8,0},{16,24},{24,16},{32,40},{40,32},{48,56},{56,48},{64,72... | collective-permute-start | bytes 1179656 | tf_op jit(solution)/shard_map/ppermute | solution.py:43
  10.4 8.5 %collective-permute-start.13 = (bf16[8,48,256]{2,1,0:T(8,128)(2,1)S(1)}, bf16[8,48,256]{2,1,0:T(8,128)(2,1)S(1)}, u32[]{:S(2)}, u32[]{:S(2)}) collective-permute-start(bf16[8,48,256]{2,1,0:T(8,128)(2,1)S(1)} %dynamic-slice_bitcast_fusion), channel_id=1, source_target_pairs={{0,128},{8,136},{16,144},{24,152},{32,160},{40,168},{48,176},{56,1... | collective-permute-start | bytes 589832 | tf_op jit(solution)/shard_map/ppermute | solution.py:43
  12.9 8.0 %collective-permute-start.1 = (bf16[8,48,256]{2,1,0:T(8,128)(2,1)S(1)}, bf16[8,48,256]{2,1,0:T(8,128)(2,1)S(1)}, u32[]{:S(2)}, u32[]{:S(2)}) collective-permute-start(bf16[8,48,256]{2,1,0:T(8,128)(2,1)S(1)} %dynamic-slice_bitcast_fusion.1), channel_id=1, source_target_pairs={{0,16},{8,24},{16,0},{24,8},{32,48},{40,56},{48,32},{56,40},{64,80... | collective-permute-start | bytes 589832 | tf_op jit(solution)/shard_map/ppermute | solution.py:43
  18.9 4.7 %collective-permute-start.14 = (bf16[4,48,256]{2,1,0:T(8,128)(2,1)S(1)}, bf16[4,48,256]{2,1,0:T(8,128)(2,1)S(1)}, u32[]{:S(2)}, u32[]{:S(2)}) collective-permute-start(bf16[4,48,256]{2,1,0:T(8,128)(2,1)S(1)} %dynamic-slice_bitcast_fusion.2), channel_id=1, source_target_pairs={{0,16},{8,24},{16,0},{24,8},{32,48},{40,56},{48,32},{56,40},{64,80... | collective-permute-start | bytes 294920 | tf_op jit(solution)/shard_map/ppermute | solution.py:43
  21.0 11.4 %collective-permute-start.2 = (bf16[4,48,256]{2,1,0:T(8,128)(2,1)S(1)}, bf16[4,48,256]{2,1,0:T(8,128)(2,1)S(1)}, u32[]{:S(2)}, u32[]{:S(2)}) collective-permute-start(bf16[4,48,256]{2,1,0:T(8,128)(2,1)S(1)} %dynamic-slice_bitcast_fusion.3), channel_id=1, source_target_pairs={{0,128},{8,136},{16,144},{24,152},{32,160},{40,168},{48,176},{56,1... | collective-permute-start | bytes 294920 | tf_op jit(solution)/shard_map/ppermute | solution.py:43
  23.7 15.4 %collective-permute-start.15 = (bf16[1,48,256]{2,1,0:T(8,128)(2,1)S(1)}, bf16[1,48,256]{2,1,0:T(8,128)(2,1)S(1)}, u32[]{:S(2)}, u32[]{:S(2)}) collective-permute-start(bf16[1,48,256]{2,1,0:T(8,128)(2,1)S(1)} %get-tuple-element.31), channel_id=1, source_target_pairs={{0,64},{8,72},{16,80},{24,88},{32,96},{40,104},{48,112},{56,120},{... | collective-permute-start | bytes 73736 | tf_op jit(solution)/shard_map/ppermute | solution.py:43
  31.0 8.1 %collective-permute-start.16 = (bf16[1,48,256]{2,1,0:T(8,128)(2,1)S(1)}, bf16[1,48,256]{2,1,0:T(8,128)(2,1)S(1)}, u32[]{:S(2)}, u32[]{:S(2)}) collective-permute-start(bf16[1,48,256]{2,1,0:T(8,128)(2,1)S(1)} %get-tuple-element.33), channel_id=1, source_target_pairs={{0,32},{8,40},{16,48},{24,56},{32,0},{40,8},{48,16},{56,24},{64,96... | collective-permute-start | bytes 73736 | tf_op jit(solution)/shard_map/ppermute | solution.py:43
  32.4 6.6 %collective-permute-start.17 = (bf16[1,48,256]{2,1,0:T(8,128)(2,1)S(1)}, bf16[1,48,256]{2,1,0:T(8,128)(2,1)S(1)}, u32[]{:S(2)}, u32[]{:S(2)}) collective-permute-start(bf16[1,48,256]{2,1,0:T(8,128)(2,1)S(1)} %get-tuple-element.32), channel_id=1, source_target_pairs={{0,96},{8,104},{16,112},{24,120},{32,64},{40,72},{48,80},{56,88},{... | collective-permute-start | bytes 73736 | tf_op jit(solution)/shard_map/ppermute | solution.py:43
  32.5 12.3 %collective-permute-start.3 = (bf16[1,48,256]{2,1,0:T(8,128)(2,1)S(1)}, bf16[1,48,256]{2,1,0:T(8,128)(2,1)S(1)}, u32[]{:S(2)}, u32[]{:S(2)}) collective-permute-start(bf16[1,48,256]{2,1,0:T(8,128)(2,1)S(1)} %get-tuple-element.38), channel_id=1, source_target_pairs={{0,64},{8,72},{16,80},{24,88},{32,96},{40,104},{48,112},{56,120},{... | collective-permute-start | bytes 73736 | tf_op jit(solution)/shard_map/ppermute | solution.py:43
  37.6 8.2 %collective-permute-start.4 = (bf16[1,48,256]{2,1,0:T(8,128)(2,1)S(1)}, bf16[1,48,256]{2,1,0:T(8,128)(2,1)S(1)}, u32[]{:S(2)}, u32[]{:S(2)}) collective-permute-start(bf16[1,48,256]{2,1,0:T(8,128)(2,1)S(1)} %get-tuple-element.40), channel_id=1, source_target_pairs={{0,32},{8,40},{16,48},{24,56},{32,0},{40,8},{48,16},{56,24},{64,96... | collective-permute-start | bytes 73736 | tf_op jit(solution)/shard_map/ppermute | solution.py:43
  39.1 6.7 %collective-permute-start.5 = (bf16[1,48,256]{2,1,0:T(8,128)(2,1)S(1)}, bf16[1,48,256]{2,1,0:T(8,128)(2,1)S(1)}, u32[]{:S(2)}, u32[]{:S(2)}) collective-permute-start(bf16[1,48,256]{2,1,0:T(8,128)(2,1)S(1)} %get-tuple-element.39), channel_id=1, source_target_pairs={{0,96},{8,104},{16,112},{24,120},{32,64},{40,72},{48,80},{56,88},{... | collective-permute-start | bytes 73736 | tf_op jit(solution)/shard_map/ppermute | solution.py:43
  39.1 12.3 %collective-permute-start.18 = (bf16[1,48,256]{2,1,0:T(8,128)(2,1)S(1)}, bf16[1,48,256]{2,1,0:T(8,128)(2,1)S(1)}, u32[]{:S(2)}, u32[]{:S(2)}) collective-permute-start(bf16[1,48,256]{2,1,0:T(8,128)(2,1)S(1)} %add_add_fusion), channel_id=1, source_target_pairs={{0,96},{8,104},{16,112},{24,120},{32,64},{40,72},{48,80},{56,88},{... | collective-permute-start | bytes 73736 | tf_op jit(solution)/shard_map/ppermute | solution.py:48
  43.3 9.1 %collective-permute-start.19 = (bf16[1,48,256]{2,1,0:T(8,128)(2,1)S(1)}, bf16[1,48,256]{2,1,0:T(8,128)(2,1)S(1)}, u32[]{:S(2)}, u32[]{:S(2)}) collective-permute-start(bf16[1,48,256]{2,1,0:T(8,128)(2,1)S(1)} %add_add_fusion), channel_id=1, source_target_pairs={{0,32},{8,40},{16,48},{24,56},{32,0},{40,8},{48,16},{56,24},{64,96... | collective-permute-start | bytes 73736 | tf_op jit(solution)/shard_map/ppermute | solution.py:48
  44.8 7.8 %collective-permute-start.20 = (bf16[1,48,256]{2,1,0:T(8,128)(2,1)S(1)}, bf16[1,48,256]{2,1,0:T(8,128)(2,1)S(1)}, u32[]{:S(2)}, u32[]{:S(2)}) collective-permute-start(bf16[1,48,256]{2,1,0:T(8,128)(2,1)S(1)} %add_add_fusion), channel_id=1, source_target_pairs={{0,64},{8,72},{16,80},{24,88},{32,96},{40,104},{48,112},{56,120},{... | collective-permute-start | bytes 73736 | tf_op jit(solution)/shard_map/ppermute | solution.py:48
  45.8 8.1 %collective-permute-start.6 = (bf16[1,48,256]{2,1,0:T(8,128)(2,1)S(1)}, bf16[1,48,256]{2,1,0:T(8,128)(2,1)S(1)}, u32[]{:S(2)}, u32[]{:S(2)}) collective-permute-start(bf16[1,48,256]{2,1,0:T(8,128)(2,1)S(1)} %add_add_fusion.1), channel_id=1, source_target_pairs={{0,96},{8,104},{16,112},{24,120},{32,64},{40,72},{48,80},{56,88},{... | collective-permute-start | bytes 73736 | tf_op jit(solution)/shard_map/ppermute | solution.py:48
  49.9 4.7 %collective-permute-start.7 = (bf16[1,48,256]{2,1,0:T(8,128)(2,1)S(1)}, bf16[1,48,256]{2,1,0:T(8,128)(2,1)S(1)}, u32[]{:S(2)}, u32[]{:S(2)}) collective-permute-start(bf16[1,48,256]{2,1,0:T(8,128)(2,1)S(1)} %add_add_fusion.1), channel_id=1, source_target_pairs={{0,32},{8,40},{16,48},{24,56},{32,0},{40,8},{48,16},{56,24},{64,96... | collective-permute-start | bytes 73736 | tf_op jit(solution)/shard_map/ppermute | solution.py:48
  51.4 7.7 %collective-permute-start.8 = (bf16[1,48,256]{2,1,0:T(8,128)(2,1)S(1)}, bf16[1,48,256]{2,1,0:T(8,128)(2,1)S(1)}, u32[]{:S(2)}, u32[]{:S(2)}) collective-permute-start(bf16[1,48,256]{2,1,0:T(8,128)(2,1)S(1)} %add_add_fusion.1), channel_id=1, source_target_pairs={{0,64},{8,72},{16,80},{24,88},{32,96},{40,104},{48,112},{56,120},{... | collective-permute-start | bytes 73736 | tf_op jit(solution)/shard_map/ppermute | solution.py:48
  52.6 8.9 %collective-permute-start.21 = (bf16[4,48,256]{2,1,0:T(8,128)(2,1)S(1)}, bf16[4,48,256]{2,1,0:T(8,128)(2,1)S(1)}, u32[]{:S(2)}, u32[]{:S(2)}) collective-permute-start(bf16[4,48,256]{2,1,0:T(8,128)(2,1)S(1)} %pad_maximum_fusion.5), channel_id=1, source_target_pairs={{0,16},{8,24},{16,0},{24,8},{32,48},{40,56},{48,32},{56,40},{64,80... | collective-permute-start | bytes 294920 | tf_op jit(solution)/shard_map/ppermute | solution.py:48
  59.2 6.2 %collective-permute-start.9 = (bf16[4,48,256]{2,1,0:T(8,128)(2,1)S(1)}, bf16[4,48,256]{2,1,0:T(8,128)(2,1)S(1)}, u32[]{:S(2)}, u32[]{:S(2)}) collective-permute-start(bf16[4,48,256]{2,1,0:T(8,128)(2,1)S(1)} %pad_maximum_fusion.4), channel_id=1, source_target_pairs={{0,128},{8,136},{16,144},{24,152},{32,160},{40,168},{48,176},{56,1... | collective-permute-start | bytes 294920 | tf_op jit(solution)/shard_map/ppermute | solution.py:48
  61.6 7.3 %collective-permute-start.22 = (bf16[8,48,256]{2,1,0:T(8,128)(2,1)S(1)}, bf16[8,48,256]{2,1,0:T(8,128)(2,1)S(1)}, u32[]{:S(2)}, u32[]{:S(2)}) collective-permute-start(bf16[8,48,256]{2,1,0:T(8,128)(2,1)S(1)} %pad_maximum_fusion.3), channel_id=1, source_target_pairs={{0,128},{8,136},{16,144},{24,152},{32,160},{40,168},{48,176},{56,1... | collective-permute-start | bytes 589832 | tf_op jit(solution)/shard_map/ppermute | solution.py:48
  65.4 5.8 %collective-permute-start.10 = (bf16[8,48,256]{2,1,0:T(8,128)(2,1)S(1)}, bf16[8,48,256]{2,1,0:T(8,128)(2,1)S(1)}, u32[]{:S(2)}, u32[]{:S(2)}) collective-permute-start(bf16[8,48,256]{2,1,0:T(8,128)(2,1)S(1)} %pad_maximum_fusion.2), channel_id=1, source_target_pairs={{0,16},{8,24},{16,0},{24,8},{32,48},{40,56},{48,32},{56,40},{64,80... | collective-permute-start | bytes 589832 | tf_op jit(solution)/shard_map/ppermute | solution.py:48
  69.0 2.6 %collective-permute-start.23 = (bf16[16,48,256]{2,1,0:T(8,128)(2,1)S(1)}, bf16[16,48,256]{2,1,0:T(8,128)(2,1)S(1)}, u32[]{:S(2)}, u32[]{:S(2)}) collective-permute-start(bf16[16,48,256]{2,1,0:T(8,128)(2,1)S(1)} %pad_maximum_fusion.1.refs_2_), channel_id=1, source_target_pairs={{0,8},{8,0},{16,24},{24,16},{32,40},{40,32},{48,56},{56,48},{64,72... | collective-permute-start | bytes 1179656 | tf_op jit(solution)/shard_map/ppermute | solution.py:48
  71.3 2.0 %collective-permute-start.11 = (bf16[16,48,256]{2,1,0:T(8,128)(2,1)S(1)}, bf16[16,48,256]{2,1,0:T(8,128)(2,1)S(1)}, u32[]{:S(2)}, u32[]{:S(2)}) collective-permute-start(bf16[16,48,256]{2,1,0:T(8,128)(2,1)S(1)} %pad_maximum_fusion.refs_0_), channel_id=1, source_target_pairs={{0,8},{8,0},{16,24},{24,16},{32,40},{40,32},{48,56},{56,48},{64,72... | collective-permute-start | bytes 1179656 | tf_op jit(solution)/shard_map/ppermute | solution.py:48
  (5 other events, 15.4 us)

commit v6 on v5

--- a/solution.py
+++ b/solution.py
@@ -31,9 +31,9 @@
     return [(i, i ^ mask) for i in range(size)]
 
 
-def broadcast(masked, me, axis, size, order):
+def broadcast(masked, me, axis, size, order, rider):
     pieces = masked
-    for bits in order:
+    for place, bits in enumerate(order):
         radix = 1 << len(bits)
         quarters = pieces.reshape(radix, pieces.shape[0] // radix, *pieces.shape[1:])
         digit = digit_of(me, bits)
@@ -41,6 +41,8 @@
         for offset in range(1, radix):
             send = lax.dynamic_index_in_dim(quarters, digit ^ offset, 0, keepdims=False)
             pieces = pieces + lax.ppermute(send, axis, xor_pairs(size, flip_mask(bits, offset)))
+        if place == 0:
+            pieces, rider = lax.optimization_barrier((pieces, rider))
     for place, bits in enumerate(reversed(order)):
         radix = 1 << len(bits)
         digit = digit_of(me, bits)
@@ -49,7 +51,7 @@
             for offset in range(1, radix)
         ]
         if place == len(order) - 1 and radix == 2:
-            return got[0], got[1], digit
+            return got[0], got[1], digit, rider
         slots = []
         for slot in range(radix):
             offset = slot ^ digit
@@ -131,25 +133,26 @@
     chan_me = lax.axis_index("chan")
     win_me = lax.axis_index("win")
     signal = traces[0].astype(jnp.float32)
-    whitened = (
-        signal * lax.rsqrt(jnp.mean(signal * signal, axis=-1, keepdims=True) + 1e-06)
-    ).astype(jnp.bfloat16)
+    scale = lax.rsqrt(jnp.mean(signal * signal, axis=-1, keepdims=True) + 1e-06)
+    whitened = (signal * scale).astype(jnp.bfloat16)
     own_flag = window_mask[0, 0].astype(jnp.float32)
-    outgoing = whitened * own_flag.astype(jnp.bfloat16)
+    pieces = traces[0].reshape(chan_dev, chan_size, samples // chan_size).transpose(1, 0, 2)
+    outgoing = (pieces.astype(jnp.float32) * scale[None]).astype(jnp.bfloat16) * own_flag.astype(
+        jnp.bfloat16
+    )
     masked = jnp.concatenate(
         [jnp.where(chan_me == owner[step], outgoing, jnp.zeros_like(outgoing)) for step in range(step_count)],
-        0,
+        1,
     )
-    rows = masked.shape[0]
-    masked = masked.reshape(rows, chan_size, samples // chan_size).transpose(1, 0, 2)
-    half = rows // 2
-    whitened, masked = lax.optimization_barrier((whitened, masked))
+    half = masked.shape[1] // 2
     halves = []
+    rider = whitened
     for which, order in enumerate(CHAN_BITS):
-        mine, other, digit = broadcast(
-            masked[:, which * half : (which + 1) * half], chan_me, "chan", chan_size, order
+        mine, other, digit, rider = broadcast(
+            masked[:, which * half : (which + 1) * half], chan_me, "chan", chan_size, order, rider
         )
         halves.append((mine, other))
+    whitened = rider
     factor = own_flag / math.sqrt(samples)
     complete = correlate(halves, digit, whitened, factor, win_size)
     reduced = jnp.sum(lax.all_to_all(complete, "win", 0, 0, tiled=True), 0)

time: 105 us -> 104 us (level)
  local copies, waits for them, and re-layouts: 4.91 us -> 3.74 us
  transfers between devices with their start and end apart: 24 -> 24, of which waited for: 10 -> 10; matrix products, arithmetic and copies ran while one was open for 1% -> 2% of each run, Pallas kernels for 0% -> 0%
where the time goes in v6:
time: 104 us
  starting transfers between devices  44.5 us (43%)
  waiting for transfers between devices  19.1 us (18%)
  blocking collectives  17.8 us (17%)
  Pallas kernels  12.2 us (12%)
  local copies, waits for them, and re-layouts  3.74 us (4%)
  other arithmetic  3.31 us (3%)
  between operations  3 us (3%)
    ppermute x12, starting transfers between devices, broadcast(): lax.ppermute(send, axis, xor_pairs(size, flip_mask(bits, offset)))  24.8 us
    ppermute x12, starting transfers between devices, broadcast(): lax.ppermute(pieces, axis, xor_pairs(size, flip_mask(bits, offset)))  19.7 us
    all_to_all x1, blocking collectives, body(): reduced = jnp.sum(lax.all_to_all(complete, 'win', 0, 0, tiled=True), 0)  17.8 us
    ppermute x12, waiting for transfers between devices, broadcast(): lax.ppermute(pieces, axis, xor_pairs(size, flip_mask(bits, offset)))  14.1 us
    pallas_call x1, Pallas kernels, correlate(): pl.pallas_call(kernel, out_shape=jax.ShapeDtypeStruct((blocks, rows, out_...  12.2 us
    ppermute x12, waiting for transfers between devices, broadcast(): lax.ppermute(send, axis, xor_pairs(size, flip_mask(bits, offset)))  5.03 us
  transfers between devices with their start and end apart: 24, of which 10 were waited for; matrix products, arithmetic and copies ran while one was open for 2% of the time, Pallas kernels for 0%

profile of v6, /device:TPU:8, one launch (start us, length us, event | category | flops | bytes accessed | tf_op | source)
XLA Modules:
  0.0 103.6 jit_solution(2061343951730218819)
XLA Ops:
  0.0 1.4 %fusion.7 = (s32[1]{0:T(128)}, s32[1]{0:T(128)}, s32[1]{0:T(128)}) fusion(s32[3]{0:T(128)} %param.4), kind=kLoop, calls=%fused_computation.61 | loop fusion | bytes 24 | tf_op jit(solution)/shard_map/slice | solution.py:144
  2.8 1.3 %fusion.1 = f32[32]{0:T(128)S(1)} fusion(bf16[1,32,8192]{2,1,0:T(8,128)(2,1)} %param.3), kind=kLoop, calls=%fused_computation.4 | loop fusion | flops 786400 | bytes 524416 | tf_op jit(solution)/shard_map/reduce_sum | solution.py:136
  8.9 2.4 %collective-permute-start.13 = (bf16[8,48,256]{2,1,0:T(8,128)(2,1)S(1)}, bf16[8,48,256]{2,1,0:T(8,128)(2,1)S(1)}, u32[]{:S(2)}, u32[]{:S(2)}) collective-permute-start(bf16[8,48,256]{2,1,0:T(8,128)(2,1)S(1)} %dynamic-slice_bitcast_fusion), channel_id=1, source_target_pairs={{0,128},{8,136},{16,144},{24,152},{32,160},{40,168},{48,176},{56,1... | collective-permute-start | bytes 589832 | tf_op jit(solution)/shard_map/ppermute | solution.py:43
  11.3 2.0 %collective-permute-start.1 = (bf16[8,48,256]{2,1,0:T(8,128)(2,1)S(1)}, bf16[8,48,256]{2,1,0:T(8,128)(2,1)S(1)}, u32[]{:S(2)}, u32[]{:S(2)}) collective-permute-start(bf16[8,48,256]{2,1,0:T(8,128)(2,1)S(1)} %dynamic-slice_bitcast_fusion.1), channel_id=1, source_target_pairs={{0,16},{8,24},{16,0},{24,8},{32,48},{40,56},{48,32},{56,40},{64,80... | collective-permute-start | bytes 589832 | tf_op jit(solution)/shard_map/ppermute | solution.py:43
  13.3 4.1 %collective-permute-done.13 = bf16[8,48,256]{2,1,0:T(8,128)(2,1)S(1)} collective-permute-done((bf16[8,48,256]{2,1,0:T(8,128)(2,1)S(1)}, bf16[8,48,256]{2,1,0:T(8,128)(2,1)S(1)}, u32[]{:S(2)}, u32[]{:S(2)}) %collective-permute-start.13) | collective-permute-done | bytes 196640 | tf_op jit(solution)/shard_map/ppermute | solution.py:43
  17.5 2.0 %collective-permute-start.14 = (bf16[4,48,256]{2,1,0:T(8,128)(2,1)S(1)}, bf16[4,48,256]{2,1,0:T(8,128)(2,1)S(1)}, u32[]{:S(2)}, u32[]{:S(2)}) collective-permute-start(bf16[4,48,256]{2,1,0:T(8,128)(2,1)S(1)} %dynamic-slice_bitcast_fusion.2), channel_id=1, source_target_pairs={{0,16},{8,24},{16,0},{24,8},{32,48},{40,56},{48,32},{56,40},{64,80... | collective-permute-start | bytes 294920 | tf_op jit(solution)/shard_map/ppermute | solution.py:43
  19.6 2.4 %collective-permute-start.2 = (bf16[4,48,256]{2,1,0:T(8,128)(2,1)S(1)}, bf16[4,48,256]{2,1,0:T(8,128)(2,1)S(1)}, u32[]{:S(2)}, u32[]{:S(2)}) collective-permute-start(bf16[4,48,256]{2,1,0:T(8,128)(2,1)S(1)} %dynamic-slice_bitcast_fusion.3), channel_id=1, source_target_pairs={{0,128},{8,136},{16,144},{24,152},{32,160},{40,168},{48,176},{56,1... | collective-permute-start | bytes 294920 | tf_op jit(solution)/shard_map/ppermute | solution.py:43
  22.3 7.3 %collective-permute-start.15 = (bf16[1,48,256]{2,1,0:T(8,128)(2,1)S(1)}, bf16[1,48,256]{2,1,0:T(8,128)(2,1)S(1)}, u32[]{:S(2)}, u32[]{:S(2)}) collective-permute-start(bf16[1,48,256]{2,1,0:T(8,128)(2,1)S(1)} %get-tuple-element.35), channel_id=1, source_target_pairs={{0,64},{8,72},{16,80},{24,88},{32,96},{40,104},{48,112},{56,120},{... | collective-permute-start | bytes 73736 | tf_op jit(solution)/shard_map/ppermute | solution.py:43
  29.5 1.5 %collective-permute-start.16 = (bf16[1,48,256]{2,1,0:T(8,128)(2,1)S(1)}, bf16[1,48,256]{2,1,0:T(8,128)(2,1)S(1)}, u32[]{:S(2)}, u32[]{:S(2)}) collective-permute-start(bf16[1,48,256]{2,1,0:T(8,128)(2,1)S(1)} %get-tuple-element.37), channel_id=1, source_target_pairs={{0,32},{8,40},{16,48},{24,56},{32,0},{40,8},{48,16},{56,24},{64,96... | collective-permute-start | bytes 73736 | tf_op jit(solution)/shard_map/ppermute | solution.py:43
  31.0 5.1 %collective-permute-start.3 = (bf16[1,48,256]{2,1,0:T(8,128)(2,1)S(1)}, bf16[1,48,256]{2,1,0:T(8,128)(2,1)S(1)}, u32[]{:S(2)}, u32[]{:S(2)}) collective-permute-start(bf16[1,48,256]{2,1,0:T(8,128)(2,1)S(1)} %get-tuple-element.42), channel_id=1, source_target_pairs={{0,64},{8,72},{16,80},{24,88},{32,96},{40,104},{48,112},{56,120},{... | collective-permute-start | bytes 73736 | tf_op jit(solution)/shard_map/ppermute | solution.py:43
  36.2 1.5 %collective-permute-start.4 = (bf16[1,48,256]{2,1,0:T(8,128)(2,1)S(1)}, bf16[1,48,256]{2,1,0:T(8,128)(2,1)S(1)}, u32[]{:S(2)}, u32[]{:S(2)}) collective-permute-start(bf16[1,48,256]{2,1,0:T(8,128)(2,1)S(1)} %get-tuple-element.44), channel_id=1, source_target_pairs={{0,32},{8,40},{16,48},{24,56},{32,0},{40,8},{48,16},{56,24},{64,96... | collective-permute-start | bytes 73736 | tf_op jit(solution)/shard_map/ppermute | solution.py:43
  37.7 4.2 %collective-permute-start.18 = (bf16[1,48,256]{2,1,0:T(8,128)(2,1)S(1)}, bf16[1,48,256]{2,1,0:T(8,128)(2,1)S(1)}, u32[]{:S(2)}, u32[]{:S(2)}) collective-permute-start(bf16[1,48,256]{2,1,0:T(8,128)(2,1)S(1)} %add_add_fusion), channel_id=1, source_target_pairs={{0,96},{8,104},{16,112},{24,120},{32,64},{40,72},{48,80},{56,88},{... | collective-permute-start | bytes 73736 | tf_op jit(solution)/shard_map/ppermute | solution.py:50
  41.9 1.5 %collective-permute-start.19 = (bf16[1,48,256]{2,1,0:T(8,128)(2,1)S(1)}, bf16[1,48,256]{2,1,0:T(8,128)(2,1)S(1)}, u32[]{:S(2)}, u32[]{:S(2)}) collective-permute-start(bf16[1,48,256]{2,1,0:T(8,128)(2,1)S(1)} %add_add_fusion), channel_id=1, source_target_pairs={{0,32},{8,40},{16,48},{24,56},{32,0},{40,8},{48,16},{56,24},{64,96... | collective-permute-start | bytes 73736 | tf_op jit(solution)/shard_map/ppermute | solution.py:50
  44.4 4.1 %collective-permute-start.6 = (bf16[1,48,256]{2,1,0:T(8,128)(2,1)S(1)}, bf16[1,48,256]{2,1,0:T(8,128)(2,1)S(1)}, u32[]{:S(2)}, u32[]{:S(2)}) collective-permute-start(bf16[1,48,256]{2,1,0:T(8,128)(2,1)S(1)} %add_add_fusion.1), channel_id=1, source_target_pairs={{0,96},{8,104},{16,112},{24,120},{32,64},{40,72},{48,80},{56,88},{... | collective-permute-start | bytes 73736 | tf_op jit(solution)/shard_map/ppermute | solution.py:50
  48.5 1.5 %collective-permute-start.7 = (bf16[1,48,256]{2,1,0:T(8,128)(2,1)S(1)}, bf16[1,48,256]{2,1,0:T(8,128)(2,1)S(1)}, u32[]{:S(2)}, u32[]{:S(2)}) collective-permute-start(bf16[1,48,256]{2,1,0:T(8,128)(2,1)S(1)} %add_add_fusion.1), channel_id=1, source_target_pairs={{0,32},{8,40},{16,48},{24,56},{32,0},{40,8},{48,16},{56,24},{64,96... | collective-permute-start | bytes 73736 | tf_op jit(solution)/shard_map/ppermute | solution.py:50
  53.2 4.5 %collective-permute-done.8 = bf16[1,48,256]{2,1,0:T(8,128)(2,1)S(1)} collective-permute-done((bf16[1,48,256]{2,1,0:T(8,128)(2,1)S(1)}, bf16[1,48,256]{2,1,0:T(8,128)(2,1)S(1)}, u32[]{:S(2)}, u32[]{:S(2)}) %collective-permute-start.8) | collective-permute-done | bytes 24608 | tf_op jit(solution)/shard_map/ppermute | solution.py:50
  57.7 2.4 %collective-permute-start.9 = (bf16[4,48,256]{2,1,0:T(8,128)(2,1)S(1)}, bf16[4,48,256]{2,1,0:T(8,128)(2,1)S(1)}, u32[]{:S(2)}, u32[]{:S(2)}) collective-permute-start(bf16[4,48,256]{2,1,0:T(8,128)(2,1)S(1)} %pad_maximum_fusion.6), channel_id=1, source_target_pairs={{0,128},{8,136},{16,144},{24,152},{32,160},{40,168},{48,176},{56,1... | collective-permute-start | bytes 294920 | tf_op jit(solution)/shard_map/ppermute | solution.py:50
  60.2 1.3 %collective-permute-start.22 = (bf16[8,48,256]{2,1,0:T(8,128)(2,1)S(1)}, bf16[8,48,256]{2,1,0:T(8,128)(2,1)S(1)}, u32[]{:S(2)}, u32[]{:S(2)}) collective-permute-start(bf16[8,48,256]{2,1,0:T(8,128)(2,1)S(1)} %pad_maximum_fusion.5), channel_id=1, source_target_pairs={{0,128},{8,136},{16,144},{24,152},{32,160},{40,168},{48,176},{56,1... | collective-permute-start | bytes 589832 | tf_op jit(solution)/shard_map/ppermute | solution.py:50
  61.5 2.4 %collective-permute-done.9 = bf16[4,48,256]{2,1,0:T(8,128)(2,1)S(1)} collective-permute-done((bf16[4,48,256]{2,1,0:T(8,128)(2,1)S(1)}, bf16[4,48,256]{2,1,0:T(8,128)(2,1)S(1)}, u32[]{:S(2)}, u32[]{:S(2)}) %collective-permute-start.9) | collective-permute-done | bytes 98336 | tf_op jit(solution)/shard_map/ppermute | solution.py:50
  65.1 2.3 %collective-permute-done.22 = bf16[8,48,256]{2,1,0:T(8,128)(2,1)S(1)} collective-permute-done((bf16[8,48,256]{2,1,0:T(8,128)(2,1)S(1)}, bf16[8,48,256]{2,1,0:T(8,128)(2,1)S(1)}, u32[]{:S(2)}, u32[]{:S(2)}) %collective-permute-start.22) | collective-permute-done | bytes 196640 | tf_op jit(solution)/shard_map/ppermute | solution.py:50
  67.6 2.1 %collective-permute-done.10 = bf16[8,48,256]{2,1,0:T(8,128)(2,1)S(1)} collective-permute-done((bf16[8,48,256]{2,1,0:T(8,128)(2,1)S(1)}, bf16[8,48,256]{2,1,0:T(8,128)(2,1)S(1)}, u32[]{:S(2)}, u32[]{:S(2)}) %collective-permute-start.10) | collective-permute-done | bytes 196640 | tf_op jit(solution)/shard_map/ppermute | solution.py:50
  70.2 1.7 %collective-permute-done.11.refs_1_ = bf16[16,48,256]{2,1,0:T(8,128)(2,1)S(1)} collective-permute-done((bf16[16,48,256]{2,1,0:T(8,128)(2,1)S(1)}, bf16[16,48,256]{2,1,0:T(8,128)(2,1)S(1)}, u32[]{:S(2)}, u32[]{:S(2)}) %collective-permute-start.11) | collective-permute-done | bytes 393248 | tf_op jit(solution)/shard_map/ppermute | solution.py:50
  72.7 12.2 %shard_map.37 = f32[8,96,256]{2,1,0:T(8,128)} custom-call(f32[1,1]{1,0:T(1,128)S(6)} %div.9.factor_ref, s32[1,1]{1,0:T(1,128)} %bitcast.digit_ref, bf16[16,48,256]{2,1,0:T(8,128)(2,1)} %copy-done.2, bf16[16,48,256]{2,1,0:T(8,128)(2,1)} %copy-done.4, bf16[16,48,256]{2,1,0:T(8,128)(2,1)} %copy-done.1, bf16[16,48,256]{2,1,0:T(8,128)(2,1)} %copy-done.3, ...), custom_call_target="tpu_custom_call" | custom-call | tf_op jit(solution)/shard_map/pallas_call | solution.py:112
  84.9 17.8 %all_to_all.5 = f32[8,96,256]{2,1,0:T(8,128)S(1)} all-to-all(f32[8,96,256]{2,1,0:T(8,128)} %shard_map.37), channel_id=1, replica_groups=mesh['chan'=32,'win'=8] {'win'}, dimensions={0} | all-to-all | bytes 1572864 | tf_op jit(solution)/shard_map/all_to_all | solution.py:158
  (75 shorter events, 11.7 us)
Async XLA Ops:
  6.2 2.5 %collective-permute-start.12 = (bf16[16,48,256]{2,1,0:T(8,128)(2,1)S(1)}, bf16[16,48,256]{2,1,0:T(8,128)(2,1)S(1)}, u32[]{:S(2)}, u32[]{:S(2)}) collective-permute-start(bf16[16,48,256]{2,1,0:T(8,128)(2,1)S(1)} %bitcast.75), channel_id=1, source_target_pairs={{0,8},{8,0},{16,24},{24,16},{32,40},{40,32},{48,56},{56,48},{64,72... | collective-permute-start | bytes 1179656 | tf_op jit(solution)/shard_map/ppermute | solution.py:43
  6.4 2.1 %collective-permute-start = (bf16[16,48,256]{2,1,0:T(8,128)(2,1)S(1)}, bf16[16,48,256]{2,1,0:T(8,128)(2,1)S(1)}, u32[]{:S(2)}, u32[]{:S(2)}) collective-permute-start(bf16[16,48,256]{2,1,0:T(8,128)(2,1)S(1)} %bitcast.76), channel_id=1, source_target_pairs={{0,8},{8,0},{16,24},{24,16},{32,40},{40,32},{48,56},{56,48},{64,72... | collective-permute-start | bytes 1179656 | tf_op jit(solution)/shard_map/ppermute | solution.py:43
  8.9 8.6 %collective-permute-start.13 = (bf16[8,48,256]{2,1,0:T(8,128)(2,1)S(1)}, bf16[8,48,256]{2,1,0:T(8,128)(2,1)S(1)}, u32[]{:S(2)}, u32[]{:S(2)}) collective-permute-start(bf16[8,48,256]{2,1,0:T(8,128)(2,1)S(1)} %dynamic-slice_bitcast_fusion), channel_id=1, source_target_pairs={{0,128},{8,136},{16,144},{24,152},{32,160},{40,168},{48,176},{56,1... | collective-permute-start | bytes 589832 | tf_op jit(solution)/shard_map/ppermute | solution.py:43
  11.3 8.2 %collective-permute-start.1 = (bf16[8,48,256]{2,1,0:T(8,128)(2,1)S(1)}, bf16[8,48,256]{2,1,0:T(8,128)(2,1)S(1)}, u32[]{:S(2)}, u32[]{:S(2)}) collective-permute-start(bf16[8,48,256]{2,1,0:T(8,128)(2,1)S(1)} %dynamic-slice_bitcast_fusion.1), channel_id=1, source_target_pairs={{0,16},{8,24},{16,0},{24,8},{32,48},{40,56},{48,32},{56,40},{64,80... | collective-permute-start | bytes 589832 | tf_op jit(solution)/shard_map/ppermute | solution.py:43
  17.5 4.7 %collective-permute-start.14 = (bf16[4,48,256]{2,1,0:T(8,128)(2,1)S(1)}, bf16[4,48,256]{2,1,0:T(8,128)(2,1)S(1)}, u32[]{:S(2)}, u32[]{:S(2)}) collective-permute-start(bf16[4,48,256]{2,1,0:T(8,128)(2,1)S(1)} %dynamic-slice_bitcast_fusion.2), channel_id=1, source_target_pairs={{0,16},{8,24},{16,0},{24,8},{32,48},{40,56},{48,32},{56,40},{64,80... | collective-permute-start | bytes 294920 | tf_op jit(solution)/shard_map/ppermute | solution.py:43
  19.6 11.4 %collective-permute-start.2 = (bf16[4,48,256]{2,1,0:T(8,128)(2,1)S(1)}, bf16[4,48,256]{2,1,0:T(8,128)(2,1)S(1)}, u32[]{:S(2)}, u32[]{:S(2)}) collective-permute-start(bf16[4,48,256]{2,1,0:T(8,128)(2,1)S(1)} %dynamic-slice_bitcast_fusion.3), channel_id=1, source_target_pairs={{0,128},{8,136},{16,144},{24,152},{32,160},{40,168},{48,176},{56,1... | collective-permute-start | bytes 294920 | tf_op jit(solution)/shard_map/ppermute | solution.py:43
  22.3 15.4 %collective-permute-start.15 = (bf16[1,48,256]{2,1,0:T(8,128)(2,1)S(1)}, bf16[1,48,256]{2,1,0:T(8,128)(2,1)S(1)}, u32[]{:S(2)}, u32[]{:S(2)}) collective-permute-start(bf16[1,48,256]{2,1,0:T(8,128)(2,1)S(1)} %get-tuple-element.35), channel_id=1, source_target_pairs={{0,64},{8,72},{16,80},{24,88},{32,96},{40,104},{48,112},{56,120},{... | collective-permute-start | bytes 73736 | tf_op jit(solution)/shard_map/ppermute | solution.py:43
  29.5 8.1 %collective-permute-start.16 = (bf16[1,48,256]{2,1,0:T(8,128)(2,1)S(1)}, bf16[1,48,256]{2,1,0:T(8,128)(2,1)S(1)}, u32[]{:S(2)}, u32[]{:S(2)}) collective-permute-start(bf16[1,48,256]{2,1,0:T(8,128)(2,1)S(1)} %get-tuple-element.37), channel_id=1, source_target_pairs={{0,32},{8,40},{16,48},{24,56},{32,0},{40,8},{48,16},{56,24},{64,96... | collective-permute-start | bytes 73736 | tf_op jit(solution)/shard_map/ppermute | solution.py:43
  31.0 6.6 %collective-permute-start.17 = (bf16[1,48,256]{2,1,0:T(8,128)(2,1)S(1)}, bf16[1,48,256]{2,1,0:T(8,128)(2,1)S(1)}, u32[]{:S(2)}, u32[]{:S(2)}) collective-permute-start(bf16[1,48,256]{2,1,0:T(8,128)(2,1)S(1)} %get-tuple-element.36), channel_id=1, source_target_pairs={{0,96},{8,104},{16,112},{24,120},{32,64},{40,72},{48,80},{56,88},{... | collective-permute-start | bytes 73736 | tf_op jit(solution)/shard_map/ppermute | solution.py:43
  31.0 12.3 %collective-permute-start.3 = (bf16[1,48,256]{2,1,0:T(8,128)(2,1)S(1)}, bf16[1,48,256]{2,1,0:T(8,128)(2,1)S(1)}, u32[]{:S(2)}, u32[]{:S(2)}) collective-permute-start(bf16[1,48,256]{2,1,0:T(8,128)(2,1)S(1)} %get-tuple-element.42), channel_id=1, source_target_pairs={{0,64},{8,72},{16,80},{24,88},{32,96},{40,104},{48,112},{56,120},{... | collective-permute-start | bytes 73736 | tf_op jit(solution)/shard_map/ppermute | solution.py:43
  36.2 8.2 %collective-permute-start.4 = (bf16[1,48,256]{2,1,0:T(8,128)(2,1)S(1)}, bf16[1,48,256]{2,1,0:T(8,128)(2,1)S(1)}, u32[]{:S(2)}, u32[]{:S(2)}) collective-permute-start(bf16[1,48,256]{2,1,0:T(8,128)(2,1)S(1)} %get-tuple-element.44), channel_id=1, source_target_pairs={{0,32},{8,40},{16,48},{24,56},{32,0},{40,8},{48,16},{56,24},{64,96... | collective-permute-start | bytes 73736 | tf_op jit(solution)/shard_map/ppermute | solution.py:43
  37.6 6.7 %collective-permute-start.5 = (bf16[1,48,256]{2,1,0:T(8,128)(2,1)S(1)}, bf16[1,48,256]{2,1,0:T(8,128)(2,1)S(1)}, u32[]{:S(2)}, u32[]{:S(2)}) collective-permute-start(bf16[1,48,256]{2,1,0:T(8,128)(2,1)S(1)} %get-tuple-element.43), channel_id=1, source_target_pairs={{0,96},{8,104},{16,112},{24,120},{32,64},{40,72},{48,80},{56,88},{... | collective-permute-start | bytes 73736 | tf_op jit(solution)/shard_map/ppermute | solution.py:43
  37.7 12.3 %collective-permute-start.18 = (bf16[1,48,256]{2,1,0:T(8,128)(2,1)S(1)}, bf16[1,48,256]{2,1,0:T(8,128)(2,1)S(1)}, u32[]{:S(2)}, u32[]{:S(2)}) collective-permute-start(bf16[1,48,256]{2,1,0:T(8,128)(2,1)S(1)} %add_add_fusion), channel_id=1, source_target_pairs={{0,96},{8,104},{16,112},{24,120},{32,64},{40,72},{48,80},{56,88},{... | collective-permute-start | bytes 73736 | tf_op jit(solution)/shard_map/ppermute | solution.py:50
  41.9 9.1 %collective-permute-start.19 = (bf16[1,48,256]{2,1,0:T(8,128)(2,1)S(1)}, bf16[1,48,256]{2,1,0:T(8,128)(2,1)S(1)}, u32[]{:S(2)}, u32[]{:S(2)}) collective-permute-start(bf16[1,48,256]{2,1,0:T(8,128)(2,1)S(1)} %add_add_fusion), channel_id=1, source_target_pairs={{0,32},{8,40},{16,48},{24,56},{32,0},{40,8},{48,16},{56,24},{64,96... | collective-permute-start | bytes 73736 | tf_op jit(solution)/shard_map/ppermute | solution.py:50
  43.3 7.8 %collective-permute-start.20 = (bf16[1,48,256]{2,1,0:T(8,128)(2,1)S(1)}, bf16[1,48,256]{2,1,0:T(8,128)(2,1)S(1)}, u32[]{:S(2)}, u32[]{:S(2)}) collective-permute-start(bf16[1,48,256]{2,1,0:T(8,128)(2,1)S(1)} %add_add_fusion), channel_id=1, source_target_pairs={{0,64},{8,72},{16,80},{24,88},{32,96},{40,104},{48,112},{56,120},{... | collective-permute-start | bytes 73736 | tf_op jit(solution)/shard_map/ppermute | solution.py:50
  44.4 8.1 %collective-permute-start.6 = (bf16[1,48,256]{2,1,0:T(8,128)(2,1)S(1)}, bf16[1,48,256]{2,1,0:T(8,128)(2,1)S(1)}, u32[]{:S(2)}, u32[]{:S(2)}) collective-permute-start(bf16[1,48,256]{2,1,0:T(8,128)(2,1)S(1)} %add_add_fusion.1), channel_id=1, source_target_pairs={{0,96},{8,104},{16,112},{24,120},{32,64},{40,72},{48,80},{56,88},{... | collective-permute-start | bytes 73736 | tf_op jit(solution)/shard_map/ppermute | solution.py:50
  48.5 4.7 %collective-permute-start.7 = (bf16[1,48,256]{2,1,0:T(8,128)(2,1)S(1)}, bf16[1,48,256]{2,1,0:T(8,128)(2,1)S(1)}, u32[]{:S(2)}, u32[]{:S(2)}) collective-permute-start(bf16[1,48,256]{2,1,0:T(8,128)(2,1)S(1)} %add_add_fusion.1), channel_id=1, source_target_pairs={{0,32},{8,40},{16,48},{24,56},{32,0},{40,8},{48,16},{56,24},{64,96... | collective-permute-start | bytes 73736 | tf_op jit(solution)/shard_map/ppermute | solution.py:50
  49.9 7.7 %collective-permute-start.8 = (bf16[1,48,256]{2,1,0:T(8,128)(2,1)S(1)}, bf16[1,48,256]{2,1,0:T(8,128)(2,1)S(1)}, u32[]{:S(2)}, u32[]{:S(2)}) collective-permute-start(bf16[1,48,256]{2,1,0:T(8,128)(2,1)S(1)} %add_add_fusion.1), channel_id=1, source_target_pairs={{0,64},{8,72},{16,80},{24,88},{32,96},{40,104},{48,112},{56,120},{... | collective-permute-start | bytes 73736 | tf_op jit(solution)/shard_map/ppermute | solution.py:50
  51.2 8.9 %collective-permute-start.21 = (bf16[4,48,256]{2,1,0:T(8,128)(2,1)S(1)}, bf16[4,48,256]{2,1,0:T(8,128)(2,1)S(1)}, u32[]{:S(2)}, u32[]{:S(2)}) collective-permute-start(bf16[4,48,256]{2,1,0:T(8,128)(2,1)S(1)} %pad_maximum_fusion.7), channel_id=1, source_target_pairs={{0,16},{8,24},{16,0},{24,8},{32,48},{40,56},{48,32},{56,40},{64,80... | collective-permute-start | bytes 294920 | tf_op jit(solution)/shard_map/ppermute | solution.py:50
  57.7 6.2 %collective-permute-start.9 = (bf16[4,48,256]{2,1,0:T(8,128)(2,1)S(1)}, bf16[4,48,256]{2,1,0:T(8,128)(2,1)S(1)}, u32[]{:S(2)}, u32[]{:S(2)}) collective-permute-start(bf16[4,48,256]{2,1,0:T(8,128)(2,1)S(1)} %pad_maximum_fusion.6), channel_id=1, source_target_pairs={{0,128},{8,136},{16,144},{24,152},{32,160},{40,168},{48,176},{56,1... | collective-permute-start | bytes 294920 | tf_op jit(solution)/shard_map/ppermute | solution.py:50
  60.2 7.3 %collective-permute-start.22 = (bf16[8,48,256]{2,1,0:T(8,128)(2,1)S(1)}, bf16[8,48,256]{2,1,0:T(8,128)(2,1)S(1)}, u32[]{:S(2)}, u32[]{:S(2)}) collective-permute-start(bf16[8,48,256]{2,1,0:T(8,128)(2,1)S(1)} %pad_maximum_fusion.5), channel_id=1, source_target_pairs={{0,128},{8,136},{16,144},{24,152},{32,160},{40,168},{48,176},{56,1... | collective-permute-start | bytes 589832 | tf_op jit(solution)/shard_map/ppermute | solution.py:50
  64.0 5.8 %collective-permute-start.10 = (bf16[8,48,256]{2,1,0:T(8,128)(2,1)S(1)}, bf16[8,48,256]{2,1,0:T(8,128)(2,1)S(1)}, u32[]{:S(2)}, u32[]{:S(2)}) collective-permute-start(bf16[8,48,256]{2,1,0:T(8,128)(2,1)S(1)} %pad_maximum_fusion.4), channel_id=1, source_target_pairs={{0,16},{8,24},{16,0},{24,8},{32,48},{40,56},{48,32},{56,40},{64,80... | collective-permute-start | bytes 589832 | tf_op jit(solution)/shard_map/ppermute | solution.py:50
  67.5 2.7 %collective-permute-start.23 = (bf16[16,48,256]{2,1,0:T(8,128)(2,1)S(1)}, bf16[16,48,256]{2,1,0:T(8,128)(2,1)S(1)}, u32[]{:S(2)}, u32[]{:S(2)}) collective-permute-start(bf16[16,48,256]{2,1,0:T(8,128)(2,1)S(1)} %pad_maximum_fusion.3.refs_2_), channel_id=1, source_target_pairs={{0,8},{8,0},{16,24},{24,16},{32,40},{40,32},{48,56},{56,48},{64,72... | collective-permute-start | bytes 1179656 | tf_op jit(solution)/shard_map/ppermute | solution.py:50
  69.9 2.0 %collective-permute-start.11 = (bf16[16,48,256]{2,1,0:T(8,128)(2,1)S(1)}, bf16[16,48,256]{2,1,0:T(8,128)(2,1)S(1)}, u32[]{:S(2)}, u32[]{:S(2)}) collective-permute-start(bf16[16,48,256]{2,1,0:T(8,128)(2,1)S(1)} %pad_maximum_fusion.2.refs_0_), channel_id=1, source_target_pairs={{0,8},{8,0},{16,24},{24,16},{32,40},{40,32},{48,56},{56,48},{64,72... | collective-permute-start | bytes 1179656 | tf_op jit(solution)/shard_map/ppermute | solution.py:50
  (5 other events, 10.8 us)

commit v7 on v6

--- a/solution.py
+++ b/solution.py
@@ -10,7 +10,7 @@
 LAGS = 64
 EDGE = 128
 TIME_BLOCK = 2048
-CHAN_BITS = (((0,), (1,), (4,), (2, 3)), ((0,), (4,), (1,), (2, 3)))
+CHAN_BITS = (((0,), (1, 4), (2, 3)), ((0,), (1, 4), (2, 3)))
 
 def digit_of(me, bits):
     digit = 0

time: 104 us -> 99.3 us (0.955)
  waiting for transfers between devices: 19.1 us -> 9.56 us
  starting transfers between devices: 44.5 us -> 48.6 us
  local copies, waits for them, and re-layouts: 3.74 us -> 4.96 us
    ppermute x12 -> x14, waiting for transfers between devices: 14.1 us -> 7.12 us  [broadcast(): lax.ppermute(pieces, axis, xor_pairs(size, flip_mask(bits, offset)))]
    ppermute x12 -> x14, starting transfers between devices: 19.7 us -> 23.8 us  [broadcast(): lax.ppermute(pieces, axis, xor_pairs(size, flip_mask(bits, offset)))]
    ppermute x12 -> x14, waiting for transfers between devices: 5.03 us -> 2.44 us  [broadcast(): lax.ppermute(send, axis, xor_pairs(size, flip_mask(bits, offset)))]
    ppermute x12 -> x14, starting transfers between devices: 24.8 us -> 24.8 us  [broadcast(): lax.ppermute(send, axis, xor_pairs(size, flip_mask(bits, offset)))]
  transfers between devices with their start and end apart: 24 -> 28, of which waited for: 10 -> 6; matrix products, arithmetic and copies ran while one was open for 2% -> 2% of each run, Pallas kernels for 0% -> 0%
where the time goes in v7:
time: 99.3 us; the launch traced here: 99 us
  starting transfers between devices  48.6 us (49%)
  blocking collectives  17.8 us (18%)
  Pallas kernels  12.2 us (12%)
  waiting for transfers between devices  9.56 us (10%)
  local copies, waits for them, and re-layouts  4.96 us (5%)
  other arithmetic  3.13 us (3%)
  between operations  2.81 us (3%)
    ppermute x14, starting transfers between devices, broadcast(): lax.ppermute(send, axis, xor_pairs(size, flip_mask(bits, offset)))  24.8 us
    ppermute x14, starting transfers between devices, broadcast(): lax.ppermute(pieces, axis, xor_pairs(size, flip_mask(bits, offset)))  23.8 us
    all_to_all x1, blocking collectives, body(): reduced = jnp.sum(lax.all_to_all(complete, 'win', 0, 0, tiled=True), 0)  17.8 us
    pallas_call x1, Pallas kernels, correlate(): pl.pallas_call(kernel, out_shape=jax.ShapeDtypeStruct((blocks, rows, out_...  12.2 us
    ppermute x14, waiting for transfers between devices, broadcast(): lax.ppermute(pieces, axis, xor_pairs(size, flip_mask(bits, offset)))  7.12 us
    ppermute x14, waiting for transfers between devices, broadcast(): lax.ppermute(send, axis, xor_pairs(size, flip_mask(bits, offset)))  2.44 us
  transfers between devices with their start and end apart: 28, of which 6 were waited for; matrix products, arithmetic and copies ran while one was open for 2% of the time, Pallas kernels for 0%

profile of v7, /device:TPU:8, one launch (start us, length us, event | category | flops | bytes accessed | tf_op | source)
XLA Modules:
  0.0 99.0 jit_solution(16951811216857586494)
XLA Ops:
  0.0 1.4 %fusion.9 = (s32[1]{0:T(128)}, s32[1]{0:T(128)}, s32[1]{0:T(128)}) fusion(s32[3]{0:T(128)} %param.4), kind=kLoop, calls=%fused_computation.57 | loop fusion | bytes 24 | tf_op jit(solution)/shard_map/slice | solution.py:144
  9.5 2.4 %collective-permute-start.15 = (bf16[4,48,256]{2,1,0:T(8,128)(2,1)S(1)}, bf16[4,48,256]{2,1,0:T(8,128)(2,1)S(1)}, u32[]{:S(2)}, u32[]{:S(2)}) collective-permute-start(bf16[4,48,256]{2,1,0:T(8,128)(2,1)S(1)} %get-tuple-element.23), channel_id=1, source_target_pairs={{0,128},{8,136},{16,144},{24,152},{32,160},{40,168},{48,176},{56,1... | collective-permute-start | bytes 294920 | tf_op jit(solution)/shard_map/ppermute | solution.py:43
  11.9 1.9 %collective-permute-start.16 = (bf16[4,48,256]{2,1,0:T(8,128)(2,1)S(1)}, bf16[4,48,256]{2,1,0:T(8,128)(2,1)S(1)}, u32[]{:S(2)}, u32[]{:S(2)}) collective-permute-start(bf16[4,48,256]{2,1,0:T(8,128)(2,1)S(1)} %get-tuple-element.25), channel_id=1, source_target_pairs={{0,16},{8,24},{16,0},{24,8},{32,48},{40,56},{48,32},{56,40},{64,80... | collective-permute-start | bytes 294920 | tf_op jit(solution)/shard_map/ppermute | solution.py:43
  14.6 2.4 %collective-permute-start.1 = (bf16[4,48,256]{2,1,0:T(8,128)(2,1)S(1)}, bf16[4,48,256]{2,1,0:T(8,128)(2,1)S(1)}, u32[]{:S(2)}, u32[]{:S(2)}) collective-permute-start(bf16[4,48,256]{2,1,0:T(8,128)(2,1)S(1)} %get-tuple-element.30), channel_id=1, source_target_pairs={{0,128},{8,136},{16,144},{24,152},{32,160},{40,168},{48,176},{56,1... | collective-permute-start | bytes 294920 | tf_op jit(solution)/shard_map/ppermute | solution.py:43
  17.0 1.9 %collective-permute-start.2 = (bf16[4,48,256]{2,1,0:T(8,128)(2,1)S(1)}, bf16[4,48,256]{2,1,0:T(8,128)(2,1)S(1)}, u32[]{:S(2)}, u32[]{:S(2)}) collective-permute-start(bf16[4,48,256]{2,1,0:T(8,128)(2,1)S(1)} %get-tuple-element.32), channel_id=1, source_target_pairs={{0,16},{8,24},{16,0},{24,8},{32,48},{40,56},{48,32},{56,40},{64,80... | collective-permute-start | bytes 294920 | tf_op jit(solution)/shard_map/ppermute | solution.py:43
  19.8 2.0 %collective-permute-done.17 = bf16[4,48,256]{2,1,0:T(8,128)(2,1)S(1)} collective-permute-done((bf16[4,48,256]{2,1,0:T(8,128)(2,1)S(1)}, bf16[4,48,256]{2,1,0:T(8,128)(2,1)S(1)}, u32[]{:S(2)}, u32[]{:S(2)}) %collective-permute-start.17) | collective-permute-done | bytes 98336 | tf_op jit(solution)/shard_map/ppermute | solution.py:43
  21.8 5.9 %collective-permute-start.18 = (bf16[1,48,256]{2,1,0:T(8,128)(2,1)S(1)}, bf16[1,48,256]{2,1,0:T(8,128)(2,1)S(1)}, u32[]{:S(2)}, u32[]{:S(2)}) collective-permute-start(bf16[1,48,256]{2,1,0:T(8,128)(2,1)S(1)} %get-tuple-element.37), channel_id=1, source_target_pairs={{0,64},{8,72},{16,80},{24,88},{32,96},{40,104},{48,112},{56,120},{... | collective-permute-start | bytes 73736 | tf_op jit(solution)/shard_map/ppermute | solution.py:43
  27.8 1.5 %collective-permute-start.19 = (bf16[1,48,256]{2,1,0:T(8,128)(2,1)S(1)}, bf16[1,48,256]{2,1,0:T(8,128)(2,1)S(1)}, u32[]{:S(2)}, u32[]{:S(2)}) collective-permute-start(bf16[1,48,256]{2,1,0:T(8,128)(2,1)S(1)} %get-tuple-element.39), channel_id=1, source_target_pairs={{0,32},{8,40},{16,48},{24,56},{32,0},{40,8},{48,16},{56,24},{64,96... | collective-permute-start | bytes 73736 | tf_op jit(solution)/shard_map/ppermute | solution.py:43
  29.3 5.1 %collective-permute-start.4 = (bf16[1,48,256]{2,1,0:T(8,128)(2,1)S(1)}, bf16[1,48,256]{2,1,0:T(8,128)(2,1)S(1)}, u32[]{:S(2)}, u32[]{:S(2)}) collective-permute-start(bf16[1,48,256]{2,1,0:T(8,128)(2,1)S(1)} %get-tuple-element.44), channel_id=1, source_target_pairs={{0,64},{8,72},{16,80},{24,88},{32,96},{40,104},{48,112},{56,120},{... | collective-permute-start | bytes 73736 | tf_op jit(solution)/shard_map/ppermute | solution.py:43
  34.4 1.5 %collective-permute-start.5 = (bf16[1,48,256]{2,1,0:T(8,128)(2,1)S(1)}, bf16[1,48,256]{2,1,0:T(8,128)(2,1)S(1)}, u32[]{:S(2)}, u32[]{:S(2)}) collective-permute-start(bf16[1,48,256]{2,1,0:T(8,128)(2,1)S(1)} %get-tuple-element.46), channel_id=1, source_target_pairs={{0,32},{8,40},{16,48},{24,56},{32,0},{40,8},{48,16},{56,24},{64,96... | collective-permute-start | bytes 73736 | tf_op jit(solution)/shard_map/ppermute | solution.py:43
  35.9 4.2 %collective-permute-start.21 = (bf16[1,48,256]{2,1,0:T(8,128)(2,1)S(1)}, bf16[1,48,256]{2,1,0:T(8,128)(2,1)S(1)}, u32[]{:S(2)}, u32[]{:S(2)}) collective-permute-start(bf16[1,48,256]{2,1,0:T(8,128)(2,1)S(1)} %add_add_fusion), channel_id=1, source_target_pairs={{0,96},{8,104},{16,112},{24,120},{32,64},{40,72},{48,80},{56,88},{... | collective-permute-start | bytes 73736 | tf_op jit(solution)/shard_map/ppermute | solution.py:50
  40.1 1.5 %collective-permute-start.22 = (bf16[1,48,256]{2,1,0:T(8,128)(2,1)S(1)}, bf16[1,48,256]{2,1,0:T(8,128)(2,1)S(1)}, u32[]{:S(2)}, u32[]{:S(2)}) collective-permute-start(bf16[1,48,256]{2,1,0:T(8,128)(2,1)S(1)} %add_add_fusion), channel_id=1, source_target_pairs={{0,32},{8,40},{16,48},{24,56},{32,0},{40,8},{48,16},{56,24},{64,96... | collective-permute-start | bytes 73736 | tf_op jit(solution)/shard_map/ppermute | solution.py:50
  42.6 4.1 %collective-permute-start.7 = (bf16[1,48,256]{2,1,0:T(8,128)(2,1)S(1)}, bf16[1,48,256]{2,1,0:T(8,128)(2,1)S(1)}, u32[]{:S(2)}, u32[]{:S(2)}) collective-permute-start(bf16[1,48,256]{2,1,0:T(8,128)(2,1)S(1)} %add_add_fusion.1), channel_id=1, source_target_pairs={{0,96},{8,104},{16,112},{24,120},{32,64},{40,72},{48,80},{56,88},{... | collective-permute-start | bytes 73736 | tf_op jit(solution)/shard_map/ppermute | solution.py:50
  46.7 1.5 %collective-permute-start.8 = (bf16[1,48,256]{2,1,0:T(8,128)(2,1)S(1)}, bf16[1,48,256]{2,1,0:T(8,128)(2,1)S(1)}, u32[]{:S(2)}, u32[]{:S(2)}) collective-permute-start(bf16[1,48,256]{2,1,0:T(8,128)(2,1)S(1)} %add_add_fusion.1), channel_id=1, source_target_pairs={{0,32},{8,40},{16,48},{24,56},{32,0},{40,8},{48,16},{56,24},{64,96... | collective-permute-start | bytes 73736 | tf_op jit(solution)/shard_map/ppermute | solution.py:50
  49.5 2.2 %collective-permute-start.24 = (bf16[4,48,256]{2,1,0:T(8,128)(2,1)S(1)}, bf16[4,48,256]{2,1,0:T(8,128)(2,1)S(1)}, u32[]{:S(2)}, u32[]{:S(2)}) collective-permute-start(bf16[4,48,256]{2,1,0:T(8,128)(2,1)S(1)} %pad_maximum_fusion.5), channel_id=1, source_target_pairs={{0,144},{8,152},{16,128},{24,136},{32,176},{40,184},{48,160},{56,1... | collective-permute-start | bytes 294920 | tf_op jit(solution)/shard_map/ppermute | solution.py:50
  52.6 1.9 %collective-permute-start.26 = (bf16[4,48,256]{2,1,0:T(8,128)(2,1)S(1)}, bf16[4,48,256]{2,1,0:T(8,128)(2,1)S(1)}, u32[]{:S(2)}, u32[]{:S(2)}) collective-permute-start(bf16[4,48,256]{2,1,0:T(8,128)(2,1)S(1)} %pad_maximum_fusion.5), channel_id=1, source_target_pairs={{0,128},{8,136},{16,144},{24,152},{32,160},{40,168},{48,176},{56,1... | collective-permute-start | bytes 294920 | tf_op jit(solution)/shard_map/ppermute | solution.py:50
  54.5 1.4 %collective-permute-done.9 = bf16[1,48,256]{2,1,0:T(8,128)(2,1)S(1)} collective-permute-done((bf16[1,48,256]{2,1,0:T(8,128)(2,1)S(1)}, bf16[1,48,256]{2,1,0:T(8,128)(2,1)S(1)}, u32[]{:S(2)}, u32[]{:S(2)}) %collective-permute-start.9) | collective-permute-done | bytes 24608 | tf_op jit(solution)/shard_map/ppermute | solution.py:50
  56.0 2.2 %collective-permute-start.10 = (bf16[4,48,256]{2,1,0:T(8,128)(2,1)S(1)}, bf16[4,48,256]{2,1,0:T(8,128)(2,1)S(1)}, u32[]{:S(2)}, u32[]{:S(2)}) collective-permute-start(bf16[4,48,256]{2,1,0:T(8,128)(2,1)S(1)} %pad_maximum_fusion.4), channel_id=1, source_target_pairs={{0,144},{8,152},{16,128},{24,136},{32,176},{40,184},{48,160},{56,1... | collective-permute-start | bytes 294920 | tf_op jit(solution)/shard_map/ppermute | solution.py:50
  59.2 1.8 %collective-permute-start.12 = (bf16[4,48,256]{2,1,0:T(8,128)(2,1)S(1)}, bf16[4,48,256]{2,1,0:T(8,128)(2,1)S(1)}, u32[]{:S(2)}, u32[]{:S(2)}) collective-permute-start(bf16[4,48,256]{2,1,0:T(8,128)(2,1)S(1)} %pad_maximum_fusion.4), channel_id=1, source_target_pairs={{0,128},{8,136},{16,144},{24,152},{32,160},{40,168},{48,176},{56,1... | collective-permute-start | bytes 294920 | tf_op jit(solution)/shard_map/ppermute | solution.py:50
  61.3 1.8 %collective-permute-done.10 = bf16[4,48,256]{2,1,0:T(8,128)(2,1)S(1)} collective-permute-done((bf16[4,48,256]{2,1,0:T(8,128)(2,1)S(1)}, bf16[4,48,256]{2,1,0:T(8,128)(2,1)S(1)}, u32[]{:S(2)}, u32[]{:S(2)}) %collective-permute-start.10) | collective-permute-done | bytes 98336 | tf_op jit(solution)/shard_map/ppermute | solution.py:50
  63.1 2.3 %collective-permute-done.12 = bf16[4,48,256]{2,1,0:T(8,128)(2,1)S(1)} collective-permute-done((bf16[4,48,256]{2,1,0:T(8,128)(2,1)S(1)}, bf16[4,48,256]{2,1,0:T(8,128)(2,1)S(1)}, u32[]{:S(2)}, u32[]{:S(2)}) %collective-permute-start.12) | collective-permute-done | bytes 98336 | tf_op jit(solution)/shard_map/ppermute | solution.py:50
  65.6 1.7 %collective-permute-done.13.refs_1_ = bf16[16,48,256]{2,1,0:T(8,128)(2,1)S(1)} collective-permute-done((bf16[16,48,256]{2,1,0:T(8,128)(2,1)S(1)}, bf16[16,48,256]{2,1,0:T(8,128)(2,1)S(1)}, u32[]{:S(2)}, u32[]{:S(2)}) %collective-permute-start.13) | collective-permute-done | bytes 393248 | tf_op jit(solution)/shard_map/ppermute | solution.py:50
  68.1 12.2 %shard_map.37 = f32[8,96,256]{2,1,0:T(8,128)} custom-call(f32[1,1]{1,0:T(1,128)S(6)} %div.9.factor_ref, s32[1,1]{1,0:T(1,128)} %bitcast.digit_ref, bf16[16,48,256]{2,1,0:T(8,128)(2,1)} %copy-done.2, bf16[16,48,256]{2,1,0:T(8,128)(2,1)} %copy-done.4, bf16[16,48,256]{2,1,0:T(8,128)(2,1)} %copy-done.1, bf16[16,48,256]{2,1,0:T(8,128)(2,1)} %copy-done.3, ...), custom_call_target="tpu_custom_call" | custom-call | tf_op jit(solution)/shard_map/pallas_call | solution.py:112
  80.3 17.8 %all_to_all.5 = f32[8,96,256]{2,1,0:T(8,128)S(1)} all-to-all(f32[8,96,256]{2,1,0:T(8,128)} %shard_map.37), channel_id=1, replica_groups=mesh['chan'=32,'win'=8] {'win'}, dimensions={0} | all-to-all | bytes 1572864 | tf_op jit(solution)/shard_map/all_to_all | solution.py:158
  (78 shorter events, 13.8 us)
Async XLA Ops:
  9.5 9.4 %collective-permute-start.15 = (bf16[4,48,256]{2,1,0:T(8,128)(2,1)S(1)}, bf16[4,48,256]{2,1,0:T(8,128)(2,1)S(1)}, u32[]{:S(2)}, u32[]{:S(2)}) collective-permute-start(bf16[4,48,256]{2,1,0:T(8,128)(2,1)S(1)} %get-tuple-element.23), channel_id=1, source_target_pairs={{0,128},{8,136},{16,144},{24,152},{32,160},{40,168},{48,176},{56,1... | collective-permute-start | bytes 294920 | tf_op jit(solution)/shard_map/ppermute | solution.py:43
  11.9 7.9 %collective-permute-start.16 = (bf16[4,48,256]{2,1,0:T(8,128)(2,1)S(1)}, bf16[4,48,256]{2,1,0:T(8,128)(2,1)S(1)}, u32[]{:S(2)}, u32[]{:S(2)}) collective-permute-start(bf16[4,48,256]{2,1,0:T(8,128)(2,1)S(1)} %get-tuple-element.25), channel_id=1, source_target_pairs={{0,16},{8,24},{16,0},{24,8},{32,48},{40,56},{48,32},{56,40},{64,80... | collective-permute-start | bytes 294920 | tf_op jit(solution)/shard_map/ppermute | solution.py:43
  13.8 7.9 %collective-permute-start.17 = (bf16[4,48,256]{2,1,0:T(8,128)(2,1)S(1)}, bf16[4,48,256]{2,1,0:T(8,128)(2,1)S(1)}, u32[]{:S(2)}, u32[]{:S(2)}) collective-permute-start(bf16[4,48,256]{2,1,0:T(8,128)(2,1)S(1)} %get-tuple-element.24), channel_id=1, source_target_pairs={{0,144},{8,152},{16,128},{24,136},{32,176},{40,184},{48,160},{56,1... | collective-permute-start | bytes 294920 | tf_op jit(solution)/shard_map/ppermute | solution.py:43
  14.6 14.6 %collective-permute-start.1 = (bf16[4,48,256]{2,1,0:T(8,128)(2,1)S(1)}, bf16[4,48,256]{2,1,0:T(8,128)(2,1)S(1)}, u32[]{:S(2)}, u32[]{:S(2)}) collective-permute-start(bf16[4,48,256]{2,1,0:T(8,128)(2,1)S(1)} %get-tuple-element.30), channel_id=1, source_target_pairs={{0,128},{8,136},{16,144},{24,152},{32,160},{40,168},{48,176},{56,1... | collective-permute-start | bytes 294920 | tf_op jit(solution)/shard_map/ppermute | solution.py:43
  17.0 12.2 %collective-permute-start.2 = (bf16[4,48,256]{2,1,0:T(8,128)(2,1)S(1)}, bf16[4,48,256]{2,1,0:T(8,128)(2,1)S(1)}, u32[]{:S(2)}, u32[]{:S(2)}) collective-permute-start(bf16[4,48,256]{2,1,0:T(8,128)(2,1)S(1)} %get-tuple-element.32), channel_id=1, source_target_pairs={{0,16},{8,24},{16,0},{24,8},{32,48},{40,56},{48,32},{56,40},{64,80... | collective-permute-start | bytes 294920 | tf_op jit(solution)/shard_map/ppermute | solution.py:43
  18.9 10.3 %collective-permute-start.3 = (bf16[4,48,256]{2,1,0:T(8,128)(2,1)S(1)}, bf16[4,48,256]{2,1,0:T(8,128)(2,1)S(1)}, u32[]{:S(2)}, u32[]{:S(2)}) collective-permute-start(bf16[4,48,256]{2,1,0:T(8,128)(2,1)S(1)} %get-tuple-element.31), channel_id=1, source_target_pairs={{0,144},{8,152},{16,128},{24,136},{32,176},{40,184},{48,160},{56,1... | collective-permute-start | bytes 294920 | tf_op jit(solution)/shard_map/ppermute | solution.py:43
  21.8 14.1 %collective-permute-start.18 = (bf16[1,48,256]{2,1,0:T(8,128)(2,1)S(1)}, bf16[1,48,256]{2,1,0:T(8,128)(2,1)S(1)}, u32[]{:S(2)}, u32[]{:S(2)}) collective-permute-start(bf16[1,48,256]{2,1,0:T(8,128)(2,1)S(1)} %get-tuple-element.37), channel_id=1, source_target_pairs={{0,64},{8,72},{16,80},{24,88},{32,96},{40,104},{48,112},{56,120},{... | collective-permute-start | bytes 73736 | tf_op jit(solution)/shard_map/ppermute | solution.py:43
  27.8 8.1 %collective-permute-start.19 = (bf16[1,48,256]{2,1,0:T(8,128)(2,1)S(1)}, bf16[1,48,256]{2,1,0:T(8,128)(2,1)S(1)}, u32[]{:S(2)}, u32[]{:S(2)}) collective-permute-start(bf16[1,48,256]{2,1,0:T(8,128)(2,1)S(1)} %get-tuple-element.39), channel_id=1, source_target_pairs={{0,32},{8,40},{16,48},{24,56},{32,0},{40,8},{48,16},{56,24},{64,96... | collective-permute-start | bytes 73736 | tf_op jit(solution)/shard_map/ppermute | solution.py:43
  29.2 6.7 %collective-permute-start.20 = (bf16[1,48,256]{2,1,0:T(8,128)(2,1)S(1)}, bf16[1,48,256]{2,1,0:T(8,128)(2,1)S(1)}, u32[]{:S(2)}, u32[]{:S(2)}) collective-permute-start(bf16[1,48,256]{2,1,0:T(8,128)(2,1)S(1)} %get-tuple-element.38), channel_id=1, source_target_pairs={{0,96},{8,104},{16,112},{24,120},{32,64},{40,72},{48,80},{56,88},{... | collective-permute-start | bytes 73736 | tf_op jit(solution)/shard_map/ppermute | solution.py:43
  29.3 12.3 %collective-permute-start.4 = (bf16[1,48,256]{2,1,0:T(8,128)(2,1)S(1)}, bf16[1,48,256]{2,1,0:T(8,128)(2,1)S(1)}, u32[]{:S(2)}, u32[]{:S(2)}) collective-permute-start(bf16[1,48,256]{2,1,0:T(8,128)(2,1)S(1)} %get-tuple-element.44), channel_id=1, source_target_pairs={{0,64},{8,72},{16,80},{24,88},{32,96},{40,104},{48,112},{56,120},{... | collective-permute-start | bytes 73736 | tf_op jit(solution)/shard_map/ppermute | solution.py:43
  34.4 8.2 %collective-permute-start.5 = (bf16[1,48,256]{2,1,0:T(8,128)(2,1)S(1)}, bf16[1,48,256]{2,1,0:T(8,128)(2,1)S(1)}, u32[]{:S(2)}, u32[]{:S(2)}) collective-permute-start(bf16[1,48,256]{2,1,0:T(8,128)(2,1)S(1)} %get-tuple-element.46), channel_id=1, source_target_pairs={{0,32},{8,40},{16,48},{24,56},{32,0},{40,8},{48,16},{56,24},{64,96... | collective-permute-start | bytes 73736 | tf_op jit(solution)/shard_map/ppermute | solution.py:43
  35.9 6.7 %collective-permute-start.6 = (bf16[1,48,256]{2,1,0:T(8,128)(2,1)S(1)}, bf16[1,48,256]{2,1,0:T(8,128)(2,1)S(1)}, u32[]{:S(2)}, u32[]{:S(2)}) collective-permute-start(bf16[1,48,256]{2,1,0:T(8,128)(2,1)S(1)} %get-tuple-element.45), channel_id=1, source_target_pairs={{0,96},{8,104},{16,112},{24,120},{32,64},{40,72},{48,80},{56,88},{... | collective-permute-start | bytes 73736 | tf_op jit(solution)/shard_map/ppermute | solution.py:43
  35.9 12.3 %collective-permute-start.21 = (bf16[1,48,256]{2,1,0:T(8,128)(2,1)S(1)}, bf16[1,48,256]{2,1,0:T(8,128)(2,1)S(1)}, u32[]{:S(2)}, u32[]{:S(2)}) collective-permute-start(bf16[1,48,256]{2,1,0:T(8,128)(2,1)S(1)} %add_add_fusion), channel_id=1, source_target_pairs={{0,96},{8,104},{16,112},{24,120},{32,64},{40,72},{48,80},{56,88},{... | collective-permute-start | bytes 73736 | tf_op jit(solution)/shard_map/ppermute | solution.py:50
  40.1 9.3 %collective-permute-start.22 = (bf16[1,48,256]{2,1,0:T(8,128)(2,1)S(1)}, bf16[1,48,256]{2,1,0:T(8,128)(2,1)S(1)}, u32[]{:S(2)}, u32[]{:S(2)}) collective-permute-start(bf16[1,48,256]{2,1,0:T(8,128)(2,1)S(1)} %add_add_fusion), channel_id=1, source_target_pairs={{0,32},{8,40},{16,48},{24,56},{32,0},{40,8},{48,16},{56,24},{64,96... | collective-permute-start | bytes 73736 | tf_op jit(solution)/shard_map/ppermute | solution.py:50
  41.6 7.8 %collective-permute-start.23 = (bf16[1,48,256]{2,1,0:T(8,128)(2,1)S(1)}, bf16[1,48,256]{2,1,0:T(8,128)(2,1)S(1)}, u32[]{:S(2)}, u32[]{:S(2)}) collective-permute-start(bf16[1,48,256]{2,1,0:T(8,128)(2,1)S(1)} %add_add_fusion), channel_id=1, source_target_pairs={{0,64},{8,72},{16,80},{24,88},{32,96},{40,104},{48,112},{56,120},{... | collective-permute-start | bytes 73736 | tf_op jit(solution)/shard_map/ppermute | solution.py:50
  42.6 10.0 %collective-permute-start.7 = (bf16[1,48,256]{2,1,0:T(8,128)(2,1)S(1)}, bf16[1,48,256]{2,1,0:T(8,128)(2,1)S(1)}, u32[]{:S(2)}, u32[]{:S(2)}) collective-permute-start(bf16[1,48,256]{2,1,0:T(8,128)(2,1)S(1)} %add_add_fusion.1), channel_id=1, source_target_pairs={{0,96},{8,104},{16,112},{24,120},{32,64},{40,72},{48,80},{56,88},{... | collective-permute-start | bytes 73736 | tf_op jit(solution)/shard_map/ppermute | solution.py:50
  46.7 7.8 %collective-permute-start.8 = (bf16[1,48,256]{2,1,0:T(8,128)(2,1)S(1)}, bf16[1,48,256]{2,1,0:T(8,128)(2,1)S(1)}, u32[]{:S(2)}, u32[]{:S(2)}) collective-permute-start(bf16[1,48,256]{2,1,0:T(8,128)(2,1)S(1)} %add_add_fusion.1), channel_id=1, source_target_pairs={{0,32},{8,40},{16,48},{24,56},{32,0},{40,8},{48,16},{56,24},{64,96... | collective-permute-start | bytes 73736 | tf_op jit(solution)/shard_map/ppermute | solution.py:50
  48.2 7.7 %collective-permute-start.9 = (bf16[1,48,256]{2,1,0:T(8,128)(2,1)S(1)}, bf16[1,48,256]{2,1,0:T(8,128)(2,1)S(1)}, u32[]{:S(2)}, u32[]{:S(2)}) collective-permute-start(bf16[1,48,256]{2,1,0:T(8,128)(2,1)S(1)} %add_add_fusion.1), channel_id=1, source_target_pairs={{0,64},{8,72},{16,80},{24,88},{32,96},{40,104},{48,112},{56,120},{... | collective-permute-start | bytes 73736 | tf_op jit(solution)/shard_map/ppermute | solution.py:50
  49.5 9.8 %collective-permute-start.24 = (bf16[4,48,256]{2,1,0:T(8,128)(2,1)S(1)}, bf16[4,48,256]{2,1,0:T(8,128)(2,1)S(1)}, u32[]{:S(2)}, u32[]{:S(2)}) collective-permute-start(bf16[4,48,256]{2,1,0:T(8,128)(2,1)S(1)} %pad_maximum_fusion.5), channel_id=1, source_target_pairs={{0,144},{8,152},{16,128},{24,136},{32,176},{40,184},{48,160},{56,1... | collective-permute-start | bytes 294920 | tf_op jit(solution)/shard_map/ppermute | solution.py:50
  51.6 9.5 %collective-permute-start.25 = (bf16[4,48,256]{2,1,0:T(8,128)(2,1)S(1)}, bf16[4,48,256]{2,1,0:T(8,128)(2,1)S(1)}, u32[]{:S(2)}, u32[]{:S(2)}) collective-permute-start(bf16[4,48,256]{2,1,0:T(8,128)(2,1)S(1)} %pad_maximum_fusion.5), channel_id=1, source_target_pairs={{0,16},{8,24},{16,0},{24,8},{32,48},{40,56},{48,32},{56,40},{64,80... | collective-permute-start | bytes 294920 | tf_op jit(solution)/shard_map/ppermute | solution.py:50
  52.6 8.5 %collective-permute-start.26 = (bf16[4,48,256]{2,1,0:T(8,128)(2,1)S(1)}, bf16[4,48,256]{2,1,0:T(8,128)(2,1)S(1)}, u32[]{:S(2)}, u32[]{:S(2)}) collective-permute-start(bf16[4,48,256]{2,1,0:T(8,128)(2,1)S(1)} %pad_maximum_fusion.5), channel_id=1, source_target_pairs={{0,128},{8,136},{16,144},{24,152},{32,160},{40,168},{48,176},{56,1... | collective-permute-start | bytes 294920 | tf_op jit(solution)/shard_map/ppermute | solution.py:50
  56.0 7.1 %collective-permute-start.10 = (bf16[4,48,256]{2,1,0:T(8,128)(2,1)S(1)}, bf16[4,48,256]{2,1,0:T(8,128)(2,1)S(1)}, u32[]{:S(2)}, u32[]{:S(2)}) collective-permute-start(bf16[4,48,256]{2,1,0:T(8,128)(2,1)S(1)} %pad_maximum_fusion.4), channel_id=1, source_target_pairs={{0,144},{8,152},{16,128},{24,136},{32,176},{40,184},{48,160},{56,1... | collective-permute-start | bytes 294920 | tf_op jit(solution)/shard_map/ppermute | solution.py:50
  58.2 4.9 %collective-permute-start.11 = (bf16[4,48,256]{2,1,0:T(8,128)(2,1)S(1)}, bf16[4,48,256]{2,1,0:T(8,128)(2,1)S(1)}, u32[]{:S(2)}, u32[]{:S(2)}) collective-permute-start(bf16[4,48,256]{2,1,0:T(8,128)(2,1)S(1)} %pad_maximum_fusion.4), channel_id=1, source_target_pairs={{0,16},{8,24},{16,0},{24,8},{32,48},{40,56},{48,32},{56,40},{64,80... | collective-permute-start | bytes 294920 | tf_op jit(solution)/shard_map/ppermute | solution.py:50
  59.2 6.1 %collective-permute-start.12 = (bf16[4,48,256]{2,1,0:T(8,128)(2,1)S(1)}, bf16[4,48,256]{2,1,0:T(8,128)(2,1)S(1)}, u32[]{:S(2)}, u32[]{:S(2)}) collective-permute-start(bf16[4,48,256]{2,1,0:T(8,128)(2,1)S(1)} %pad_maximum_fusion.4), channel_id=1, source_target_pairs={{0,128},{8,136},{16,144},{24,152},{32,160},{40,168},{48,176},{56,1... | collective-permute-start | bytes 294920 | tf_op jit(solution)/shard_map/ppermute | solution.py:50
  (9 other events, 22.1 us)

commit v8 on v7

--- a/solution.py
+++ b/solution.py
@@ -9,7 +9,7 @@
 
 LAGS = 64
 EDGE = 128
-TIME_BLOCK = 2048
+TIME_BLOCK = 4096
 CHAN_BITS = (((0,), (1, 4), (2, 3)), ((0,), (1, 4), (2, 3)))
 
 def digit_of(me, bits):

time: 99.3 us -> 99 us (level)
  no operation moved by 1% of the time
where the time goes in v8:
time: 99 us; the launch traced here: 98.8 us
  starting transfers between devices  48.6 us (49%)
  blocking collectives  17.8 us (18%)
  Pallas kernels  11.9 us (12%)
  waiting for transfers between devices  9.56 us (10%)
  local copies, waits for them, and re-layouts  4.96 us (5%)
  other arithmetic  3.13 us (3%)
  between operations  2.81 us (3%)
    ppermute x14, starting transfers between devices, broadcast(): lax.ppermute(send, axis, xor_pairs(size, flip_mask(bits, offset)))  24.8 us
    ppermute x14, starting transfers between devices, broadcast(): lax.ppermute(pieces, axis, xor_pairs(size, flip_mask(bits, offset)))  23.8 us
    all_to_all x1, blocking collectives, body(): reduced = jnp.sum(lax.all_to_all(complete, 'win', 0, 0, tiled=True), 0)  17.8 us
    pallas_call x1, Pallas kernels, correlate(): pl.pallas_call(kernel, out_shape=jax.ShapeDtypeStruct((blocks, rows, out_...  11.9 us
    ppermute x14, waiting for transfers between devices, broadcast(): lax.ppermute(pieces, axis, xor_pairs(size, flip_mask(bits, offset)))  7.12 us
    ppermute x14, waiting for transfers between devices, broadcast(): lax.ppermute(send, axis, xor_pairs(size, flip_mask(bits, offset)))  2.44 us
  transfers between devices with their start and end apart: 28, of which 6 were waited for; matrix products, arithmetic and copies ran while one was open for 2% of the time, Pallas kernels for 0%

profile of v8, /device:TPU:8, one launch (start us, length us, event | category | flops | bytes accessed | tf_op | source)
XLA Modules:
  0.0 98.8 jit_solution(18435030167220879872)
XLA Ops:
  0.0 1.4 %fusion.9 = (s32[1]{0:T(128)}, s32[1]{0:T(128)}, s32[1]{0:T(128)}) fusion(s32[3]{0:T(128)} %param.4), kind=kLoop, calls=%fused_computation.57 | loop fusion | bytes 24 | tf_op jit(solution)/shard_map/slice | solution.py:144
  9.5 2.4 %collective-permute-start.15 = (bf16[4,48,256]{2,1,0:T(8,128)(2,1)S(1)}, bf16[4,48,256]{2,1,0:T(8,128)(2,1)S(1)}, u32[]{:S(2)}, u32[]{:S(2)}) collective-permute-start(bf16[4,48,256]{2,1,0:T(8,128)(2,1)S(1)} %get-tuple-element.23), channel_id=1, source_target_pairs={{0,128},{8,136},{16,144},{24,152},{32,160},{40,168},{48,176},{56,1... | collective-permute-start | bytes 294920 | tf_op jit(solution)/shard_map/ppermute | solution.py:43
  11.9 1.9 %collective-permute-start.16 = (bf16[4,48,256]{2,1,0:T(8,128)(2,1)S(1)}, bf16[4,48,256]{2,1,0:T(8,128)(2,1)S(1)}, u32[]{:S(2)}, u32[]{:S(2)}) collective-permute-start(bf16[4,48,256]{2,1,0:T(8,128)(2,1)S(1)} %get-tuple-element.25), channel_id=1, source_target_pairs={{0,16},{8,24},{16,0},{24,8},{32,48},{40,56},{48,32},{56,40},{64,80... | collective-permute-start | bytes 294920 | tf_op jit(solution)/shard_map/ppermute | solution.py:43
  14.6 2.4 %collective-permute-start.1 = (bf16[4,48,256]{2,1,0:T(8,128)(2,1)S(1)}, bf16[4,48,256]{2,1,0:T(8,128)(2,1)S(1)}, u32[]{:S(2)}, u32[]{:S(2)}) collective-permute-start(bf16[4,48,256]{2,1,0:T(8,128)(2,1)S(1)} %get-tuple-element.30), channel_id=1, source_target_pairs={{0,128},{8,136},{16,144},{24,152},{32,160},{40,168},{48,176},{56,1... | collective-permute-start | bytes 294920 | tf_op jit(solution)/shard_map/ppermute | solution.py:43
  17.0 1.9 %collective-permute-start.2 = (bf16[4,48,256]{2,1,0:T(8,128)(2,1)S(1)}, bf16[4,48,256]{2,1,0:T(8,128)(2,1)S(1)}, u32[]{:S(2)}, u32[]{:S(2)}) collective-permute-start(bf16[4,48,256]{2,1,0:T(8,128)(2,1)S(1)} %get-tuple-element.32), channel_id=1, source_target_pairs={{0,16},{8,24},{16,0},{24,8},{32,48},{40,56},{48,32},{56,40},{64,80... | collective-permute-start | bytes 294920 | tf_op jit(solution)/shard_map/ppermute | solution.py:43
  19.8 2.0 %collective-permute-done.17 = bf16[4,48,256]{2,1,0:T(8,128)(2,1)S(1)} collective-permute-done((bf16[4,48,256]{2,1,0:T(8,128)(2,1)S(1)}, bf16[4,48,256]{2,1,0:T(8,128)(2,1)S(1)}, u32[]{:S(2)}, u32[]{:S(2)}) %collective-permute-start.17) | collective-permute-done | bytes 98336 | tf_op jit(solution)/shard_map/ppermute | solution.py:43
  21.8 5.9 %collective-permute-start.18 = (bf16[1,48,256]{2,1,0:T(8,128)(2,1)S(1)}, bf16[1,48,256]{2,1,0:T(8,128)(2,1)S(1)}, u32[]{:S(2)}, u32[]{:S(2)}) collective-permute-start(bf16[1,48,256]{2,1,0:T(8,128)(2,1)S(1)} %get-tuple-element.37), channel_id=1, source_target_pairs={{0,64},{8,72},{16,80},{24,88},{32,96},{40,104},{48,112},{56,120},{... | collective-permute-start | bytes 73736 | tf_op jit(solution)/shard_map/ppermute | solution.py:43
  27.8 1.5 %collective-permute-start.19 = (bf16[1,48,256]{2,1,0:T(8,128)(2,1)S(1)}, bf16[1,48,256]{2,1,0:T(8,128)(2,1)S(1)}, u32[]{:S(2)}, u32[]{:S(2)}) collective-permute-start(bf16[1,48,256]{2,1,0:T(8,128)(2,1)S(1)} %get-tuple-element.39), channel_id=1, source_target_pairs={{0,32},{8,40},{16,48},{24,56},{32,0},{40,8},{48,16},{56,24},{64,96... | collective-permute-start | bytes 73736 | tf_op jit(solution)/shard_map/ppermute | solution.py:43
  29.3 5.1 %collective-permute-start.4 = (bf16[1,48,256]{2,1,0:T(8,128)(2,1)S(1)}, bf16[1,48,256]{2,1,0:T(8,128)(2,1)S(1)}, u32[]{:S(2)}, u32[]{:S(2)}) collective-permute-start(bf16[1,48,256]{2,1,0:T(8,128)(2,1)S(1)} %get-tuple-element.44), channel_id=1, source_target_pairs={{0,64},{8,72},{16,80},{24,88},{32,96},{40,104},{48,112},{56,120},{... | collective-permute-start | bytes 73736 | tf_op jit(solution)/shard_map/ppermute | solution.py:43
  34.4 1.5 %collective-permute-start.5 = (bf16[1,48,256]{2,1,0:T(8,128)(2,1)S(1)}, bf16[1,48,256]{2,1,0:T(8,128)(2,1)S(1)}, u32[]{:S(2)}, u32[]{:S(2)}) collective-permute-start(bf16[1,48,256]{2,1,0:T(8,128)(2,1)S(1)} %get-tuple-element.46), channel_id=1, source_target_pairs={{0,32},{8,40},{16,48},{24,56},{32,0},{40,8},{48,16},{56,24},{64,96... | collective-permute-start | bytes 73736 | tf_op jit(solution)/shard_map/ppermute | solution.py:43
  35.9 4.2 %collective-permute-start.21 = (bf16[1,48,256]{2,1,0:T(8,128)(2,1)S(1)}, bf16[1,48,256]{2,1,0:T(8,128)(2,1)S(1)}, u32[]{:S(2)}, u32[]{:S(2)}) collective-permute-start(bf16[1,48,256]{2,1,0:T(8,128)(2,1)S(1)} %add_add_fusion), channel_id=1, source_target_pairs={{0,96},{8,104},{16,112},{24,120},{32,64},{40,72},{48,80},{56,88},{... | collective-permute-start | bytes 73736 | tf_op jit(solution)/shard_map/ppermute | solution.py:50
  40.1 1.5 %collective-permute-start.22 = (bf16[1,48,256]{2,1,0:T(8,128)(2,1)S(1)}, bf16[1,48,256]{2,1,0:T(8,128)(2,1)S(1)}, u32[]{:S(2)}, u32[]{:S(2)}) collective-permute-start(bf16[1,48,256]{2,1,0:T(8,128)(2,1)S(1)} %add_add_fusion), channel_id=1, source_target_pairs={{0,32},{8,40},{16,48},{24,56},{32,0},{40,8},{48,16},{56,24},{64,96... | collective-permute-start | bytes 73736 | tf_op jit(solution)/shard_map/ppermute | solution.py:50
  42.6 4.1 %collective-permute-start.7 = (bf16[1,48,256]{2,1,0:T(8,128)(2,1)S(1)}, bf16[1,48,256]{2,1,0:T(8,128)(2,1)S(1)}, u32[]{:S(2)}, u32[]{:S(2)}) collective-permute-start(bf16[1,48,256]{2,1,0:T(8,128)(2,1)S(1)} %add_add_fusion.1), channel_id=1, source_target_pairs={{0,96},{8,104},{16,112},{24,120},{32,64},{40,72},{48,80},{56,88},{... | collective-permute-start | bytes 73736 | tf_op jit(solution)/shard_map/ppermute | solution.py:50
  46.7 1.5 %collective-permute-start.8 = (bf16[1,48,256]{2,1,0:T(8,128)(2,1)S(1)}, bf16[1,48,256]{2,1,0:T(8,128)(2,1)S(1)}, u32[]{:S(2)}, u32[]{:S(2)}) collective-permute-start(bf16[1,48,256]{2,1,0:T(8,128)(2,1)S(1)} %add_add_fusion.1), channel_id=1, source_target_pairs={{0,32},{8,40},{16,48},{24,56},{32,0},{40,8},{48,16},{56,24},{64,96... | collective-permute-start | bytes 73736 | tf_op jit(solution)/shard_map/ppermute | solution.py:50
  49.5 2.2 %collective-permute-start.24 = (bf16[4,48,256]{2,1,0:T(8,128)(2,1)S(1)}, bf16[4,48,256]{2,1,0:T(8,128)(2,1)S(1)}, u32[]{:S(2)}, u32[]{:S(2)}) collective-permute-start(bf16[4,48,256]{2,1,0:T(8,128)(2,1)S(1)} %pad_maximum_fusion.5), channel_id=1, source_target_pairs={{0,144},{8,152},{16,128},{24,136},{32,176},{40,184},{48,160},{56,1... | collective-permute-start | bytes 294920 | tf_op jit(solution)/shard_map/ppermute | solution.py:50
  52.6 1.9 %collective-permute-start.26 = (bf16[4,48,256]{2,1,0:T(8,128)(2,1)S(1)}, bf16[4,48,256]{2,1,0:T(8,128)(2,1)S(1)}, u32[]{:S(2)}, u32[]{:S(2)}) collective-permute-start(bf16[4,48,256]{2,1,0:T(8,128)(2,1)S(1)} %pad_maximum_fusion.5), channel_id=1, source_target_pairs={{0,128},{8,136},{16,144},{24,152},{32,160},{40,168},{48,176},{56,1... | collective-permute-start | bytes 294920 | tf_op jit(solution)/shard_map/ppermute | solution.py:50
  54.5 1.4 %collective-permute-done.9 = bf16[1,48,256]{2,1,0:T(8,128)(2,1)S(1)} collective-permute-done((bf16[1,48,256]{2,1,0:T(8,128)(2,1)S(1)}, bf16[1,48,256]{2,1,0:T(8,128)(2,1)S(1)}, u32[]{:S(2)}, u32[]{:S(2)}) %collective-permute-start.9) | collective-permute-done | bytes 24608 | tf_op jit(solution)/shard_map/ppermute | solution.py:50
  56.0 2.2 %collective-permute-start.10 = (bf16[4,48,256]{2,1,0:T(8,128)(2,1)S(1)}, bf16[4,48,256]{2,1,0:T(8,128)(2,1)S(1)}, u32[]{:S(2)}, u32[]{:S(2)}) collective-permute-start(bf16[4,48,256]{2,1,0:T(8,128)(2,1)S(1)} %pad_maximum_fusion.4), channel_id=1, source_target_pairs={{0,144},{8,152},{16,128},{24,136},{32,176},{40,184},{48,160},{56,1... | collective-permute-start | bytes 294920 | tf_op jit(solution)/shard_map/ppermute | solution.py:50
  59.2 1.8 %collective-permute-start.12 = (bf16[4,48,256]{2,1,0:T(8,128)(2,1)S(1)}, bf16[4,48,256]{2,1,0:T(8,128)(2,1)S(1)}, u32[]{:S(2)}, u32[]{:S(2)}) collective-permute-start(bf16[4,48,256]{2,1,0:T(8,128)(2,1)S(1)} %pad_maximum_fusion.4), channel_id=1, source_target_pairs={{0,128},{8,136},{16,144},{24,152},{32,160},{40,168},{48,176},{56,1... | collective-permute-start | bytes 294920 | tf_op jit(solution)/shard_map/ppermute | solution.py:50
  61.3 1.8 %collective-permute-done.10 = bf16[4,48,256]{2,1,0:T(8,128)(2,1)S(1)} collective-permute-done((bf16[4,48,256]{2,1,0:T(8,128)(2,1)S(1)}, bf16[4,48,256]{2,1,0:T(8,128)(2,1)S(1)}, u32[]{:S(2)}, u32[]{:S(2)}) %collective-permute-start.10) | collective-permute-done | bytes 98336 | tf_op jit(solution)/shard_map/ppermute | solution.py:50
  63.1 2.3 %collective-permute-done.12 = bf16[4,48,256]{2,1,0:T(8,128)(2,1)S(1)} collective-permute-done((bf16[4,48,256]{2,1,0:T(8,128)(2,1)S(1)}, bf16[4,48,256]{2,1,0:T(8,128)(2,1)S(1)}, u32[]{:S(2)}, u32[]{:S(2)}) %collective-permute-start.12) | collective-permute-done | bytes 98336 | tf_op jit(solution)/shard_map/ppermute | solution.py:50
  65.6 1.7 %collective-permute-done.13.refs_1_ = bf16[16,48,256]{2,1,0:T(8,128)(2,1)S(1)} collective-permute-done((bf16[16,48,256]{2,1,0:T(8,128)(2,1)S(1)}, bf16[16,48,256]{2,1,0:T(8,128)(2,1)S(1)}, u32[]{:S(2)}, u32[]{:S(2)}) %collective-permute-start.13) | collective-permute-done | bytes 393248 | tf_op jit(solution)/shard_map/ppermute | solution.py:50
  68.1 11.9 %shard_map.37 = f32[8,96,256]{2,1,0:T(8,128)} custom-call(f32[1,1]{1,0:T(1,128)S(6)} %div.9.factor_ref, s32[1,1]{1,0:T(1,128)} %bitcast.digit_ref, bf16[16,48,256]{2,1,0:T(8,128)(2,1)} %copy-done.2, bf16[16,48,256]{2,1,0:T(8,128)(2,1)} %copy-done.4, bf16[16,48,256]{2,1,0:T(8,128)(2,1)} %copy-done.1, bf16[16,48,256]{2,1,0:T(8,128)(2,1)} %copy-done.3, ...), custom_call_target="tpu_custom_call" | custom-call | tf_op jit(solution)/shard_map/pallas_call | solution.py:112
  80.0 17.8 %all_to_all.5 = f32[8,96,256]{2,1,0:T(8,128)S(1)} all-to-all(f32[8,96,256]{2,1,0:T(8,128)} %shard_map.37), channel_id=1, replica_groups=mesh['chan'=32,'win'=8] {'win'}, dimensions={0} | all-to-all | bytes 1572864 | tf_op jit(solution)/shard_map/all_to_all | solution.py:158
  (78 shorter events, 13.8 us)
Async XLA Ops:
  9.5 9.4 %collective-permute-start.15 = (bf16[4,48,256]{2,1,0:T(8,128)(2,1)S(1)}, bf16[4,48,256]{2,1,0:T(8,128)(2,1)S(1)}, u32[]{:S(2)}, u32[]{:S(2)}) collective-permute-start(bf16[4,48,256]{2,1,0:T(8,128)(2,1)S(1)} %get-tuple-element.23), channel_id=1, source_target_pairs={{0,128},{8,136},{16,144},{24,152},{32,160},{40,168},{48,176},{56,1... | collective-permute-start | bytes 294920 | tf_op jit(solution)/shard_map/ppermute | solution.py:43
  11.9 7.9 %collective-permute-start.16 = (bf16[4,48,256]{2,1,0:T(8,128)(2,1)S(1)}, bf16[4,48,256]{2,1,0:T(8,128)(2,1)S(1)}, u32[]{:S(2)}, u32[]{:S(2)}) collective-permute-start(bf16[4,48,256]{2,1,0:T(8,128)(2,1)S(1)} %get-tuple-element.25), channel_id=1, source_target_pairs={{0,16},{8,24},{16,0},{24,8},{32,48},{40,56},{48,32},{56,40},{64,80... | collective-permute-start | bytes 294920 | tf_op jit(solution)/shard_map/ppermute | solution.py:43
  13.8 7.9 %collective-permute-start.17 = (bf16[4,48,256]{2,1,0:T(8,128)(2,1)S(1)}, bf16[4,48,256]{2,1,0:T(8,128)(2,1)S(1)}, u32[]{:S(2)}, u32[]{:S(2)}) collective-permute-start(bf16[4,48,256]{2,1,0:T(8,128)(2,1)S(1)} %get-tuple-element.24), channel_id=1, source_target_pairs={{0,144},{8,152},{16,128},{24,136},{32,176},{40,184},{48,160},{56,1... | collective-permute-start | bytes 294920 | tf_op jit(solution)/shard_map/ppermute | solution.py:43
  14.6 14.6 %collective-permute-start.1 = (bf16[4,48,256]{2,1,0:T(8,128)(2,1)S(1)}, bf16[4,48,256]{2,1,0:T(8,128)(2,1)S(1)}, u32[]{:S(2)}, u32[]{:S(2)}) collective-permute-start(bf16[4,48,256]{2,1,0:T(8,128)(2,1)S(1)} %get-tuple-element.30), channel_id=1, source_target_pairs={{0,128},{8,136},{16,144},{24,152},{32,160},{40,168},{48,176},{56,1... | collective-permute-start | bytes 294920 | tf_op jit(solution)/shard_map/ppermute | solution.py:43
  17.0 12.2 %collective-permute-start.2 = (bf16[4,48,256]{2,1,0:T(8,128)(2,1)S(1)}, bf16[4,48,256]{2,1,0:T(8,128)(2,1)S(1)}, u32[]{:S(2)}, u32[]{:S(2)}) collective-permute-start(bf16[4,48,256]{2,1,0:T(8,128)(2,1)S(1)} %get-tuple-element.32), channel_id=1, source_target_pairs={{0,16},{8,24},{16,0},{24,8},{32,48},{40,56},{48,32},{56,40},{64,80... | collective-permute-start | bytes 294920 | tf_op jit(solution)/shard_map/ppermute | solution.py:43
  18.9 10.3 %collective-permute-start.3 = (bf16[4,48,256]{2,1,0:T(8,128)(2,1)S(1)}, bf16[4,48,256]{2,1,0:T(8,128)(2,1)S(1)}, u32[]{:S(2)}, u32[]{:S(2)}) collective-permute-start(bf16[4,48,256]{2,1,0:T(8,128)(2,1)S(1)} %get-tuple-element.31), channel_id=1, source_target_pairs={{0,144},{8,152},{16,128},{24,136},{32,176},{40,184},{48,160},{56,1... | collective-permute-start | bytes 294920 | tf_op jit(solution)/shard_map/ppermute | solution.py:43
  21.8 14.1 %collective-permute-start.18 = (bf16[1,48,256]{2,1,0:T(8,128)(2,1)S(1)}, bf16[1,48,256]{2,1,0:T(8,128)(2,1)S(1)}, u32[]{:S(2)}, u32[]{:S(2)}) collective-permute-start(bf16[1,48,256]{2,1,0:T(8,128)(2,1)S(1)} %get-tuple-element.37), channel_id=1, source_target_pairs={{0,64},{8,72},{16,80},{24,88},{32,96},{40,104},{48,112},{56,120},{... | collective-permute-start | bytes 73736 | tf_op jit(solution)/shard_map/ppermute | solution.py:43
  27.8 8.1 %collective-permute-start.19 = (bf16[1,48,256]{2,1,0:T(8,128)(2,1)S(1)}, bf16[1,48,256]{2,1,0:T(8,128)(2,1)S(1)}, u32[]{:S(2)}, u32[]{:S(2)}) collective-permute-start(bf16[1,48,256]{2,1,0:T(8,128)(2,1)S(1)} %get-tuple-element.39), channel_id=1, source_target_pairs={{0,32},{8,40},{16,48},{24,56},{32,0},{40,8},{48,16},{56,24},{64,96... | collective-permute-start | bytes 73736 | tf_op jit(solution)/shard_map/ppermute | solution.py:43
  29.2 6.7 %collective-permute-start.20 = (bf16[1,48,256]{2,1,0:T(8,128)(2,1)S(1)}, bf16[1,48,256]{2,1,0:T(8,128)(2,1)S(1)}, u32[]{:S(2)}, u32[]{:S(2)}) collective-permute-start(bf16[1,48,256]{2,1,0:T(8,128)(2,1)S(1)} %get-tuple-element.38), channel_id=1, source_target_pairs={{0,96},{8,104},{16,112},{24,120},{32,64},{40,72},{48,80},{56,88},{... | collective-permute-start | bytes 73736 | tf_op jit(solution)/shard_map/ppermute | solution.py:43
  29.3 12.3 %collective-permute-start.4 = (bf16[1,48,256]{2,1,0:T(8,128)(2,1)S(1)}, bf16[1,48,256]{2,1,0:T(8,128)(2,1)S(1)}, u32[]{:S(2)}, u32[]{:S(2)}) collective-permute-start(bf16[1,48,256]{2,1,0:T(8,128)(2,1)S(1)} %get-tuple-element.44), channel_id=1, source_target_pairs={{0,64},{8,72},{16,80},{24,88},{32,96},{40,104},{48,112},{56,120},{... | collective-permute-start | bytes 73736 | tf_op jit(solution)/shard_map/ppermute | solution.py:43
  34.4 8.2 %collective-permute-start.5 = (bf16[1,48,256]{2,1,0:T(8,128)(2,1)S(1)}, bf16[1,48,256]{2,1,0:T(8,128)(2,1)S(1)}, u32[]{:S(2)}, u32[]{:S(2)}) collective-permute-start(bf16[1,48,256]{2,1,0:T(8,128)(2,1)S(1)} %get-tuple-element.46), channel_id=1, source_target_pairs={{0,32},{8,40},{16,48},{24,56},{32,0},{40,8},{48,16},{56,24},{64,96... | collective-permute-start | bytes 73736 | tf_op jit(solution)/shard_map/ppermute | solution.py:43
  35.9 6.7 %collective-permute-start.6 = (bf16[1,48,256]{2,1,0:T(8,128)(2,1)S(1)}, bf16[1,48,256]{2,1,0:T(8,128)(2,1)S(1)}, u32[]{:S(2)}, u32[]{:S(2)}) collective-permute-start(bf16[1,48,256]{2,1,0:T(8,128)(2,1)S(1)} %get-tuple-element.45), channel_id=1, source_target_pairs={{0,96},{8,104},{16,112},{24,120},{32,64},{40,72},{48,80},{56,88},{... | collective-permute-start | bytes 73736 | tf_op jit(solution)/shard_map/ppermute | solution.py:43
  35.9 12.3 %collective-permute-start.21 = (bf16[1,48,256]{2,1,0:T(8,128)(2,1)S(1)}, bf16[1,48,256]{2,1,0:T(8,128)(2,1)S(1)}, u32[]{:S(2)}, u32[]{:S(2)}) collective-permute-start(bf16[1,48,256]{2,1,0:T(8,128)(2,1)S(1)} %add_add_fusion), channel_id=1, source_target_pairs={{0,96},{8,104},{16,112},{24,120},{32,64},{40,72},{48,80},{56,88},{... | collective-permute-start | bytes 73736 | tf_op jit(solution)/shard_map/ppermute | solution.py:50
  40.1 9.3 %collective-permute-start.22 = (bf16[1,48,256]{2,1,0:T(8,128)(2,1)S(1)}, bf16[1,48,256]{2,1,0:T(8,128)(2,1)S(1)}, u32[]{:S(2)}, u32[]{:S(2)}) collective-permute-start(bf16[1,48,256]{2,1,0:T(8,128)(2,1)S(1)} %add_add_fusion), channel_id=1, source_target_pairs={{0,32},{8,40},{16,48},{24,56},{32,0},{40,8},{48,16},{56,24},{64,96... | collective-permute-start | bytes 73736 | tf_op jit(solution)/shard_map/ppermute | solution.py:50
  41.6 7.8 %collective-permute-start.23 = (bf16[1,48,256]{2,1,0:T(8,128)(2,1)S(1)}, bf16[1,48,256]{2,1,0:T(8,128)(2,1)S(1)}, u32[]{:S(2)}, u32[]{:S(2)}) collective-permute-start(bf16[1,48,256]{2,1,0:T(8,128)(2,1)S(1)} %add_add_fusion), channel_id=1, source_target_pairs={{0,64},{8,72},{16,80},{24,88},{32,96},{40,104},{48,112},{56,120},{... | collective-permute-start | bytes 73736 | tf_op jit(solution)/shard_map/ppermute | solution.py:50
  42.6 10.0 %collective-permute-start.7 = (bf16[1,48,256]{2,1,0:T(8,128)(2,1)S(1)}, bf16[1,48,256]{2,1,0:T(8,128)(2,1)S(1)}, u32[]{:S(2)}, u32[]{:S(2)}) collective-permute-start(bf16[1,48,256]{2,1,0:T(8,128)(2,1)S(1)} %add_add_fusion.1), channel_id=1, source_target_pairs={{0,96},{8,104},{16,112},{24,120},{32,64},{40,72},{48,80},{56,88},{... | collective-permute-start | bytes 73736 | tf_op jit(solution)/shard_map/ppermute | solution.py:50
  46.7 7.8 %collective-permute-start.8 = (bf16[1,48,256]{2,1,0:T(8,128)(2,1)S(1)}, bf16[1,48,256]{2,1,0:T(8,128)(2,1)S(1)}, u32[]{:S(2)}, u32[]{:S(2)}) collective-permute-start(bf16[1,48,256]{2,1,0:T(8,128)(2,1)S(1)} %add_add_fusion.1), channel_id=1, source_target_pairs={{0,32},{8,40},{16,48},{24,56},{32,0},{40,8},{48,16},{56,24},{64,96... | collective-permute-start | bytes 73736 | tf_op jit(solution)/shard_map/ppermute | solution.py:50
  48.2 7.7 %collective-permute-start.9 = (bf16[1,48,256]{2,1,0:T(8,128)(2,1)S(1)}, bf16[1,48,256]{2,1,0:T(8,128)(2,1)S(1)}, u32[]{:S(2)}, u32[]{:S(2)}) collective-permute-start(bf16[1,48,256]{2,1,0:T(8,128)(2,1)S(1)} %add_add_fusion.1), channel_id=1, source_target_pairs={{0,64},{8,72},{16,80},{24,88},{32,96},{40,104},{48,112},{56,120},{... | collective-permute-start | bytes 73736 | tf_op jit(solution)/shard_map/ppermute | solution.py:50
  49.5 9.8 %collective-permute-start.24 = (bf16[4,48,256]{2,1,0:T(8,128)(2,1)S(1)}, bf16[4,48,256]{2,1,0:T(8,128)(2,1)S(1)}, u32[]{:S(2)}, u32[]{:S(2)}) collective-permute-start(bf16[4,48,256]{2,1,0:T(8,128)(2,1)S(1)} %pad_maximum_fusion.5), channel_id=1, source_target_pairs={{0,144},{8,152},{16,128},{24,136},{32,176},{40,184},{48,160},{56,1... | collective-permute-start | bytes 294920 | tf_op jit(solution)/shard_map/ppermute | solution.py:50
  51.6 9.5 %collective-permute-start.25 = (bf16[4,48,256]{2,1,0:T(8,128)(2,1)S(1)}, bf16[4,48,256]{2,1,0:T(8,128)(2,1)S(1)}, u32[]{:S(2)}, u32[]{:S(2)}) collective-permute-start(bf16[4,48,256]{2,1,0:T(8,128)(2,1)S(1)} %pad_maximum_fusion.5), channel_id=1, source_target_pairs={{0,16},{8,24},{16,0},{24,8},{32,48},{40,56},{48,32},{56,40},{64,80... | collective-permute-start | bytes 294920 | tf_op jit(solution)/shard_map/ppermute | solution.py:50
  52.6 8.5 %collective-permute-start.26 = (bf16[4,48,256]{2,1,0:T(8,128)(2,1)S(1)}, bf16[4,48,256]{2,1,0:T(8,128)(2,1)S(1)}, u32[]{:S(2)}, u32[]{:S(2)}) collective-permute-start(bf16[4,48,256]{2,1,0:T(8,128)(2,1)S(1)} %pad_maximum_fusion.5), channel_id=1, source_target_pairs={{0,128},{8,136},{16,144},{24,152},{32,160},{40,168},{48,176},{56,1... | collective-permute-start | bytes 294920 | tf_op jit(solution)/shard_map/ppermute | solution.py:50
  56.0 7.1 %collective-permute-start.10 = (bf16[4,48,256]{2,1,0:T(8,128)(2,1)S(1)}, bf16[4,48,256]{2,1,0:T(8,128)(2,1)S(1)}, u32[]{:S(2)}, u32[]{:S(2)}) collective-permute-start(bf16[4,48,256]{2,1,0:T(8,128)(2,1)S(1)} %pad_maximum_fusion.4), channel_id=1, source_target_pairs={{0,144},{8,152},{16,128},{24,136},{32,176},{40,184},{48,160},{56,1... | collective-permute-start | bytes 294920 | tf_op jit(solution)/shard_map/ppermute | solution.py:50
  58.2 4.9 %collective-permute-start.11 = (bf16[4,48,256]{2,1,0:T(8,128)(2,1)S(1)}, bf16[4,48,256]{2,1,0:T(8,128)(2,1)S(1)}, u32[]{:S(2)}, u32[]{:S(2)}) collective-permute-start(bf16[4,48,256]{2,1,0:T(8,128)(2,1)S(1)} %pad_maximum_fusion.4), channel_id=1, source_target_pairs={{0,16},{8,24},{16,0},{24,8},{32,48},{40,56},{48,32},{56,40},{64,80... | collective-permute-start | bytes 294920 | tf_op jit(solution)/shard_map/ppermute | solution.py:50
  59.2 6.1 %collective-permute-start.12 = (bf16[4,48,256]{2,1,0:T(8,128)(2,1)S(1)}, bf16[4,48,256]{2,1,0:T(8,128)(2,1)S(1)}, u32[]{:S(2)}, u32[]{:S(2)}) collective-permute-start(bf16[4,48,256]{2,1,0:T(8,128)(2,1)S(1)} %pad_maximum_fusion.4), channel_id=1, source_target_pairs={{0,128},{8,136},{16,144},{24,152},{32,160},{40,168},{48,176},{56,1... | collective-permute-start | bytes 294920 | tf_op jit(solution)/shard_map/ppermute | solution.py:50
  (9 other events, 22.1 us)

commit v9 on v8

--- a/solution.py
+++ b/solution.py
@@ -140,10 +140,9 @@
     outgoing = (pieces.astype(jnp.float32) * scale[None]).astype(jnp.bfloat16) * own_flag.astype(
         jnp.bfloat16
     )
-    masked = jnp.concatenate(
-        [jnp.where(chan_me == owner[step], outgoing, jnp.zeros_like(outgoing)) for step in range(step_count)],
-        1,
-    )
+    hits = (owner == chan_me)[None, :, None, None]
+    masked = jnp.where(hits, outgoing[:, None], jnp.zeros_like(outgoing)[:, None])
+    masked = masked.reshape(chan_size, step_count * chan_dev, samples // chan_size)
     half = masked.shape[1] // 2
     halves = []
     rider = whitened

time: 99 us -> 97.3 us (0.983)
  between operations: 2.81 us -> 0.93 us
  starting transfers between devices: 48.6 us -> 50 us
  waiting for transfers between devices: 9.56 us -> 8.28 us
    ppermute x14, starting transfers between devices: 24.8 us -> 26.3 us  [broadcast(): lax.ppermute(send, axis, xor_pairs(size, flip_mask(bits, offset)))]
    slice x1 -> x0, local copies, waits for them, and re-layouts: 1.37 us -> none  [body(): owner[step]]
    ppermute x14, waiting for transfers between devices: 2.44 us -> 1.2 us  [broadcast(): lax.ppermute(send, axis, xor_pairs(size, flip_mask(bits, offset)))]
    unnamed x11, local copies, waits for them, and re-layouts: 0.93 us -> 1.95 us
  transfers between devices with their start and end apart: 28 -> 28, of which waited for: 6 -> 8; matrix products, arithmetic and copies ran while one was open for 2% -> 2% of each run, Pallas kernels for 0% -> 0%
where the time goes in v9:
time: 97.3 us; the launch traced here: 97 us
  starting transfers between devices  50 us (51%)
  blocking collectives  17.8 us (18%)
  Pallas kernels  11.9 us (12%)
  waiting for transfers between devices  8.28 us (9%)
  local copies, waits for them, and re-layouts  4.29 us (4%)
  other arithmetic  3.74 us (4%)
    ppermute x14, starting transfers between devices, broadcast(): lax.ppermute(send, axis, xor_pairs(size, flip_mask(bits, offset)))  26.3 us
    ppermute x14, starting transfers between devices, broadcast(): lax.ppermute(pieces, axis, xor_pairs(size, flip_mask(bits, offset)))  23.7 us
    all_to_all x1, blocking collectives, body(): reduced = jnp.sum(lax.all_to_all(complete, 'win', 0, 0, tiled=True), 0)  17.8 us
    pallas_call x1, Pallas kernels, correlate(): pl.pallas_call(kernel, out_shape=jax.ShapeDtypeStruct((blocks, rows, out_...  11.9 us
    ppermute x14, waiting for transfers between devices, broadcast(): lax.ppermute(pieces, axis, xor_pairs(size, flip_mask(bits, offset)))  7.08 us
    unnamed x11, local copies, waits for them, and re-layouts  1.95 us
  transfers between devices with their start and end apart: 28, of which 8 were waited for; matrix products, arithmetic and copies ran while one was open for 2% of the time, Pallas kernels for 0%

profile of v9, /device:TPU:8, one launch (start us, length us, event | category | flops | bytes accessed | tf_op | source)
XLA Modules:
  0.0 97.0 jit_solution(4531034637327075708)
XLA Ops:
  1.5 1.3 %fusion.1 = f32[32]{0:T(128)S(1)} fusion(bf16[1,32,8192]{2,1,0:T(8,128)(2,1)} %param.3), kind=kLoop, calls=%fused_computation.5 | loop fusion | flops 786400 | bytes 524416 | tf_op jit(solution)/shard_map/reduce_sum | solution.py:136
  7.5 3.7 %collective-permute-start.3 = (bf16[4,48,256]{2,1,0:T(8,128)(2,1)S(1)}, bf16[4,48,256]{2,1,0:T(8,128)(2,1)S(1)}, u32[]{:S(2)}, u32[]{:S(2)}) collective-permute-start(bf16[4,48,256]{2,1,0:T(8,128)(2,1)S(1)} %get-tuple-element.27), channel_id=1, source_target_pairs={{0,144},{8,152},{16,128},{24,136},{32,176},{40,184},{48,160},{56,1... | collective-permute-start | bytes 294920 | tf_op jit(solution)/shard_map/ppermute | solution.py:43
  11.4 1.2 %collective-permute-start.1 = (bf16[4,48,256]{2,1,0:T(8,128)(2,1)S(1)}, bf16[4,48,256]{2,1,0:T(8,128)(2,1)S(1)}, u32[]{:S(2)}, u32[]{:S(2)}) collective-permute-start(bf16[4,48,256]{2,1,0:T(8,128)(2,1)S(1)} %get-tuple-element.26), channel_id=1, source_target_pairs={{0,128},{8,136},{16,144},{24,152},{32,160},{40,168},{48,176},{56,1... | collective-permute-start | bytes 294920 | tf_op jit(solution)/shard_map/ppermute | solution.py:43
  12.7 3.7 %collective-permute-start.17 = (bf16[4,48,256]{2,1,0:T(8,128)(2,1)S(1)}, bf16[4,48,256]{2,1,0:T(8,128)(2,1)S(1)}, u32[]{:S(2)}, u32[]{:S(2)}) collective-permute-start(bf16[4,48,256]{2,1,0:T(8,128)(2,1)S(1)} %get-tuple-element.20), channel_id=1, source_target_pairs={{0,144},{8,152},{16,128},{24,136},{32,176},{40,184},{48,160},{56,1... | collective-permute-start | bytes 294920 | tf_op jit(solution)/shard_map/ppermute | solution.py:43
  16.5 1.2 %collective-permute-start.15 = (bf16[4,48,256]{2,1,0:T(8,128)(2,1)S(1)}, bf16[4,48,256]{2,1,0:T(8,128)(2,1)S(1)}, u32[]{:S(2)}, u32[]{:S(2)}) collective-permute-start(bf16[4,48,256]{2,1,0:T(8,128)(2,1)S(1)} %get-tuple-element.19), channel_id=1, source_target_pairs={{0,128},{8,136},{16,144},{24,152},{32,160},{40,168},{48,176},{56,1... | collective-permute-start | bytes 294920 | tf_op jit(solution)/shard_map/ppermute | solution.py:43
  18.6 6.4 %collective-permute-start.6 = (bf16[1,48,256]{2,1,0:T(8,128)(2,1)S(1)}, bf16[1,48,256]{2,1,0:T(8,128)(2,1)S(1)}, u32[]{:S(2)}, u32[]{:S(2)}) collective-permute-start(bf16[1,48,256]{2,1,0:T(8,128)(2,1)S(1)} %get-tuple-element.41), channel_id=1, source_target_pairs={{0,96},{8,104},{16,112},{24,120},{32,64},{40,72},{48,80},{56,88},{... | collective-permute-start | bytes 73736 | tf_op jit(solution)/shard_map/ppermute | solution.py:43
  25.0 1.5 %collective-permute-start.5 = (bf16[1,48,256]{2,1,0:T(8,128)(2,1)S(1)}, bf16[1,48,256]{2,1,0:T(8,128)(2,1)S(1)}, u32[]{:S(2)}, u32[]{:S(2)}) collective-permute-start(bf16[1,48,256]{2,1,0:T(8,128)(2,1)S(1)} %get-tuple-element.42), channel_id=1, source_target_pairs={{0,32},{8,40},{16,48},{24,56},{32,0},{40,8},{48,16},{56,24},{64,96... | collective-permute-start | bytes 73736 | tf_op jit(solution)/shard_map/ppermute | solution.py:43
  27.6 4.0 %collective-permute-start.20 = (bf16[1,48,256]{2,1,0:T(8,128)(2,1)S(1)}, bf16[1,48,256]{2,1,0:T(8,128)(2,1)S(1)}, u32[]{:S(2)}, u32[]{:S(2)}) collective-permute-start(bf16[1,48,256]{2,1,0:T(8,128)(2,1)S(1)} %get-tuple-element.34), channel_id=1, source_target_pairs={{0,96},{8,104},{16,112},{24,120},{32,64},{40,72},{48,80},{56,88},{... | collective-permute-start | bytes 73736 | tf_op jit(solution)/shard_map/ppermute | solution.py:43
  31.6 1.5 %collective-permute-start.19 = (bf16[1,48,256]{2,1,0:T(8,128)(2,1)S(1)}, bf16[1,48,256]{2,1,0:T(8,128)(2,1)S(1)}, u32[]{:S(2)}, u32[]{:S(2)}) collective-permute-start(bf16[1,48,256]{2,1,0:T(8,128)(2,1)S(1)} %get-tuple-element.35), channel_id=1, source_target_pairs={{0,32},{8,40},{16,48},{24,56},{32,0},{40,8},{48,16},{56,24},{64,96... | collective-permute-start | bytes 73736 | tf_op jit(solution)/shard_map/ppermute | solution.py:43
  34.3 3.9 %collective-permute-start.7 = (bf16[1,48,256]{2,1,0:T(8,128)(2,1)S(1)}, bf16[1,48,256]{2,1,0:T(8,128)(2,1)S(1)}, u32[]{:S(2)}, u32[]{:S(2)}) collective-permute-start(bf16[1,48,256]{2,1,0:T(8,128)(2,1)S(1)} %add_add_fusion.1), channel_id=1, source_target_pairs={{0,96},{8,104},{16,112},{24,120},{32,64},{40,72},{48,80},{56,88},{... | collective-permute-start | bytes 73736 | tf_op jit(solution)/shard_map/ppermute | solution.py:50
  38.2 1.5 %collective-permute-start.8 = (bf16[1,48,256]{2,1,0:T(8,128)(2,1)S(1)}, bf16[1,48,256]{2,1,0:T(8,128)(2,1)S(1)}, u32[]{:S(2)}, u32[]{:S(2)}) collective-permute-start(bf16[1,48,256]{2,1,0:T(8,128)(2,1)S(1)} %add_add_fusion.1), channel_id=1, source_target_pairs={{0,32},{8,40},{16,48},{24,56},{32,0},{40,8},{48,16},{56,24},{64,96... | collective-permute-start | bytes 73736 | tf_op jit(solution)/shard_map/ppermute | solution.py:50
  39.7 1.2 %collective-permute-start.9 = (bf16[1,48,256]{2,1,0:T(8,128)(2,1)S(1)}, bf16[1,48,256]{2,1,0:T(8,128)(2,1)S(1)}, u32[]{:S(2)}, u32[]{:S(2)}) collective-permute-start(bf16[1,48,256]{2,1,0:T(8,128)(2,1)S(1)} %add_add_fusion.1), channel_id=1, source_target_pairs={{0,64},{8,72},{16,80},{24,88},{32,96},{40,104},{48,112},{56,120},{... | collective-permute-start | bytes 73736 | tf_op jit(solution)/shard_map/ppermute | solution.py:50
  40.9 3.9 %collective-permute-start.21 = (bf16[1,48,256]{2,1,0:T(8,128)(2,1)S(1)}, bf16[1,48,256]{2,1,0:T(8,128)(2,1)S(1)}, u32[]{:S(2)}, u32[]{:S(2)}) collective-permute-start(bf16[1,48,256]{2,1,0:T(8,128)(2,1)S(1)} %add_add_fusion), channel_id=1, source_target_pairs={{0,96},{8,104},{16,112},{24,120},{32,64},{40,72},{48,80},{56,88},{... | collective-permute-start | bytes 73736 | tf_op jit(solution)/shard_map/ppermute | solution.py:50
  44.8 1.5 %collective-permute-start.22 = (bf16[1,48,256]{2,1,0:T(8,128)(2,1)S(1)}, bf16[1,48,256]{2,1,0:T(8,128)(2,1)S(1)}, u32[]{:S(2)}, u32[]{:S(2)}) collective-permute-start(bf16[1,48,256]{2,1,0:T(8,128)(2,1)S(1)} %add_add_fusion), channel_id=1, source_target_pairs={{0,32},{8,40},{16,48},{24,56},{32,0},{40,8},{48,16},{56,24},{64,96... | collective-permute-start | bytes 73736 | tf_op jit(solution)/shard_map/ppermute | solution.py:50
  46.3 1.2 %collective-permute-start.23 = (bf16[1,48,256]{2,1,0:T(8,128)(2,1)S(1)}, bf16[1,48,256]{2,1,0:T(8,128)(2,1)S(1)}, u32[]{:S(2)}, u32[]{:S(2)}) collective-permute-start(bf16[1,48,256]{2,1,0:T(8,128)(2,1)S(1)} %add_add_fusion), channel_id=1, source_target_pairs={{0,64},{8,72},{16,80},{24,88},{32,96},{40,104},{48,112},{56,120},{... | collective-permute-start | bytes 73736 | tf_op jit(solution)/shard_map/ppermute | solution.py:50
  48.2 2.1 %collective-permute-start.10 = (bf16[4,48,256]{2,1,0:T(8,128)(2,1)S(1)}, bf16[4,48,256]{2,1,0:T(8,128)(2,1)S(1)}, u32[]{:S(2)}, u32[]{:S(2)}) collective-permute-start(bf16[4,48,256]{2,1,0:T(8,128)(2,1)S(1)} %pad_maximum_fusion.2), channel_id=1, source_target_pairs={{0,144},{8,152},{16,128},{24,136},{32,176},{40,184},{48,160},{56,1... | collective-permute-start | bytes 294920 | tf_op jit(solution)/shard_map/ppermute | solution.py:50
  51.5 1.8 %collective-permute-start.12 = (bf16[4,48,256]{2,1,0:T(8,128)(2,1)S(1)}, bf16[4,48,256]{2,1,0:T(8,128)(2,1)S(1)}, u32[]{:S(2)}, u32[]{:S(2)}) collective-permute-start(bf16[4,48,256]{2,1,0:T(8,128)(2,1)S(1)} %pad_maximum_fusion.2), channel_id=1, source_target_pairs={{0,128},{8,136},{16,144},{24,152},{32,160},{40,168},{48,176},{56,1... | collective-permute-start | bytes 294920 | tf_op jit(solution)/shard_map/ppermute | solution.py:50
  54.2 2.0 %collective-permute-start.24 = (bf16[4,48,256]{2,1,0:T(8,128)(2,1)S(1)}, bf16[4,48,256]{2,1,0:T(8,128)(2,1)S(1)}, u32[]{:S(2)}, u32[]{:S(2)}) collective-permute-start(bf16[4,48,256]{2,1,0:T(8,128)(2,1)S(1)} %pad_maximum_fusion.3), channel_id=1, source_target_pairs={{0,144},{8,152},{16,128},{24,136},{32,176},{40,184},{48,160},{56,1... | collective-permute-start | bytes 294920 | tf_op jit(solution)/shard_map/ppermute | solution.py:50
  57.3 2.0 %collective-permute-start.26 = (bf16[4,48,256]{2,1,0:T(8,128)(2,1)S(1)}, bf16[4,48,256]{2,1,0:T(8,128)(2,1)S(1)}, u32[]{:S(2)}, u32[]{:S(2)}) collective-permute-start(bf16[4,48,256]{2,1,0:T(8,128)(2,1)S(1)} %pad_maximum_fusion.3), channel_id=1, source_target_pairs={{0,128},{8,136},{16,144},{24,152},{32,160},{40,168},{48,176},{56,1... | collective-permute-start | bytes 294920 | tf_op jit(solution)/shard_map/ppermute | solution.py:50
  59.6 1.8 %collective-permute-done.24 = bf16[4,48,256]{2,1,0:T(8,128)(2,1)S(1)} collective-permute-done((bf16[4,48,256]{2,1,0:T(8,128)(2,1)S(1)}, bf16[4,48,256]{2,1,0:T(8,128)(2,1)S(1)}, u32[]{:S(2)}, u32[]{:S(2)}) %collective-permute-start.24) | collective-permute-done | bytes 98336 | tf_op jit(solution)/shard_map/ppermute | solution.py:50
  61.3 2.1 %collective-permute-done.26 = bf16[4,48,256]{2,1,0:T(8,128)(2,1)S(1)} collective-permute-done((bf16[4,48,256]{2,1,0:T(8,128)(2,1)S(1)}, bf16[4,48,256]{2,1,0:T(8,128)(2,1)S(1)}, u32[]{:S(2)}, u32[]{:S(2)}) %collective-permute-start.26) | collective-permute-done | bytes 98336 | tf_op jit(solution)/shard_map/ppermute | solution.py:50
  63.9 1.7 %collective-permute-done.27.refs_3_ = bf16[16,48,256]{2,1,0:T(8,128)(2,1)S(1)} collective-permute-done((bf16[16,48,256]{2,1,0:T(8,128)(2,1)S(1)}, bf16[16,48,256]{2,1,0:T(8,128)(2,1)S(1)}, u32[]{:S(2)}, u32[]{:S(2)}) %collective-permute-start.27) | collective-permute-done | bytes 393248 | tf_op jit(solution)/shard_map/ppermute | solution.py:50
  66.3 11.9 %shard_map.37 = f32[8,96,256]{2,1,0:T(8,128)} custom-call(f32[1,1]{1,0:T(1,128)S(6)} %div.9.factor_ref, s32[1,1]{1,0:T(1,128)} %bitcast.digit_ref, bf16[16,48,256]{2,1,0:T(8,128)(2,1)} %copy-done.1, bf16[16,48,256]{2,1,0:T(8,128)(2,1)} %copy-done.3, bf16[16,48,256]{2,1,0:T(8,128)(2,1)} %copy-done.2, bf16[16,48,256]{2,1,0:T(8,128)(2,1)} %copy-done.4, ...), custom_call_target="tpu_custom_call" | custom-call | tf_op jit(solution)/shard_map/pallas_call | solution.py:112
  78.3 17.8 %all_to_all.5 = f32[8,96,256]{2,1,0:T(8,128)S(1)} all-to-all(f32[8,96,256]{2,1,0:T(8,128)} %shard_map.37), channel_id=1, replica_groups=mesh['chan'=32,'win'=8] {'win'}, dimensions={0} | all-to-all | bytes 1572864 | tf_op jit(solution)/shard_map/all_to_all | solution.py:157
  (79 shorter events, 15.2 us)
Async XLA Ops:
  5.5 7.1 %collective-permute-start.14 = (bf16[16,48,256]{2,1,0:T(8,128)(2,1)S(1)}, bf16[16,48,256]{2,1,0:T(8,128)(2,1)S(1)}, u32[]{:S(2)}, u32[]{:S(2)}) collective-permute-start(bf16[16,48,256]{2,1,0:T(8,128)(2,1)S(1)} %dynamic-slice_bitcast_fusion), channel_id=1, source_target_pairs={{0,8},{8,0},{16,24},{24,16},{32,40},{40,32},{48,56},{56,48},{64,72... | collective-permute-start | bytes 1179656 | tf_op jit(solution)/shard_map/ppermute | solution.py:43
  7.5 9.0 %collective-permute-start.3 = (bf16[4,48,256]{2,1,0:T(8,128)(2,1)S(1)}, bf16[4,48,256]{2,1,0:T(8,128)(2,1)S(1)}, u32[]{:S(2)}, u32[]{:S(2)}) collective-permute-start(bf16[4,48,256]{2,1,0:T(8,128)(2,1)S(1)} %get-tuple-element.27), channel_id=1, source_target_pairs={{0,144},{8,152},{16,128},{24,136},{32,176},{40,184},{48,160},{56,1... | collective-permute-start | bytes 294920 | tf_op jit(solution)/shard_map/ppermute | solution.py:43
  11.2 6.5 %collective-permute-start.2 = (bf16[4,48,256]{2,1,0:T(8,128)(2,1)S(1)}, bf16[4,48,256]{2,1,0:T(8,128)(2,1)S(1)}, u32[]{:S(2)}, u32[]{:S(2)}) collective-permute-start(bf16[4,48,256]{2,1,0:T(8,128)(2,1)S(1)} %get-tuple-element.28), channel_id=1, source_target_pairs={{0,16},{8,24},{16,0},{24,8},{32,48},{40,56},{48,32},{56,40},{64,80... | collective-permute-start | bytes 294920 | tf_op jit(solution)/shard_map/ppermute | solution.py:43
  11.4 7.2 %collective-permute-start.1 = (bf16[4,48,256]{2,1,0:T(8,128)(2,1)S(1)}, bf16[4,48,256]{2,1,0:T(8,128)(2,1)S(1)}, u32[]{:S(2)}, u32[]{:S(2)}) collective-permute-start(bf16[4,48,256]{2,1,0:T(8,128)(2,1)S(1)} %get-tuple-element.26), channel_id=1, source_target_pairs={{0,128},{8,136},{16,144},{24,152},{32,160},{40,168},{48,176},{56,1... | collective-permute-start | bytes 294920 | tf_op jit(solution)/shard_map/ppermute | solution.py:43
  12.7 13.7 %collective-permute-start.17 = (bf16[4,48,256]{2,1,0:T(8,128)(2,1)S(1)}, bf16[4,48,256]{2,1,0:T(8,128)(2,1)S(1)}, u32[]{:S(2)}, u32[]{:S(2)}) collective-permute-start(bf16[4,48,256]{2,1,0:T(8,128)(2,1)S(1)} %get-tuple-element.20), channel_id=1, source_target_pairs={{0,144},{8,152},{16,128},{24,136},{32,176},{40,184},{48,160},{56,1... | collective-permute-start | bytes 294920 | tf_op jit(solution)/shard_map/ppermute | solution.py:43
  16.4 11.1 %collective-permute-start.16 = (bf16[4,48,256]{2,1,0:T(8,128)(2,1)S(1)}, bf16[4,48,256]{2,1,0:T(8,128)(2,1)S(1)}, u32[]{:S(2)}, u32[]{:S(2)}) collective-permute-start(bf16[4,48,256]{2,1,0:T(8,128)(2,1)S(1)} %get-tuple-element.21), channel_id=1, source_target_pairs={{0,16},{8,24},{16,0},{24,8},{32,48},{40,56},{48,32},{56,40},{64,80... | collective-permute-start | bytes 294920 | tf_op jit(solution)/shard_map/ppermute | solution.py:43
  16.5 11.0 %collective-permute-start.15 = (bf16[4,48,256]{2,1,0:T(8,128)(2,1)S(1)}, bf16[4,48,256]{2,1,0:T(8,128)(2,1)S(1)}, u32[]{:S(2)}, u32[]{:S(2)}) collective-permute-start(bf16[4,48,256]{2,1,0:T(8,128)(2,1)S(1)} %get-tuple-element.19), channel_id=1, source_target_pairs={{0,128},{8,136},{16,144},{24,152},{32,160},{40,168},{48,176},{56,1... | collective-permute-start | bytes 294920 | tf_op jit(solution)/shard_map/ppermute | solution.py:43
  18.6 14.5 %collective-permute-start.6 = (bf16[1,48,256]{2,1,0:T(8,128)(2,1)S(1)}, bf16[1,48,256]{2,1,0:T(8,128)(2,1)S(1)}, u32[]{:S(2)}, u32[]{:S(2)}) collective-permute-start(bf16[1,48,256]{2,1,0:T(8,128)(2,1)S(1)} %get-tuple-element.41), channel_id=1, source_target_pairs={{0,96},{8,104},{16,112},{24,120},{32,64},{40,72},{48,80},{56,88},{... | collective-permute-start | bytes 73736 | tf_op jit(solution)/shard_map/ppermute | solution.py:43
  25.0 9.2 %collective-permute-start.5 = (bf16[1,48,256]{2,1,0:T(8,128)(2,1)S(1)}, bf16[1,48,256]{2,1,0:T(8,128)(2,1)S(1)}, u32[]{:S(2)}, u32[]{:S(2)}) collective-permute-start(bf16[1,48,256]{2,1,0:T(8,128)(2,1)S(1)} %get-tuple-element.42), channel_id=1, source_target_pairs={{0,32},{8,40},{16,48},{24,56},{32,0},{40,8},{48,16},{56,24},{64,96... | collective-permute-start | bytes 73736 | tf_op jit(solution)/shard_map/ppermute | solution.py:43
  26.4 7.8 %collective-permute-start.4 = (bf16[1,48,256]{2,1,0:T(8,128)(2,1)S(1)}, bf16[1,48,256]{2,1,0:T(8,128)(2,1)S(1)}, u32[]{:S(2)}, u32[]{:S(2)}) collective-permute-start(bf16[1,48,256]{2,1,0:T(8,128)(2,1)S(1)} %get-tuple-element.40), channel_id=1, source_target_pairs={{0,64},{8,72},{16,80},{24,88},{32,96},{40,104},{48,112},{56,120},{... | collective-permute-start | bytes 73736 | tf_op jit(solution)/shard_map/ppermute | solution.py:43
  27.6 12.1 %collective-permute-start.20 = (bf16[1,48,256]{2,1,0:T(8,128)(2,1)S(1)}, bf16[1,48,256]{2,1,0:T(8,128)(2,1)S(1)}, u32[]{:S(2)}, u32[]{:S(2)}) collective-permute-start(bf16[1,48,256]{2,1,0:T(8,128)(2,1)S(1)} %get-tuple-element.34), channel_id=1, source_target_pairs={{0,96},{8,104},{16,112},{24,120},{32,64},{40,72},{48,80},{56,88},{... | collective-permute-start | bytes 73736 | tf_op jit(solution)/shard_map/ppermute | solution.py:43
  31.6 9.3 %collective-permute-start.19 = (bf16[1,48,256]{2,1,0:T(8,128)(2,1)S(1)}, bf16[1,48,256]{2,1,0:T(8,128)(2,1)S(1)}, u32[]{:S(2)}, u32[]{:S(2)}) collective-permute-start(bf16[1,48,256]{2,1,0:T(8,128)(2,1)S(1)} %get-tuple-element.35), channel_id=1, source_target_pairs={{0,32},{8,40},{16,48},{24,56},{32,0},{40,8},{48,16},{56,24},{64,96... | collective-permute-start | bytes 73736 | tf_op jit(solution)/shard_map/ppermute | solution.py:43
  33.1 7.8 %collective-permute-start.18 = (bf16[1,48,256]{2,1,0:T(8,128)(2,1)S(1)}, bf16[1,48,256]{2,1,0:T(8,128)(2,1)S(1)}, u32[]{:S(2)}, u32[]{:S(2)}) collective-permute-start(bf16[1,48,256]{2,1,0:T(8,128)(2,1)S(1)} %get-tuple-element.33), channel_id=1, source_target_pairs={{0,64},{8,72},{16,80},{24,88},{32,96},{40,104},{48,112},{56,120},{... | collective-permute-start | bytes 73736 | tf_op jit(solution)/shard_map/ppermute | solution.py:43
  34.3 12.0 %collective-permute-start.7 = (bf16[1,48,256]{2,1,0:T(8,128)(2,1)S(1)}, bf16[1,48,256]{2,1,0:T(8,128)(2,1)S(1)}, u32[]{:S(2)}, u32[]{:S(2)}) collective-permute-start(bf16[1,48,256]{2,1,0:T(8,128)(2,1)S(1)} %add_add_fusion.1), channel_id=1, source_target_pairs={{0,96},{8,104},{16,112},{24,120},{32,64},{40,72},{48,80},{56,88},{... | collective-permute-start | bytes 73736 | tf_op jit(solution)/shard_map/ppermute | solution.py:50
  38.2 9.3 %collective-permute-start.8 = (bf16[1,48,256]{2,1,0:T(8,128)(2,1)S(1)}, bf16[1,48,256]{2,1,0:T(8,128)(2,1)S(1)}, u32[]{:S(2)}, u32[]{:S(2)}) collective-permute-start(bf16[1,48,256]{2,1,0:T(8,128)(2,1)S(1)} %add_add_fusion.1), channel_id=1, source_target_pairs={{0,32},{8,40},{16,48},{24,56},{32,0},{40,8},{48,16},{56,24},{64,96... | collective-permute-start | bytes 73736 | tf_op jit(solution)/shard_map/ppermute | solution.py:50
  39.7 8.4 %collective-permute-start.9 = (bf16[1,48,256]{2,1,0:T(8,128)(2,1)S(1)}, bf16[1,48,256]{2,1,0:T(8,128)(2,1)S(1)}, u32[]{:S(2)}, u32[]{:S(2)}) collective-permute-start(bf16[1,48,256]{2,1,0:T(8,128)(2,1)S(1)} %add_add_fusion.1), channel_id=1, source_target_pairs={{0,64},{8,72},{16,80},{24,88},{32,96},{40,104},{48,112},{56,120},{... | collective-permute-start | bytes 73736 | tf_op jit(solution)/shard_map/ppermute | solution.py:50
  40.9 10.6 %collective-permute-start.21 = (bf16[1,48,256]{2,1,0:T(8,128)(2,1)S(1)}, bf16[1,48,256]{2,1,0:T(8,128)(2,1)S(1)}, u32[]{:S(2)}, u32[]{:S(2)}) collective-permute-start(bf16[1,48,256]{2,1,0:T(8,128)(2,1)S(1)} %add_add_fusion), channel_id=1, source_target_pairs={{0,96},{8,104},{16,112},{24,120},{32,64},{40,72},{48,80},{56,88},{... | collective-permute-start | bytes 73736 | tf_op jit(solution)/shard_map/ppermute | solution.py:50
  44.8 8.4 %collective-permute-start.22 = (bf16[1,48,256]{2,1,0:T(8,128)(2,1)S(1)}, bf16[1,48,256]{2,1,0:T(8,128)(2,1)S(1)}, u32[]{:S(2)}, u32[]{:S(2)}) collective-permute-start(bf16[1,48,256]{2,1,0:T(8,128)(2,1)S(1)} %add_add_fusion), channel_id=1, source_target_pairs={{0,32},{8,40},{16,48},{24,56},{32,0},{40,8},{48,16},{56,24},{64,96... | collective-permute-start | bytes 73736 | tf_op jit(solution)/shard_map/ppermute | solution.py:50
  46.3 7.9 %collective-permute-start.23 = (bf16[1,48,256]{2,1,0:T(8,128)(2,1)S(1)}, bf16[1,48,256]{2,1,0:T(8,128)(2,1)S(1)}, u32[]{:S(2)}, u32[]{:S(2)}) collective-permute-start(bf16[1,48,256]{2,1,0:T(8,128)(2,1)S(1)} %add_add_fusion), channel_id=1, source_target_pairs={{0,64},{8,72},{16,80},{24,88},{32,96},{40,104},{48,112},{56,120},{... | collective-permute-start | bytes 73736 | tf_op jit(solution)/shard_map/ppermute | solution.py:50
  48.2 9.1 %collective-permute-start.10 = (bf16[4,48,256]{2,1,0:T(8,128)(2,1)S(1)}, bf16[4,48,256]{2,1,0:T(8,128)(2,1)S(1)}, u32[]{:S(2)}, u32[]{:S(2)}) collective-permute-start(bf16[4,48,256]{2,1,0:T(8,128)(2,1)S(1)} %pad_maximum_fusion.2), channel_id=1, source_target_pairs={{0,144},{8,152},{16,128},{24,136},{32,176},{40,184},{48,160},{56,1... | collective-permute-start | bytes 294920 | tf_op jit(solution)/shard_map/ppermute | solution.py:50
  50.3 9.0 %collective-permute-start.11 = (bf16[4,48,256]{2,1,0:T(8,128)(2,1)S(1)}, bf16[4,48,256]{2,1,0:T(8,128)(2,1)S(1)}, u32[]{:S(2)}, u32[]{:S(2)}) collective-permute-start(bf16[4,48,256]{2,1,0:T(8,128)(2,1)S(1)} %pad_maximum_fusion.2), channel_id=1, source_target_pairs={{0,16},{8,24},{16,0},{24,8},{32,48},{40,56},{48,32},{56,40},{64,80... | collective-permute-start | bytes 294920 | tf_op jit(solution)/shard_map/ppermute | solution.py:50
  51.5 7.8 %collective-permute-start.12 = (bf16[4,48,256]{2,1,0:T(8,128)(2,1)S(1)}, bf16[4,48,256]{2,1,0:T(8,128)(2,1)S(1)}, u32[]{:S(2)}, u32[]{:S(2)}) collective-permute-start(bf16[4,48,256]{2,1,0:T(8,128)(2,1)S(1)} %pad_maximum_fusion.2), channel_id=1, source_target_pairs={{0,128},{8,136},{16,144},{24,152},{32,160},{40,168},{48,176},{56,1... | collective-permute-start | bytes 294920 | tf_op jit(solution)/shard_map/ppermute | solution.py:50
  54.2 7.1 %collective-permute-start.24 = (bf16[4,48,256]{2,1,0:T(8,128)(2,1)S(1)}, bf16[4,48,256]{2,1,0:T(8,128)(2,1)S(1)}, u32[]{:S(2)}, u32[]{:S(2)}) collective-permute-start(bf16[4,48,256]{2,1,0:T(8,128)(2,1)S(1)} %pad_maximum_fusion.3), channel_id=1, source_target_pairs={{0,144},{8,152},{16,128},{24,136},{32,176},{40,184},{48,160},{56,1... | collective-permute-start | bytes 294920 | tf_op jit(solution)/shard_map/ppermute | solution.py:50
  57.3 6.1 %collective-permute-start.26 = (bf16[4,48,256]{2,1,0:T(8,128)(2,1)S(1)}, bf16[4,48,256]{2,1,0:T(8,128)(2,1)S(1)}, u32[]{:S(2)}, u32[]{:S(2)}) collective-permute-start(bf16[4,48,256]{2,1,0:T(8,128)(2,1)S(1)} %pad_maximum_fusion.3), channel_id=1, source_target_pairs={{0,128},{8,136},{16,144},{24,152},{32,160},{40,168},{48,176},{56,1... | collective-permute-start | bytes 294920 | tf_op jit(solution)/shard_map/ppermute | solution.py:50
  (9 other events, 25.5 us)
